TPU v7x, 32 devices: a whole 2x2x4 slice. The times are simulated.
32 devices in a mesh: expert: 16 (over z, y, core), dp: 2 (over x).
Axes of the slice: x: 2, y: 2, z: 4, core: 2. Of those that a mesh axis runs over, the one named last changes fastest.
Arguments:
- tokens: bfloat16 [4096, 2048], P(('expert', 'dp')), may hold values from -6 to 6
- cotangent: bfloat16 [4096, 2048], P(('expert', 'dp')), may hold values from -6 to 6
- expert_ids: int32 [4096, 6], P(('expert', 'dp')), may hold values from 0 to 15, all different within a row; in each aligned block of 128 rows (0 to 127, 128 to 255, ...) at most 60 rows name the same one
- gate_vals: float32 [4096, 6], P(('expert', 'dp')), may hold values from 0.05 to 0.5
- capacity: int32 [16], replicated, may hold values from 384 to 960
- w_gate: bfloat16 [16, 384, 2048], P('expert', 'dp'), may hold values from -0.125 to 0.125
- w_up: bfloat16 [16, 384, 2048], P('expert', 'dp'), may hold values from -0.125 to 0.125
- w_down: bfloat16 [16, 384, 2048], P('expert', 'dp'), may hold values from -0.3125 to 0.3125
Outputs:
- layer_out: bfloat16 [4096, 2048], P(('expert', 'dp'))
- grad_tokens: bfloat16 [4096, 2048], P(('expert', 'dp'))
- grad_gates: float32 [4096, 6], P(('expert', 'dp'))
- grad_gate_w: bfloat16 [16, 384, 2048], P('expert', 'dp')
- grad_up_w: bfloat16 [16, 384, 2048], P('expert', 'dp')
- grad_down_w: bfloat16 [16, 384, 2048], P('expert', 'dp')
Inputs may be any that keep to these rules, and one draw needn't show every extreme that they name: `expert_ids`: within the 128 rows of one device no expert is named more than 60 times, a bound that some block reaches.
All inputs are finite; a program needn't handle non-finite values.
Results may differ from a plain program's by a relative error of at most 0.0065.
Values may be sent and summed in bfloat16 or wider, within the bound.
No kernel may reach another device: no remote copies, remote signals or barrier semaphores. Data moves between devices by JAX's collectives and lax.ppermute only.
A program may use at most 128 MiB of HBM per device.

v0:
```python
import jax
import jax.numpy as jnp
from jax import lax
from jax.sharding import PartitionSpec as P


def entering(value, axis, join, neutral):
    count, mine = (lax.axis_size(axis), lax.axis_index(axis))
    pieces = lax.all_gather(value, axis)
    subtotal = jnp.full_like(value, 0) + jnp.asarray(neutral, value.dtype)

    def lap(position, subtotal):
        longer = join(subtotal, pieces[position])
        return jnp.where(position < mine, longer, subtotal)

    return lax.fori_loop(0, count - 1, lap, subtotal)


def add_counts(earlier, later):
    return earlier + later


def on_device(tokens, cotangent, expert_ids, gate_vals, capacity, w_gate, w_up, w_down):
    tok_rows, width = tokens.shape
    top_count = expert_ids.shape[1]
    experts = capacity.shape[0]
    local_experts = w_gate.shape[0]
    slots = max(2, (5 * tok_rows * top_count + 4 * experts - 1) // (4 * experts))
    n_expert = lax.axis_size("expert")
    flat_ids = expert_ids.reshape(-1)
    one_hot = (flat_ids[:, None] == jnp.arange(experts, dtype=jnp.int32)[None, :]).astype(jnp.int32)
    running = jnp.cumsum(one_hot, axis=0)
    local_rank = jnp.sum(running * one_hot, axis=1) - 1
    counts = running[-1]
    earlier = entering(counts, "expert", add_counts, jnp.zeros_like(counts))
    offset = jnp.sum(one_hot * earlier[None, :], axis=1)
    limit = jnp.sum(one_hot * capacity[None, :], axis=1)
    kept = offset + local_rank < limit
    slot_index = jnp.where(kept, flat_ids * slots + local_rank, experts * slots)
    input_routes = jnp.broadcast_to(tokens[:, None, :], (tok_rows, top_count, width)).reshape(
        -1, width
    )
    cot_routes = (
        (gate_vals[:, :, None] * cotangent.astype(jnp.float32)[:, None, :])
        .astype(jnp.bfloat16)
        .reshape(-1, width)
    )
    input_buf = (
        jnp.zeros((experts * slots, width), jnp.bfloat16)
        .at[slot_index]
        .set(input_routes, mode="drop")
    )
    cot_buf = (
        jnp.zeros((experts * slots, width), jnp.bfloat16)
        .at[slot_index]
        .set(cot_routes, mode="drop")
    )
    input_buf = input_buf.reshape(experts, slots, width)
    cot_buf = cot_buf.reshape(experts, slots, width)
    full_gate, full_up, full_down = (
        lax.all_gather(w_gate, "dp", axis=1, tiled=True),
        lax.all_gather(w_up, "dp", axis=1, tiled=True),
        lax.all_gather(w_down, "dp", axis=1, tiled=True),
    )
    rows_in, rows_cot = (
        lax.all_to_all(input_buf, "expert", split_axis=0, concat_axis=0, tiled=True),
        lax.all_to_all(cot_buf, "expert", split_axis=0, concat_axis=0, tiled=True),
    )
    rows_in = rows_in.reshape(n_expert, local_experts, slots, width)
    gate_pre = jnp.einsum("secd,efd->secf", rows_in, full_gate, preferred_element_type=jnp.float32)
    up_pre = jnp.einsum("secd,efd->secf", rows_in, full_up, preferred_element_type=jnp.float32)
    sigmoid_gate = jax.nn.sigmoid(gate_pre)
    activated = gate_pre * sigmoid_gate
    hidden = (activated * up_pre).astype(jnp.bfloat16)
    out_rows = jnp.einsum(
        "secf,efd->secd", hidden, full_down, preferred_element_type=jnp.float32
    ).astype(jnp.bfloat16)
    rows_cot = rows_cot.reshape(n_expert, local_experts, slots, width)
    d_hidden = jnp.einsum("secd,efd->secf", rows_cot, full_down, preferred_element_type=jnp.float32)
    d_gate = (d_hidden * up_pre * (sigmoid_gate + activated * (1.0 - sigmoid_gate))).astype(
        jnp.bfloat16
    )
    d_up = (d_hidden * activated).astype(jnp.bfloat16)
    dx_rows = jnp.einsum("secf,efd->secd", d_gate, full_gate, preferred_element_type=jnp.float32)
    dx_rows = (
        dx_rows + jnp.einsum("secf,efd->secd", d_up, full_up, preferred_element_type=jnp.float32)
    ).astype(jnp.bfloat16)
    part_down = jnp.einsum("secf,secd->efd", hidden, rows_cot, preferred_element_type=jnp.float32)
    part_gate = jnp.einsum("secf,secd->efd", d_gate, rows_in, preferred_element_type=jnp.float32)
    part_up = jnp.einsum("secf,secd->efd", d_up, rows_in, preferred_element_type=jnp.float32)
    summed_gate, summed_up, summed_down = (
        lax.psum_scatter(part_gate, "dp", scatter_dimension=1, tiled=True),
        lax.psum_scatter(part_up, "dp", scatter_dimension=1, tiled=True),
        lax.psum_scatter(part_down, "dp", scatter_dimension=1, tiled=True),
    )
    grad_gate_w = summed_gate.astype(jnp.bfloat16)
    grad_up_w = summed_up.astype(jnp.bfloat16)
    grad_down_w = summed_down.astype(jnp.bfloat16)
    out_rows = out_rows.reshape(n_expert * local_experts, slots, width)
    dx_rows = dx_rows.reshape(n_expert * local_experts, slots, width)
    back_out, back_dx = (
        lax.all_to_all(out_rows, "expert", split_axis=0, concat_axis=0, tiled=True),
        lax.all_to_all(dx_rows, "expert", split_axis=0, concat_axis=0, tiled=True),
    )
    picked_out = jnp.take(
        back_out.reshape(-1, width), slot_index, axis=0, mode="fill", fill_value=0
    )
    picked_dx = jnp.take(back_dx.reshape(-1, width), slot_index, axis=0, mode="fill", fill_value=0)
    picked_out = picked_out.reshape(tok_rows, top_count, width).astype(jnp.float32)
    picked_dx = picked_dx.reshape(tok_rows, top_count, width).astype(jnp.float32)
    layer_out = jnp.sum(gate_vals[:, :, None] * picked_out, axis=1).astype(jnp.bfloat16)
    grad_tokens = jnp.sum(picked_dx, axis=1).astype(jnp.bfloat16)
    grad_gates = jnp.sum(cotangent.astype(jnp.float32)[:, None, :] * picked_out, axis=-1)
    return (layer_out, grad_tokens, grad_gates, grad_gate_w, grad_up_w, grad_down_w)


def solution(mesh):
    placed = (
        P(("expert", "dp"), None),
        P(("expert", "dp"), None),
        P(("expert", "dp"), None),
        P(("expert", "dp"), None),
        P(),
        P("expert", "dp", None),
        P("expert", "dp", None),
        P("expert", "dp", None),
    )
    return jax.shard_map(
        on_device,
        mesh=mesh,
        in_specs=placed,
        out_specs=(
            P(("expert", "dp"), None),
            P(("expert", "dp"), None),
            P(("expert", "dp"), None),
            P("expert", "dp", None),
            P("expert", "dp", None),
            P("expert", "dp", None),
        ),
        check_vma=False,
    )
```

profile of v0, /device:TPU:13, one launch (start us, length us, event | category | flops | bytes accessed | tf_op | source)
XLA Modules:
  0.0 526.3 jit_solution(4731755545639999676)
XLA Ops:
  11.5 15.5 %all-gather = s32[16,1,16]{2,1,0:T(1,128)S(1)} all-gather(s32[1,1,16]{2,1,0:T(1,128)S(1)} %bitcast.121), channel_id=1, replica_groups=mesh['expert'=16,'dp'=2] {'expert'}, dimensions={0}, use_global_device_ids=true | all-gather | bytes 1088 | tf_op jit(solution)/shard_map/all_gather | solution.py:9
  32.0 4.9 reshape.202
  36.9 9.2 %scatter_custom_fusion = bf16[960,2048]{1,0:T(8,128)(2,1)} fusion(s32[768]{0:T(1024)S(1)} %fusion.27, bf16[768,2048]{1,0:T(8,128)(2,1)S(1)} %reshape.202, bf16[]{:T(256)} %constant.54.clone.1), kind=kCustom, calls=%fused_computation.19 | custom fusion | bytes 3932162 | tf_op jit(solution)/shard_map/scatter | solution.py:51
  46.1 4.9 reshape.170
  51.0 11.6 %all-to-all-start = ((bf16[16,60,2048]{2,1,0:T(8,128)(2,1)}), bf16[16,60,2048]{2,1,0:T(8,128)(2,1)}, u32[]{:S(2)}, u32[]{:S(2)}) async-start(bf16[16,60,2048]{2,1,0:T(8,128)(2,1)} %reshape.170), calls=%async_computation | async-start | bytes 8388608 | tf_op jit(solution)/shard_map/all_to_all | solution.py:66
  67.2 8.3 %mul.107 = f32[768,2048]{1,0:T(8,128)} reshape(f32[128,6,2048]{2,1,0:T(8,128)} %mul.106) | data formatting | bytes 12582912 | tf_op jit(solution)/shard_map/mul | solution.py:44
  75.4 14.3 %scatter_custom_fusion.1 = bf16[960,2048]{1,0:T(8,128)(2,1)} fusion(s32[768]{0:T(1024)S(1)} %fusion.27, f32[768,2048]{1,0:T(8,128)} %mul.107, f32[768]{0:T(1024)S(1)} %mul.104, bf16[]{:T(256)} %constant.54.clone.1), kind=kCustom, calls=%fused_computation.11 | custom fusion | flops 3145728 | bytes 10227714 | tf_op jit(solution)/shard_map/scatter | solution.py:56
  89.8 4.9 reshape.176
  94.6 60.3 %all-to-all-done = bf16[16,60,2048]{2,1,0:T(8,128)(2,1)} async-done(((bf16[16,60,2048]{2,1,0:T(8,128)(2,1)}), bf16[16,60,2048]{2,1,0:T(8,128)(2,1)}, u32[]{:S(2)}, u32[]{:S(2)}) %all-to-all-start) | async-done | bytes 3932192 | tf_op jit(solution)/shard_map/all_to_all | solution.py:66
  162.3 27.7 %all-gather.7.cloned.1.call-done = bf16[1,384,2048]{2,1,0:T(8,128)(2,1)} async-done(((bf16[1,192,2048]{2,1,0:T(8,128)(2,1)}), bf16[1,384,2048]{2,1,0:T(8,128)(2,1)}) %all-gather.7.cloned.1.call-update) | async-done | bytes 1572880 | tf_op jit(solution)/shard_map/all_gather | solution.py:62
  190.0 6.2 %fusion.13 = f32[16,60,384]{2,1,0:T(8,128)} fusion(bf16[16,60,2048]{2,1,0:T(8,128)(2,1)} %all-to-all-done, bf16[1,384,2048]{2,1,0:T(8,128)(2,1)} %all-gather.7.cloned.1.call-done), kind=kOutput, calls=%fused_computation.32 | convolution fusion | flops 1509949440 | bytes 6979584 | tf_op jit(solution)/shard_map/secd,efd->secf/dot_general | solution.py:71
  196.2 22.6 %all-gather.9.cloned.1.call-done = bf16[1,384,2048]{2,1,0:T(8,128)(2,1)} async-done(((bf16[1,192,2048]{2,1,0:T(8,128)(2,1)}), bf16[1,384,2048]{2,1,0:T(8,128)(2,1)}) %all-gather.9.cloned.1.call-update) | async-done | bytes 1572880 | tf_op jit(solution)/shard_map/all_gather | solution.py:63
  218.8 33.5 %all-to-all-done.2 = bf16[16,60,2048]{2,1,0:T(8,128)(2,1)} async-done(((bf16[16,60,2048]{2,1,0:T(8,128)(2,1)}), bf16[16,60,2048]{2,1,0:T(8,128)(2,1)}, u32[]{:S(2)}, u32[]{:S(2)}) %all-to-all-start.2) | async-done | bytes 3932192 | tf_op jit(solution)/shard_map/all_to_all | solution.py:67
  252.3 6.2 %fusion.9 = f32[16,60,384]{2,1,0:T(8,128)} fusion(bf16[16,60,2048]{2,1,0:T(8,128)(2,1)} %all-to-all-done.2, bf16[1,384,2048]{2,1,0:T(8,128)(2,1)} %all-gather.9.cloned.1.call-done), kind=kOutput, calls=%fused_computation.28 | convolution fusion | flops 1509949440 | bytes 6979584 | tf_op jit(solution)/shard_map/secd,efd->secf/dot_general | solution.py:79
  258.4 6.4 %fusion.23 = (bf16[16,60,384]{2,1,0:T(8,128)(2,1)S(1)}, bf16[16,1,60,384]{3,2,0,1:T(8,128)(2,1)S(1)}, bf16[16,60,384]{2,1,0:T(8,128)(2,1)S(1)}) fusion(f32[16,60,384]{2,1,0:T(8,128)} %fusion.9, f32[16,60,384]{2,1,0:T(8,128)} %fusion.13, bf16[16,60,2048]{2,1,0:T(8,128)(2,1)} %all-to-all-done, bf16[1,384,2048]{2,1,0:T(8,128)(2,1)} %all-gather.5.cloned.1.call-done), kind=kOutput, calls=%fused_computation.44 | convolution fusion | flops 1515110400 | bytes 10665984 | tf_op jit(solution)/shard_map/secd,efd->secf/dot_general | solution.py:70
  264.9 5.7 %convolution_bitcast_fusion = f32[1,384,2048]{2,1,0:T(8,128)} fusion(bf16[16,60,384]{2,1,0:T(8,128)(2,1)S(1)} %get-tuple-element.135, bf16[16,60,2048]{2,1,0:T(8,128)(2,1)} %all-to-all-done.2), kind=kOutput, calls=%fused_computation.15 | convolution fusion | flops 1509949440 | bytes 7815168 | tf_op jit(solution)/shard_map/secf,secd->efd/dot_general | solution.py:88
  270.6 5.7 %convolution_convert_fusion = bf16[16,60,2048]{2,1,0:T(8,128)(2,1)} fusion(bf16[16,60,384]{2,1,0:T(8,128)(2,1)S(1)} %get-tuple-element.135, bf16[1,384,2048]{2,1,0:T(8,128)(2,1)} %all-gather.9.cloned.1.call-done), kind=kOutput, calls=%fused_computation.10 | convolution fusion | flops 1511915520 | bytes 6242304 | tf_op jit(solution)/shard_map/secf,efd->secd/dot_general | solution.py:75
  276.3 4.9 all-to-all-start.1
  281.7 5.6 %convolution_bitcast_fusion.2 = f32[1,384,2048]{2,1,0:T(8,128)} fusion(bf16[16,60,2048]{2,1,0:T(8,128)(2,1)} %all-to-all-done, bf16[16,1,60,384]{3,2,0,1:T(8,128)(2,1)S(1)} %get-tuple-element.134), kind=kOutput, calls=%fused_computation.17 | convolution fusion | flops 1509949440 | bytes 7815168 | tf_op jit(solution)/shard_map/secf,secd->efd/dot_general | solution.py:89
  295.6 78.1 %all-to-all-done.1 = bf16[16,60,2048]{2,1,0:T(8,128)(2,1)} async-done(((bf16[16,60,2048]{2,1,0:T(8,128)(2,1)}), bf16[16,60,2048]{2,1,0:T(8,128)(2,1)}, u32[]{:S(2)}, u32[]{:S(2)}) %all-to-all-start.1) | async-done | bytes 3932192 | tf_op jit(solution)/shard_map/all_to_all | solution.py:102
  373.7 4.9 all-to-all-start.3
  378.7 5.7 %convolution_bitcast_fusion.1 = f32[1,384,2048]{2,1,0:T(8,128)} fusion(bf16[16,60,384]{2,1,0:T(8,128)(2,1)S(1)} %get-tuple-element.133, bf16[16,60,2048]{2,1,0:T(8,128)(2,1)} %all-to-all-done), kind=kOutput, calls=%fused_computation.16 | convolution fusion | flops 1509949440 | bytes 7815168 | tf_op jit(solution)/shard_map/secf,secd->efd/dot_general | solution.py:90
  389.2 39.2 %reduce-scatter.6.cloned.1.call-done = f32[1,192,2048]{2,1,0:T(8,128)} async-done(((f32[1,384,2048]{2,1,0:T(8,128)}), f32[1,192,2048]{2,1,0:T(8,128)}) %reduce-scatter.6.cloned.1.call-update) | async-done | bytes 1572880 | tf_op jit(solution)/shard_map/reduce_scatter | solution.py:93
  430.8 5.0 reshape.175
  435.9 9.0 %gather_fusion = bf16[768,2048]{1,0:T(8,128)(2,1)S(1)} fusion(bf16[960,2048]{1,0:T(8,128)(2,1)} %reshape.175, s32[1024]{0:T(1024)S(1)} %pad_clamp_fusion), kind=kCustom, calls=%fused_computation.clone | custom fusion | bytes 6294528 | tf_op jit(solution)/shard_map/jit(_take)/gather | solution.py:105
  449.4 21.7 %all-to-all-done.3 = bf16[16,60,2048]{2,1,0:T(8,128)(2,1)} async-done(((bf16[16,60,2048]{2,1,0:T(8,128)(2,1)}), bf16[16,60,2048]{2,1,0:T(8,128)(2,1)}, u32[]{:S(2)}, u32[]{:S(2)}) %all-to-all-start.3) | async-done | bytes 3932192 | tf_op jit(solution)/shard_map/all_to_all | solution.py:103
  475.9 9.7 %gather_fusion.1 = bf16[768,2048]{1,0:T(8,128)(2,1)} fusion(bf16[960,2048]{1,0:T(8,128)(2,1)} %reshape.179, s32[1024]{0:T(1024)S(1)} %pad_clamp_fusion), kind=kCustom, calls=%fused_computation.1.clone | custom fusion | bytes 6294528 | tf_op jit(solution)/shard_map/jit(_take)/gather | solution.py:108
  485.7 6.2 %broadcast_select_fusion.2 = (bf16[768,2048]{1,0:T(8,128)(2,1)}, f32[768,2048]{1,0:T(8,128)}) fusion(bf16[768,2048]{1,0:T(8,128)(2,1)} %gather_fusion.1, pred[768]{0:T(1024)(128)(4,1)S(1)} %get-tuple-element.131, bf16[768,2048]{1,0:T(8,128)(2,1)S(1)} %gather_fusion), kind=kLoop, calls=%fused_computation.14 | loop fusion | flops 4718592 | bytes 15729408 | tf_op jit(solution)/shard_map/jit(_take)/select_n | solution.py:108
  491.9 6.3 %reshape.180 = bf16[128,6,2048]{2,1,0:T(8,128)(2,1)} reshape(bf16[768,2048]{1,0:T(8,128)(2,1)} %get-tuple-element.136) | data formatting | bytes 6291456 | tf_op jit(solution)/shard_map/reshape | solution.py:110
  498.1 5.7 %reduce_sum.69 = bf16[128,2048]{1,0:T(8,128)(2,1)} reduce(bf16[128,6,2048]{2,1,0:T(8,128)(2,1)} %reshape.180, bf16[]{:T(256)} %constant.54.clone.1), dimensions={1}, to_apply=%region_10.12 | reduce | flops 1310720 | bytes 3670018 | tf_op jit(solution)/shard_map/reduce_sum | solution.py:112
  503.8 8.0 %reshape.181 = f32[128,6,2048]{2,1,0:T(8,128)} reshape(f32[768,2048]{1,0:T(8,128)} %get-tuple-element.137) | data formatting | bytes 12582912 | tf_op jit(solution)/shard_map/convert_element_type | solution.py:109
  511.9 7.4 %multiply_reduce_fusion = bf16[128,2048]{1,0:T(8,128)(2,1)} fusion(f32[128,6,2048]{2,1,0:T(8,128)} %reshape.181, f32[128,6]{1,0:T(8,128)S(1)} %copy.29), kind=kLoop, calls=%fused_computation.7 | loop fusion | flops 2883584 | bytes 6818816 | tf_op jit(solution)/shard_map/reduce_sum | solution.py:111
  (71 shorter events, 46.8 us)
Async XLA Ops:
  51.0 11.6 %copy-start.3 = (f32[128,6]{0,1:T(8,128)S(1)}, f32[128,6]{0,1:T(8,128)}, u32[]{:S(2)}) copy-start(f32[128,6]{0,1:T(8,128)} %param.15) | copy-start | bytes 9220
  51.0 11.8 %copy-start.2 = (bf16[128,2048]{1,0:T(8,128)(2,1)S(1)}, bf16[128,2048]{1,0:T(8,128)(2,1)}, u32[]{:S(2)}) copy-start(bf16[128,2048]{1,0:T(8,128)(2,1)} %param.13) | copy-start | bytes 1572868
  51.0 103.9 %all-to-all-start = ((bf16[16,60,2048]{2,1,0:T(8,128)(2,1)}), bf16[16,60,2048]{2,1,0:T(8,128)(2,1)}, u32[]{:S(2)}, u32[]{:S(2)}) async-start(bf16[16,60,2048]{2,1,0:T(8,128)(2,1)} %reshape.170), calls=%async_computation | async-start | bytes 8388608 | tf_op jit(solution)/shard_map/all_to_all | solution.py:66
  154.9 97.3 %all-to-all-start.2 = ((bf16[16,60,2048]{2,1,0:T(8,128)(2,1)}), bf16[16,60,2048]{2,1,0:T(8,128)(2,1)}, u32[]{:S(2)}, u32[]{:S(2)}) async-start(bf16[16,60,2048]{2,1,0:T(8,128)(2,1)} %reshape.176), calls=%async_computation.2 | async-start | bytes 8388608 | tf_op jit(solution)/shard_map/all_to_all | solution.py:67
  159.8 30.2 %all-gather.7.cloned.1.call-start = ((), (), s32[]{:S(2)}) async-start(), calls=%async_computation.8 | async-start | bytes 2359296 | tf_op jit(solution)/shard_map/all_gather | solution.py:62
  160.5 58.2 %all-gather.9.cloned.1.call-start = ((), (), s32[]{:S(2)}) async-start(), calls=%async_computation.9 | async-start | bytes 2359296 | tf_op jit(solution)/shard_map/all_gather | solution.py:63
  161.3 97.2 %all-gather.5.cloned.1.call-start = ((), (), s32[]{:S(2)}) async-start(), calls=%async_computation.7 | async-start | bytes 2359296 | tf_op jit(solution)/shard_map/all_gather | solution.py:61
  162.0 222.4 %reduce-scatter.8.cloned.1.call-start = ((), (), s32[]{:S(2)}) async-start(), calls=%async_computation.12 | async-start | bytes 4718592 | tf_op jit(solution)/shard_map/reduce_scatter | solution.py:94
  276.3 97.4 %all-to-all-start.1 = ((bf16[16,60,2048]{2,1,0:T(8,128)(2,1)}), bf16[16,60,2048]{2,1,0:T(8,128)(2,1)}, u32[]{:S(2)}, u32[]{:S(2)}) async-start(bf16[16,60,2048]{2,1,0:T(8,128)(2,1)} %convolution_convert_fusion), calls=%async_computation.1 | async-start | bytes 8388608 | tf_op jit(solution)/shard_map/all_to_all | solution.py:102
  281.2 105.6 %reduce-scatter.4.cloned.1.call-start = ((), (), s32[]{:S(2)}) async-start(), calls=%async_computation.10 | async-start | bytes 4718592 | tf_op jit(solution)/shard_map/reduce_scatter | solution.py:92
  287.4 1.5 copy-start.1
  288.9 2.3 copy-start
  373.7 97.4 %all-to-all-start.3 = ((bf16[16,60,2048]{2,1,0:T(8,128)(2,1)}), bf16[16,60,2048]{2,1,0:T(8,128)(2,1)}, u32[]{:S(2)}, u32[]{:S(2)}) async-start(bf16[16,60,2048]{2,1,0:T(8,128)(2,1)} %add_convert_fusion), calls=%async_computation.3 | async-start | bytes 8388608 | tf_op jit(solution)/shard_map/all_to_all | solution.py:103
  378.6 49.8 %reduce-scatter.6.cloned.1.call-start = ((), (), s32[]{:S(2)}) async-start(), calls=%async_computation.11 | async-start | bytes 4718592 | tf_op jit(solution)/shard_map/reduce_scatter | solution.py:93
Sparse Core Ops, SparseCore 0:
  162.2 27.7 all-gather.6
  191.5 27.2 all-gather.8
  220.3 27.1 all-gather.4
  270.7 42.8 reduce-scatter.7
  315.8 43.3 reduce-scatter.3
  384.5 43.8 reduce-scatter.5
where the time goes:
time: 534 us; the launch traced here: 526 us
  waiting for transfers between devices  285 us (53%)
  local copies, waits for them, and re-layouts  87.2 us (16%)
  matrix products  48.3 us (9%)
  other arithmetic  48.1 us (9%)
  starting transfers between devices  27.2 us (5%)
  blocking collectives  15.5 us (3%)
  between operations  14.5 us (3%)
    all_to_all x1, waiting for transfers between devices, on_device(): lax.all_to_all(out_rows, 'expert', split_axis=0, concat_axis=0, tiled=True)  78.1 us
    all_to_all x1, waiting for transfers between devices, on_device(): lax.all_to_all(input_buf, 'expert', split_axis=0, concat_axis=0, tiled=True)  60.3 us
    reduce_scatter x1, waiting for transfers between devices, on_device(): lax.psum_scatter(part_up, 'dp', scatter_dimension=1, tiled=True)  39.2 us
    all_to_all x1, waiting for transfers between devices, on_device(): lax.all_to_all(cot_buf, 'expert', split_axis=0, concat_axis=0, tiled=True)  33.5 us
    all_gather x1, waiting for transfers between devices, on_device(): lax.all_gather(w_up, 'dp', axis=1, tiled=True)  27.7 us
    all_gather x1, waiting for transfers between devices, on_device(): lax.all_gather(w_down, 'dp', axis=1, tiled=True)  22.6 us
    all_to_all x1, waiting for transfers between devices, on_device(): lax.all_to_all(dx_rows, 'expert', split_axis=0, concat_axis=0, tiled=True)  21.7 us
    all_gather x1, blocking collectives, entering(): pieces = lax.all_gather(value, axis)  15.5 us
  transfers between devices with their start and end apart: 10, of which 7 were waited for; matrix products, arithmetic and copies ran while one was open for 18% of the time, Pallas kernels for 0%

commit v1 on v0

v1 whole, which is shorter than its diff:
```python
import jax
import jax.numpy as jnp
import numpy as np
from jax import lax
from jax.sharding import Mesh
from jax.sharding import PartitionSpec as P


def shifted(value, axis, count, shift):
    return lax.ppermute(value, axis, [(j, (j + shift) % count) for j in range(count)])


def on_device(tokens, cotangent, expert_ids, gate_vals, capacity, w_gate, w_up, w_down):
    tok_rows, width = tokens.shape
    top_count = expert_ids.shape[1]
    experts = capacity.shape[0]
    local_experts, hidden_part, _ = w_gate.shape
    slots = max(2, (5 * tok_rows * top_count + 4 * experts - 1) // (4 * experts))
    n_in = lax.axis_size("inner")
    n_dp = lax.axis_size("dp")
    half = lax.axis_index("half")
    source = half * n_in + lax.axis_index("inner")
    n_src = 2 * n_in
    half_experts = n_in * local_experts
    half_rows = half_experts * slots

    both_rows = jnp.concatenate([tokens, cotangent], axis=1)
    partner_rows = shifted(both_rows, "half", 2, 1)
    partner_gates = shifted(gate_vals, "half", 2, 1)

    weights = jnp.concatenate([w_gate, w_up, w_down], axis=0)
    pieces = [weights] + [shifted(weights, "dp", n_dp, d) for d in range(1, n_dp)]
    full = jnp.concatenate(pieces, axis=1)
    full_gate = full[:local_experts]
    full_up = full[local_experts : 2 * local_experts]
    full_down = full[2 * local_experts :]

    flat_ids = expert_ids.reshape(-1)
    one_hot = (flat_ids[:, None] == jnp.arange(experts, dtype=jnp.int32)[None, :]).astype(jnp.int32)
    running = jnp.cumsum(one_hot, axis=0)
    local_rank = jnp.sum(running * one_hot, axis=1) - 1
    counts = running[-1]
    all_counts = lax.all_gather(counts, ("half", "inner"))
    lower = jnp.arange(n_src, dtype=jnp.int32)[:, None] < source
    earlier = jnp.sum(jnp.where(lower, all_counts, 0), axis=0)
    offset = jnp.sum(one_hot * earlier[None, :], axis=1)
    limit = jnp.sum(one_hot * capacity[None, :], axis=1)
    kept = offset + local_rank < limit
    code = jnp.where(kept, flat_ids * slots + local_rank, -1).reshape(tok_rows, top_count)
    partner_code = shifted(code, "half", 2, 1)

    def place(codes):
        local = codes // slots - half * half_experts
        inside = (codes >= 0) & (local >= 0) & (local < half_experts)
        return jnp.where(inside, local * slots + codes % slots, -1)

    own_place = place(code)
    partner_place = place(partner_code)

    all_rows = jnp.stack([both_rows, partner_rows])
    all_gates = jnp.stack([gate_vals, partner_gates])
    all_place = jnp.stack([own_place, partner_place])
    x_routes = jnp.broadcast_to(all_rows[:, :, None, :width], (2, tok_rows, top_count, width))
    c_routes = (
        all_gates[:, :, :, None] * all_rows[:, :, None, width:].astype(jnp.float32)
    ).astype(jnp.bfloat16)
    routes = jnp.concatenate([x_routes, c_routes], axis=-1).reshape(-1, 2 * width)
    side = jnp.arange(2, dtype=jnp.int32)[:, None, None]
    dest = jnp.where(
        all_place >= 0,
        (all_place // slots * 2 + side) * slots + all_place % slots,
        2 * half_rows,
    ).reshape(-1)
    send = jnp.zeros((2 * half_rows, 2 * width), jnp.bfloat16).at[dest].set(routes, mode="drop")
    send = send.reshape(half_experts, 2 * slots, 2 * width)
    got = lax.all_to_all(send, "inner", split_axis=0, concat_axis=0, tiled=True)
    got = got.reshape(n_in, local_experts, 2 * slots, 2 * width).transpose(1, 0, 2, 3)
    got = got.reshape(local_experts, n_in * 2 * slots, 2 * width)
    rows_in = got[:, :, :width]
    rows_cot = got[:, :, width:]

    gate_pre = jnp.einsum("erd,efd->erf", rows_in, full_gate, preferred_element_type=jnp.float32)
    up_pre = jnp.einsum("erd,efd->erf", rows_in, full_up, preferred_element_type=jnp.float32)
    sigmoid_gate = jax.nn.sigmoid(gate_pre)
    activated = gate_pre * sigmoid_gate
    hidden = (activated * up_pre).astype(jnp.bfloat16)
    out_rows = jnp.einsum(
        "erf,efd->erd", hidden, full_down, preferred_element_type=jnp.float32
    ).astype(jnp.bfloat16)
    d_hidden = jnp.einsum("erd,efd->erf", rows_cot, full_down, preferred_element_type=jnp.float32)
    d_gate = (d_hidden * up_pre * (sigmoid_gate + activated * (1.0 - sigmoid_gate))).astype(
        jnp.bfloat16
    )
    d_up = (d_hidden * activated).astype(jnp.bfloat16)
    dx_rows = jnp.einsum("erf,efd->erd", d_gate, full_gate, preferred_element_type=jnp.float32)
    dx_rows = (
        dx_rows + jnp.einsum("erf,efd->erd", d_up, full_up, preferred_element_type=jnp.float32)
    ).astype(jnp.bfloat16)
    part_down = jnp.einsum("erf,erd->efd", hidden, rows_cot, preferred_element_type=jnp.float32)
    part_gate = jnp.einsum("erf,erd->efd", d_gate, rows_in, preferred_element_type=jnp.float32)
    part_up = jnp.einsum("erf,erd->efd", d_up, rows_in, preferred_element_type=jnp.float32)

    back = jnp.concatenate([out_rows, dx_rows], axis=-1)
    back = back.reshape(local_experts, n_in, 2 * slots, 2 * width).transpose(1, 0, 2, 3)
    back = back.reshape(half_experts, 2 * slots, 2 * width)
    back = lax.all_to_all(back, "inner", split_axis=0, concat_axis=0, tiled=True)
    back = back.reshape(half_experts, 2, slots, 2 * width)

    parts = jnp.concatenate([part_gate, part_up, part_down], axis=0)
    summed = parts[:, :hidden_part]
    for d in range(1, n_dp):
        block = parts[:, d * hidden_part : (d + 1) * hidden_part].astype(jnp.bfloat16)
        summed = summed + shifted(block, "dp", n_dp, -d).astype(jnp.float32)
    summed = summed.astype(jnp.bfloat16)
    grad_gate_w = summed[:local_experts]
    grad_up_w = summed[local_experts : 2 * local_experts]
    grad_down_w = summed[2 * local_experts :]

    columns = jnp.arange(half_rows, dtype=jnp.int32)

    def combine(which):
        rows = back[:, which].reshape(half_rows, 2 * width)
        out_part = rows[:, :width]
        dx_part = rows[:, width:]
        hit = all_place[which][:, :, None] == columns[None, None, :]
        weight = jnp.sum(jnp.where(hit, all_gates[which][:, :, None], 0.0), axis=1)
        ones = jnp.sum(hit.astype(jnp.float32), axis=1).astype(jnp.bfloat16)
        layer = jnp.dot(
            weight, out_part.astype(jnp.float32), precision=lax.Precision.HIGHEST,
            preferred_element_type=jnp.float32,
        )
        grads = jnp.dot(ones, dx_part, preferred_element_type=jnp.float32)
        scores = jnp.dot(
            all_rows[which][:, width:], out_part.T, preferred_element_type=jnp.float32
        )
        gates = jnp.sum(jnp.where(hit, scores[:, None, :], 0.0), axis=2)
        return layer, grads, gates

    partner_layer, partner_grads, partner_gg = combine(1)
    returned = shifted(
        jnp.concatenate([partner_layer, partner_grads], axis=1).astype(jnp.bfloat16), "half", 2, 1
    )
    returned_gg = shifted(partner_gg, "half", 2, 1)
    own_layer, own_grads, own_gg = combine(0)
    layer_out = (own_layer + returned[:, :width].astype(jnp.float32)).astype(jnp.bfloat16)
    grad_tokens = (own_grads + returned[:, width:].astype(jnp.float32)).astype(jnp.bfloat16)
    grad_gates = own_gg + returned_gg
    return (layer_out, grad_tokens, grad_gates, grad_gate_w, grad_up_w, grad_down_w)


def solution(mesh):
    n_expert = mesh.shape["expert"]
    n_dp = mesh.shape["dp"]
    devices = np.asarray(mesh.devices).reshape(2, n_expert // 2, n_dp)
    split = Mesh(devices, ("half", "inner", "dp"))
    rows = P(("half", "inner", "dp"), None)
    weights = P(("half", "inner"), "dp", None)
    return jax.shard_map(
        on_device,
        mesh=split,
        in_specs=(rows, rows, rows, rows, P(), weights, weights, weights),
        out_specs=(rows, rows, rows, weights, weights, weights),
        check_vma=False,
    )
```

time: 534 us -> 468 us (0.88)
  the two profiles are of different devices: /device:TPU:13 before, /device:TPU:0 now
where the time goes in v1:
time: 468 us; the launch traced here: 463 us
  waiting for transfers between devices  182 us (39%)
  local copies, waits for them, and re-layouts  103 us (22%)
  other arithmetic  52.5 us (11%)
  matrix products  49.8 us (11%)
  starting transfers between devices  39.9 us (9%)
  blocking collectives  34.4 us (7%)
    ppermute x7, waiting for transfers between devices, shifted(): lax.ppermute(value, axis, [(j, (j + shift) % count) for j in range(count)])  82.4 us
    all_to_all x1, waiting for transfers between devices, on_device(): lax.all_to_all(back, 'inner', split_axis=0, concat_axis=0, tiled=True)  67.1 us
    all_gather x1, blocking collectives, on_device(): all_counts = lax.all_gather(counts, ('half', 'inner'))  34.4 us
    all_to_all x1, waiting for transfers between devices, on_device(): got = lax.all_to_all(send, 'inner', split_axis=0, concat_axis=0, tiled=True)  32.4 us
    ppermute x7, starting transfers between devices, shifted(): lax.ppermute(value, axis, [(j, (j + shift) % count) for j in range(count)])  29.5 us
    concatenate x3, local copies, waits for them, and re-layouts, on_device(): jnp.concatenate([x_routes, c_routes], axis=-1).reshape(-1, 2 * width)  28.6 us
    scatter x1, other arithmetic, on_device(): jnp.zeros((2 * half_rows, 2 * width), jnp.bfloat16).at[dest]  24.8 us
    mul x3, local copies, waits for them, and re-layouts, on_device(): all_gates[:, :, :, None] * all_rows[:, :, None, width:].astype(jnp.float32)  24.2 us
  transfers between devices with their start and end apart: 9, of which 5 were waited for; matrix products, arithmetic and copies ran while one was open for 14% of the time, Pallas kernels for 0%

profile of v1, /device:TPU:0, one launch (start us, length us, event | category | flops | bytes accessed | tf_op | source)
XLA Modules:
  0.0 462.6 jit_solution(15959298366253839287)
XLA Ops:
  2.8 4.1 collective-permute-start.1
  10.3 34.4 %all-gather = s32[16,1,16]{2,1,0:T(1,128)S(1)} all-gather(s32[1,1,16]{2,1,0:T(1,128)S(1)} %bitcast.90), channel_id=1, replica_groups=mesh['half'=2,'inner'=8,'dp'=2] {'half','inner'}, dimensions={0}, use_global_device_ids=true | all-gather | bytes 1088 | tf_op jit(solution)/shard_map/all_gather | solution.py:43
  46.9 19.2 %collective-permute-start = (s32[128,6]{1,0:T(8,128)S(1)}, s32[128,6]{1,0:T(8,128)S(1)}, u32[]{:S(2)}, u32[]{:S(2)}) collective-permute-start(s32[128,6]{1,0:T(8,128)S(1)} %get-tuple-element.16), channel_id=1, source_target_pairs={{0,16},{16,0},{1,17},{17,1},{2,18},{18,2},{3,19},{19,3},{4,20},{20... | collective-permute-start | bytes 9224 | tf_op jit(solution)/shard_map/ppermute | solution.py:10
  74.8 7.9 %mul.120 = f32[2,128,6,2048]{3,2,1,0:T(8,128)} broadcast(f32[2,128,2048]{2,1,0:T(8,128)S(1)} %get-tuple-element.25), dimensions={0,1,3} | broadcast | bytes 14680064 | tf_op jit(solution)/shard_map/mul | solution.py:65
  82.7 16.1 %mul.121 = f32[1536,2048]{1,0:T(8,128)} reshape(f32[2,128,6,2048]{3,2,1,0:T(8,128)} %mul.120) | data formatting | bytes 25165824 | tf_op jit(solution)/shard_map/mul | solution.py:65
  98.8 4.8 %broadcast_in_dim.82 = bf16[2,128,6,2048]{3,2,1,0:T(8,128)(2,1)} broadcast(bf16[2,128,2048]{2,1,0:T(8,128)(2,1)S(1)} %get-tuple-element.26), dimensions={0,1,3} | broadcast | bytes 7340032 | tf_op jit(solution)/shard_map/broadcast_in_dim | solution.py:63
  103.6 11.1 %concatenate.31 = bf16[1536,2048]{1,0:T(8,128)(2,1)} reshape(bf16[2,128,6,2048]{3,2,1,0:T(8,128)(2,1)} %broadcast_in_dim.82) | data formatting | bytes 12582912 | tf_op jit(solution)/shard_map/concatenate | solution.py:67
  114.7 8.0 %multiply_convert_fusion = bf16[1536,2048]{1,0:T(8,128)(2,1)} fusion(f32[1536,2048]{1,0:T(8,128)} %mul.121, f32[1536]{0:T(1024)S(1)} %mul.118), kind=kLoop, calls=%fused_computation.3 | loop fusion | flops 6291456 | bytes 18880512 | tf_op jit(solution)/shard_map/convert_element_type | solution.py:66
  122.7 8.5 %pad.10 = bf16[1536,4096]{1,0:T(8,128)(2,1)} pad(bf16[1536,2048]{1,0:T(8,128)(2,1)} %multiply_convert_fusion, bf16[]{:T(256)} %constant.84), padding=0_0x2048_0 | pad | bytes 18874370 | tf_op jit(solution)/shard_map/concatenate | solution.py:67
  131.1 9.0 %pad.9 = bf16[1536,4096]{1,0:T(8,128)(2,1)} pad(bf16[1536,2048]{1,0:T(8,128)(2,1)} %concatenate.31, bf16[]{:T(256)} %constant.84), padding=0_0x0_2048 | pad | bytes 18874370 | tf_op jit(solution)/shard_map/concatenate | solution.py:67
  140.2 24.8 %scatter_custom_fusion = bf16[960,4096]{1,0:T(8,128)(2,1)} fusion(s32[1536]{0:T(1024)S(1)} %fusion.47, bf16[1536,4096]{1,0:T(8,128)(2,1)} %pad.9, bf16[1536,4096]{1,0:T(8,128)(2,1)} %pad.10, bf16[]{:T(256)} %constant.73.clone.1), kind=kCustom, calls=%fused_computation.1 | custom fusion | flops 6291456 | bytes 33030146 | tf_op jit(solution)/shard_map/scatter | solution.py:74
  165.0 5.1 %all-to-all-start = ((bf16[8,120,4096]{2,1,0:T(8,128)(2,1)}), bf16[8,120,4096]{2,1,0:T(8,128)(2,1)}, u32[]{:S(2)}, u32[]{:S(2)}) async-start(bf16[8,120,4096]{2,1,0:T(8,128)(2,1)} %bitcast.78), calls=%async_computation | async-start | bytes 15728640 | tf_op jit(solution)/shard_map/all_to_all | solution.py:76
  173.2 52.1 %collective-permute-done.3 = bf16[3,192,2048]{2,1,0:T(8,128)(2,1)} collective-permute-done((bf16[3,192,2048]{2,1,0:T(8,128)(2,1)S(1)}, bf16[3,192,2048]{2,1,0:T(8,128)(2,1)}, u32[]{:S(2)}, u32[]{:S(2)}) %collective-permute-start.3) | collective-permute-done | bytes 2359328 | tf_op jit(solution)/shard_map/ppermute | solution.py:10
  225.3 32.4 %all-to-all-done = bf16[8,120,4096]{2,1,0:T(8,128)(2,1)} async-done(((bf16[8,120,4096]{2,1,0:T(8,128)(2,1)}), bf16[8,120,4096]{2,1,0:T(8,128)(2,1)}, u32[]{:S(2)}, u32[]{:S(2)}) %all-to-all-start) | async-done | bytes 7864352 | tf_op jit(solution)/shard_map/all_to_all | solution.py:76
  257.6 4.5 fusion.5
  262.1 4.5 fusion.8
  266.7 5.0 %multiply_convert_fusion.3 = (bf16[960,384]{1,0:T(8,128)(2,1)S(1)}, bf16[960,384]{1,0:T(8,128)(2,1)S(1)}, bf16[960,384]{1,0:T(8,128)(2,1)S(1)}) fusion(f32[960,384]{1,0:T(8,128)S(1)} %fusion.8, f32[960,384]{1,0:T(8,128)S(1)} %fusion.5, bf16[3,192,2048]{2,1,0:T(8,128)(2,1)S(1)} %constant_dynamic-update-slice_fusion.2, ...), kind=kOutput, calls=%fused_computation.53 | convolution fusion | flops 1518256128 | bytes 13811712 | tf_op jit(solution)/shard_map/erd,efd->erf/dot_general | solution.py:83
  271.7 5.8 %convolution_convert_fusion = bf16[960,2048]{1,0:T(8,128)(2,1)} fusion(bf16[960,384]{1,0:T(8,128)(2,1)S(1)} %get-tuple-element.19, bf16[3,192,2048]{2,1,0:T(8,128)(2,1)} %collective-permute-done.3, bf16[3,192,2048]{2,1,0:T(8,128)(2,1)S(1)} %constant_dynamic-update-slice_fusion.2), kind=kOutput, calls=%fused_computation.17 | convolution fusion | flops 1515061248 | bytes 9388032 | tf_op jit(solution)/shard_map/erf,efd->erd/dot_general | solution.py:87
  280.9 5.3 %add_convert_fusion = bf16[960,2048]{1,0:T(8,128)(2,1)} fusion(f32[960,2048]{1,0:T(8,128)S(1)} %fusion.53, bf16[960,384]{1,0:T(8,128)(2,1)S(1)} %get-tuple-element.20, bf16[3,192,2048]{2,1,0:T(8,128)(2,1)S(1)} %constant_dynamic-update-slice_fusion.2, bf16[3,192,2048]{2,1,0:T(8,128)(2,1)} %collective-permute-done.3), kind=kOutput, calls=%fused_computation.6 | convolution fusion | flops 1517027328 | bytes 17252352 | tf_op jit(solution)/shard_map/erf,efd->erd/dot_general | solution.py:95
  286.1 7.5 %pad_maximum_fusion.1 = bf16[8,120,4096]{2,1,0:T(8,128)(2,1)} fusion(bf16[8,120,2048]{2,1,0:T(8,128)(2,1)} %bitcast.80, bf16[8,120,2048]{2,1,0:T(8,128)(2,1)} %bitcast.81), kind=kLoop, calls=%fused_computation.5 | loop fusion | flops 15728640 | bytes 15728640 | tf_op jit(solution)/shard_map/concatenate | solution.py:103
  293.6 5.3 %all-to-all-start.1 = ((bf16[8,120,4096]{2,1,0:T(8,128)(2,1)}), bf16[8,120,4096]{2,1,0:T(8,128)(2,1)}, u32[]{:S(2)}, u32[]{:S(2)}) async-start(bf16[8,120,4096]{2,1,0:T(8,128)(2,1)} %pad_maximum_fusion.1), calls=%async_computation.1 | async-start | bytes 15728640 | tf_op jit(solution)/shard_map/all_to_all | solution.py:106
  299.1 4.0 convolution_bitcast_fusion.1
  303.1 4.0 convolution_bitcast_fusion
  307.1 4.0 fusion.6
  319.2 67.1 %all-to-all-done.1 = bf16[8,120,4096]{2,1,0:T(8,128)(2,1)} async-done(((bf16[8,120,4096]{2,1,0:T(8,128)(2,1)}), bf16[8,120,4096]{2,1,0:T(8,128)(2,1)}, u32[]{:S(2)}, u32[]{:S(2)}) %all-to-all-start.1) | async-done | bytes 7864352 | tf_op jit(solution)/shard_map/all_to_all | solution.py:106
  386.3 7.5 %copy.80 = bf16[8,120,4096]{2,0,1:T(8,128)(2,1)S(1)} copy(bf16[8,120,4096]{2,1,0:T(8,128)(2,1)} %all-to-all-done.1) | data formatting | bytes 15728640 | tf_op jit(solution)/shard_map/all_to_all | solution.py:106
  396.4 4.2 copy.83
  400.6 5.0 %reshape_squeeze.7 = bf16[480,4096]{1,0:T(8,128)(2,1)} reshape(bf16[8,1,60,4096]{3,2,0,1:T(8,128)(2,1)} %copy.83) | data formatting | bytes 7864320 | tf_op jit(solution)/shard_map/reshape;squeeze | solution.py:122
  411.9 3.9 fusion.2
  418.8 4.1 copy.81
  422.9 4.9 %reshape_squeeze.6 = bf16[480,4096]{1,0:T(8,128)(2,1)} reshape(bf16[8,1,60,4096]{3,2,0,1:T(8,128)(2,1)} %copy.81) | data formatting | bytes 7864320 | tf_op jit(solution)/shard_map/reshape;squeeze | solution.py:122
  431.7 26.7 %collective-permute-done.5 = f32[128,6]{0,1:T(8,128)S(1)} collective-permute-done((f32[128,6]{0,1:T(8,128)S(1)}, f32[128,6]{0,1:T(8,128)S(1)}, u32[]{:S(2)}, u32[]{:S(2)}) %collective-permute-start.5) | collective-permute-done | bytes 3104 | tf_op jit(solution)/shard_map/ppermute | solution.py:10
  (102 shorter events, 50.2 us)
Async XLA Ops:
  0.6 65.5 %copy-start.12 = (f32[128,6]{0,1:T(8,128)S(1)}, f32[128,6]{0,1:T(8,128)}, u32[]{:S(2)}) copy-start(f32[128,6]{0,1:T(8,128)} %param.11) | copy-start | bytes 9220
  2.8 69.2 %copy-start.4 = (bf16[128,4096]{1,0:T(8,128)(2,1)}, bf16[128,4096]{1,0:T(8,128)(2,1)S(1)}, u32[]{:S(2)}) copy-start(bf16[128,4096]{1,0:T(8,128)(2,1)S(1)} %constant_dynamic-update-slice_fusion) | copy-start | bytes 3145732
  2.8 69.1 %collective-permute-start.1 = (bf16[128,4096]{1,0:T(8,128)(2,1)S(1)}, bf16[128,4096]{1,0:T(8,128)(2,1)S(1)}, u32[]{:S(2)}, u32[]{:S(2)}) collective-permute-start(bf16[128,4096]{1,0:T(8,128)(2,1)S(1)} %constant_dynamic-update-slice_fusion), channel_id=1, source_target_pairs={{0,16},{16,0},{1,17},{17,1},{2,18},{18,2},{3,19},{19,3},{4,20},{20... | collective-permute-start | bytes 3145736 | tf_op jit(solution)/shard_map/ppermute | solution.py:10
  46.9 23.2 %collective-permute-start = (s32[128,6]{1,0:T(8,128)S(1)}, s32[128,6]{1,0:T(8,128)S(1)}, u32[]{:S(2)}, u32[]{:S(2)}) collective-permute-start(s32[128,6]{1,0:T(8,128)S(1)} %get-tuple-element.16), channel_id=1, source_target_pairs={{0,16},{16,0},{1,17},{17,1},{2,18},{18,2},{3,19},{19,3},{4,20},{20... | collective-permute-start | bytes 9224 | tf_op jit(solution)/shard_map/ppermute | solution.py:10
  66.1 5.5 %collective-permute-start.2 = (f32[128,6]{0,1:T(8,128)S(1)}, f32[128,6]{0,1:T(8,128)S(1)}, u32[]{:S(2)}, u32[]{:S(2)}) collective-permute-start(f32[128,6]{0,1:T(8,128)S(1)} %copy-done.12), channel_id=1, source_target_pairs={{0,16},{16,0},{1,17},{17,1},{2,18},{18,2},{3,19},{19,3},{4,20},{20... | collective-permute-start | bytes 9224 | tf_op jit(solution)/shard_map/ppermute | solution.py:10
  72.0 1.0 copy-start.5
  165.0 5.1 %copy-start.7 = (bf16[1,192,2048]{2,1,0:T(8,128)(2,1)S(1)}, bf16[1,192,2048]{2,1,0:T(8,128)(2,1)}, u32[]{:S(2)}) copy-start(bf16[1,192,2048]{2,1,0:T(8,128)(2,1)} %param.13) | copy-start | bytes 2359300
  165.0 92.6 %all-to-all-start = ((bf16[8,120,4096]{2,1,0:T(8,128)(2,1)}), bf16[8,120,4096]{2,1,0:T(8,128)(2,1)}, u32[]{:S(2)}, u32[]{:S(2)}) async-start(bf16[8,120,4096]{2,1,0:T(8,128)(2,1)} %bitcast.78), calls=%async_computation | async-start | bytes 15728640 | tf_op jit(solution)/shard_map/all_to_all | solution.py:76
  170.1 1.4 copy-start.8
  171.6 53.7 %collective-permute-start.3 = (bf16[3,192,2048]{2,1,0:T(8,128)(2,1)S(1)}, bf16[3,192,2048]{2,1,0:T(8,128)(2,1)}, u32[]{:S(2)}, u32[]{:S(2)}) collective-permute-start(bf16[3,192,2048]{2,1,0:T(8,128)(2,1)S(1)} %constant_dynamic-update-slice_fusion.2), channel_id=1, source_target_pairs={{0,1},{1,0},{2,3},{3,2},{4,5},{5,4},{6,7},{7,6},{8,9},{9,8},{10,11... | collective-permute-start | bytes 7077896 | tf_op jit(solution)/shard_map/ppermute | solution.py:10
  271.7 5.8 %copy-start.13 = (bf16[960,384]{1,0:T(8,128)(2,1)}, bf16[960,384]{1,0:T(8,128)(2,1)S(1)}, u32[]{:S(2)}) copy-start(bf16[960,384]{1,0:T(8,128)(2,1)S(1)} %get-tuple-element.19) | copy-start | bytes 2211844
  271.7 9.2 %copy-start.9 = (bf16[960,384]{1,0:T(8,128)(2,1)}, bf16[960,384]{1,0:T(8,128)(2,1)S(1)}, u32[]{:S(2)}) copy-start(bf16[960,384]{1,0:T(8,128)(2,1)S(1)} %get-tuple-element.20) | copy-start | bytes 2211844
  293.6 5.5 %copy-start.10 = (bf16[960,384]{1,0:T(8,128)(2,1)S(1)}, bf16[960,384]{1,0:T(8,128)(2,1)}, u32[]{:S(2)}) copy-start(bf16[960,384]{1,0:T(8,128)(2,1)} %copy-done.9) | copy-start | bytes 2211844
  293.6 92.7 %all-to-all-start.1 = ((bf16[8,120,4096]{2,1,0:T(8,128)(2,1)}), bf16[8,120,4096]{2,1,0:T(8,128)(2,1)}, u32[]{:S(2)}, u32[]{:S(2)}) async-start(bf16[8,120,4096]{2,1,0:T(8,128)(2,1)} %pad_maximum_fusion.1), calls=%async_computation.1 | async-start | bytes 15728640 | tf_op jit(solution)/shard_map/all_to_all | solution.py:106
  303.1 4.0 copy-start.14
  312.3 3.7 copy-start
  317.7 94.3 %collective-permute-start.6 = (bf16[3,192,2048]{2,1,0:T(8,128)(2,1)}, bf16[3,192,2048]{2,1,0:T(8,128)(2,1)}, u32[]{:S(2)}, u32[]{:S(2)}) collective-permute-start(bf16[3,192,2048]{2,1,0:T(8,128)(2,1)} %slice.187), channel_id=1, source_target_pairs={{0,1},{1,0},{2,3},{3,2},{4,5},{5,4},{6,7},{7,6},{8,9},{9,8},{10,11... | collective-permute-start | bytes 7077896 | tf_op jit(solution)/shard_map/ppermute | solution.py:10
  400.6 5.0 %copy-start.6 = (bf16[128,4096]{1,0:T(8,128)(2,1)S(1)}, bf16[128,4096]{1,0:T(8,128)(2,1)}, u32[]{:S(2)}) copy-start(bf16[128,4096]{1,0:T(8,128)(2,1)} %copy-done.5) | copy-start | bytes 3145732
  405.6 2.8 copy-start.1
  410.1 48.9 %collective-permute-start.4 = (bf16[128,4096]{1,0:T(8,128)(2,1)S(1)}, bf16[128,4096]{1,0:T(8,128)(2,1)S(1)}, u32[]{:S(2)}, u32[]{:S(2)}) collective-permute-start(bf16[128,4096]{1,0:T(8,128)(2,1)S(1)} %pad_maximum_fusion.4), channel_id=1, source_target_pairs={{0,16},{16,0},{1,17},{17,1},{2,18},{18,2},{3,19},{19,3},{4,20},{20... | collective-permute-start | bytes 3145736 | tf_op jit(solution)/shard_map/ppermute | solution.py:10
  415.8 3.0 copy-start.2
  422.9 6.0 %copy-start.11 = (bf16[128,2048]{1,0:T(8,128)(2,1)S(1)}, bf16[128,2048]{1,0:T(8,128)(2,1)}, u32[]{:S(2)}) copy-start(bf16[128,2048]{1,0:T(8,128)(2,1)} %param.9) | copy-start | bytes 1572868
  427.8 31.1 %copy-start.3 = (bf16[480,4096]{1,0:T(8,128)(2,1)S(1)}, bf16[480,4096]{1,0:T(8,128)(2,1)}, u32[]{:S(2)}) copy-start(bf16[480,4096]{1,0:T(8,128)(2,1)} %reshape_squeeze.6) | copy-start | bytes 11796484
  427.9 30.5 %collective-permute-start.5 = (f32[128,6]{0,1:T(8,128)S(1)}, f32[128,6]{0,1:T(8,128)S(1)}, u32[]{:S(2)}, u32[]{:S(2)}) collective-permute-start(f32[128,6]{0,1:T(8,128)S(1)} %get-tuple-element.6), channel_id=1, source_target_pairs={{0,16},{16,0},{1,17},{17,1},{2,18},{18,2},{3,19},{19,3},{4,20},{20... | collective-permute-start | bytes 9224 | tf_op jit(solution)/shard_map/ppermute | solution.py:10

commit v2 on v1

v2 whole, which is shorter than its diff:
```python
import jax
import jax.numpy as jnp
import numpy as np
from jax import lax
from jax.sharding import Mesh
from jax.sharding import PartitionSpec as P


def shifted(value, axis, count, shift):
    return lax.ppermute(value, axis, [(j, (j + shift) % count) for j in range(count)])


def in_three(value):
    first = value.astype(jnp.bfloat16)
    rest = value - first.astype(jnp.float32)
    second = rest.astype(jnp.bfloat16)
    third = (rest - second.astype(jnp.float32)).astype(jnp.bfloat16)
    return jnp.concatenate([first, second, third], axis=0)


def on_device(tokens, cotangent, expert_ids, gate_vals, capacity, w_gate, w_up, w_down):
    tok_rows, width = tokens.shape
    top_count = expert_ids.shape[1]
    experts = capacity.shape[0]
    local_experts, hidden_part, _ = w_gate.shape
    slots = max(2, (5 * tok_rows * top_count + 4 * experts - 1) // (4 * experts))
    n_in = lax.axis_size("inner")
    n_dp = lax.axis_size("dp")
    half = lax.axis_index("half")
    inner = lax.axis_index("inner")
    source = half * n_in + inner
    n_src = 2 * n_in
    half_experts = n_in * local_experts
    half_rows = half_experts * slots

    weights = jnp.concatenate([w_gate, w_up, w_down], axis=0)
    pieces = [weights] + [shifted(weights, "dp", n_dp, d) for d in range(1, n_dp)]

    both_rows = jnp.concatenate([tokens, cotangent], axis=1)
    partner_rows = shifted(both_rows, "half", 2, 1)
    partner_gates = shifted(gate_vals, "half", 2, 1)

    flat_ids = expert_ids.reshape(-1)
    one_hot = (flat_ids[:, None] == jnp.arange(experts, dtype=jnp.int32)[None, :]).astype(jnp.int32)
    running = jnp.cumsum(one_hot, axis=0)
    local_rank = jnp.sum(running * one_hot, axis=1) - 1
    counts = running[-1]
    count_rows = jnp.where(jnp.arange(n_src, dtype=jnp.int32)[:, None] == source, counts[None, :], 0)
    all_counts = lax.psum(count_rows, ("half", "inner"))
    code = (flat_ids * slots + local_rank).reshape(tok_rows, top_count)
    partner_code = shifted(code, "half", 2, 1)

    all_rows = jnp.concatenate([both_rows, partner_rows], axis=0)
    all_gates = jnp.concatenate([gate_vals, partner_gates], axis=0)
    all_code = jnp.concatenate([code, partner_code], axis=0)
    local = all_code // slots - half * half_experts
    inside = (local >= 0) & (local < half_experts)
    side = (jnp.arange(2 * tok_rows, dtype=jnp.int32) >= tok_rows).astype(jnp.int32)[:, None]
    dest = jnp.where(inside, (local * 2 + side) * slots + all_code % slots, 2 * half_rows)

    row_of = jnp.broadcast_to(jnp.arange(2 * tok_rows, dtype=jnp.int32)[:, None], dest.shape)
    filled_by = jnp.full((2 * half_rows,), -1, jnp.int32).at[dest.reshape(-1)].set(
        row_of.reshape(-1), mode="drop"
    )
    slot_gate = jnp.zeros((2 * half_rows,), jnp.float32).at[dest.reshape(-1)].set(
        all_gates.reshape(-1), mode="drop"
    )
    pick = (filled_by[:, None] == jnp.arange(2 * tok_rows, dtype=jnp.int32)[None, :]).astype(
        jnp.bfloat16
    )
    picked = jnp.dot(pick, all_rows, preferred_element_type=jnp.float32)
    send_x = picked[:, :width].astype(jnp.bfloat16)
    send_c = (slot_gate[:, None] * picked[:, width:]).astype(jnp.bfloat16)
    send = jnp.stack(
        [send_x.reshape(half_experts, 2 * slots, width), send_c.reshape(half_experts, 2 * slots, width)],
        axis=1,
    )
    got = lax.all_to_all(send, "inner", split_axis=0, concat_axis=0, tiled=True)
    got = got.reshape(n_in, local_experts, 2, 2, slots, width)

    earlier = jnp.cumsum(all_counts, axis=0) - all_counts
    holders = jnp.arange(n_in, dtype=jnp.int32)[:, None]
    halves = jnp.stack([half, 1 - half])[None, :]
    sources = halves * n_in + holders
    mine = (half * n_in + inner) * local_experts + jnp.arange(local_experts, dtype=jnp.int32)
    before = earlier[sources][:, :, mine].transpose(0, 2, 1)
    ranks = jnp.arange(slots, dtype=jnp.int32)
    keep = before[..., None] + ranks < capacity[mine][None, :, None, None]
    got = jnp.where(keep[:, :, None, :, :, None], got, jnp.zeros((), got.dtype))
    got = got.transpose(1, 2, 0, 3, 4, 5).reshape(local_experts, 2, n_in * 2 * slots, width)
    rows_in = got[:, 0]
    rows_cot = got[:, 1]

    full = jnp.concatenate(pieces, axis=1)
    full_gate = full[:local_experts]
    full_up = full[local_experts : 2 * local_experts]
    full_down = full[2 * local_experts :]

    gate_pre = jnp.einsum("erd,efd->erf", rows_in, full_gate, preferred_element_type=jnp.float32)
    up_pre = jnp.einsum("erd,efd->erf", rows_in, full_up, preferred_element_type=jnp.float32)
    sigmoid_gate = jax.nn.sigmoid(gate_pre)
    activated = gate_pre * sigmoid_gate
    hidden = (activated * up_pre).astype(jnp.bfloat16)
    out_rows = jnp.einsum(
        "erf,efd->erd", hidden, full_down, preferred_element_type=jnp.float32
    ).astype(jnp.bfloat16)
    d_hidden = jnp.einsum("erd,efd->erf", rows_cot, full_down, preferred_element_type=jnp.float32)
    d_gate = (d_hidden * up_pre * (sigmoid_gate + activated * (1.0 - sigmoid_gate))).astype(
        jnp.bfloat16
    )
    d_up = (d_hidden * activated).astype(jnp.bfloat16)
    dx_rows = jnp.einsum("erf,efd->erd", d_gate, full_gate, preferred_element_type=jnp.float32)
    dx_rows = (
        dx_rows + jnp.einsum("erf,efd->erd", d_up, full_up, preferred_element_type=jnp.float32)
    ).astype(jnp.bfloat16)
    part_down = jnp.einsum("erf,erd->efd", hidden, rows_cot, preferred_element_type=jnp.float32)
    part_gate = jnp.einsum("erf,erd->efd", d_gate, rows_in, preferred_element_type=jnp.float32)
    part_up = jnp.einsum("erf,erd->efd", d_up, rows_in, preferred_element_type=jnp.float32)

    back = jnp.stack([out_rows, dx_rows], axis=1)
    back = back.reshape(local_experts, 2, n_in, 2 * slots, width).transpose(2, 0, 1, 3, 4)
    back = back.reshape(half_experts, 2, 2 * slots, width)
    back = lax.all_to_all(back, "inner", split_axis=0, concat_axis=0, tiled=True)

    parts = jnp.concatenate([part_gate, part_up, part_down], axis=0)
    summed = parts[:, :hidden_part]
    for d in range(1, n_dp):
        block = parts[:, d * hidden_part : (d + 1) * hidden_part].astype(jnp.bfloat16)
        summed = summed + shifted(block, "dp", n_dp, -d).astype(jnp.float32)
    summed = summed.astype(jnp.bfloat16)
    grad_gate_w = summed[:local_experts]
    grad_up_w = summed[local_experts : 2 * local_experts]
    grad_down_w = summed[2 * local_experts :]

    out_part = back[:, 0].reshape(2 * half_rows, width)
    dx_part = back[:, 1].reshape(2 * half_rows, width)
    hit = dest[:, :, None] == jnp.arange(2 * half_rows, dtype=jnp.int32)[None, None, :]
    weight = jnp.sum(jnp.where(hit, all_gates[:, :, None], 0.0), axis=1)
    ones = jnp.sum(hit.astype(jnp.float32), axis=1).astype(jnp.bfloat16)
    layer = jnp.dot(in_three(weight), out_part, preferred_element_type=jnp.float32)
    n_all = 2 * tok_rows
    layer = layer[:n_all] + layer[n_all : 2 * n_all] + layer[2 * n_all :]
    grads = jnp.dot(ones, dx_part, preferred_element_type=jnp.float32)
    scores = jnp.dot(all_rows[:, width:], out_part.T, preferred_element_type=jnp.float32)
    gg = jnp.sum(jnp.where(hit, scores[:, None, :], 0.0), axis=2)

    returned = shifted(
        jnp.concatenate([layer[tok_rows:], grads[tok_rows:]], axis=1).astype(jnp.bfloat16),
        "half",
        2,
        1,
    )
    returned_gg = shifted(gg[tok_rows:], "half", 2, 1)
    layer_out = (layer[:tok_rows] + returned[:, :width].astype(jnp.float32)).astype(jnp.bfloat16)
    grad_tokens = (grads[:tok_rows] + returned[:, width:].astype(jnp.float32)).astype(jnp.bfloat16)
    grad_gates = gg[:tok_rows] + returned_gg
    return (layer_out, grad_tokens, grad_gates, grad_gate_w, grad_up_w, grad_down_w)


def solution(mesh):
    n_expert = mesh.shape["expert"]
    n_dp = mesh.shape["dp"]
    devices = np.asarray(mesh.devices).reshape(2, n_expert // 2, n_dp)
    split = Mesh(devices, ("half", "inner", "dp"))
    rows = P(("half", "inner", "dp"), None)
    weights = P(("half", "inner"), "dp", None)
    return jax.shard_map(
        on_device,
        mesh=split,
        in_specs=(rows, rows, rows, rows, P(), weights, weights, weights),
        out_specs=(rows, rows, rows, weights, weights, weights),
        check_vma=False,
    )
```

time: 468 us -> 411 us (0.88)
  blocking collectives: 34.4 us -> 89.7 us
  local copies, waits for them, and re-layouts: 103 us -> 71 us
  waiting for transfers between devices: 182 us -> 150 us
  other arithmetic: 52.5 us -> 25.7 us
  starting transfers between devices: 39.9 us -> 22.5 us
  matrix products: 49.8 us -> 42.9 us
    psum x0 -> x1, blocking collectives: none -> 89.7 us  [on_device(): all_counts = lax.psum(count_rows, ('half', 'inner'))]
    all_gather x1 -> x0, blocking collectives: 34.4 us -> none  [on_device(): all_counts = lax.all_gather(counts, ('half', 'inner'))]
    all_to_all x1, waiting for transfers between devices: 32.4 us -> 0.01 us  [on_device(): got = lax.all_to_all(send, 'inner', split_axis=0, concat_axis=0, tiled=True)]
    concatenate x3 -> x2, local copies, waits for them, and re-layouts: 28.6 us -> 0.14 us  [on_device(): all_gates = jnp.concatenate([gate_vals, partner_gates], axis=0)]
    scatter x1 -> x0, other arithmetic: 24.8 us -> none  [on_device(): jnp.zeros((2 * half_rows, 2 * width), jnp.bfloat16).at[dest]]
    mul x4 -> x0, local copies, waits for them, and re-layouts: 24.3 us -> none  [the longest x3 24.2 us: on_device(): all_gates[:, :, :, None] * all_rows[:, :, None, width:].astype(jnp.float32)]
    ppermute x7, starting transfers between devices: 29.5 us -> 12.5 us  [shifted(): lax.ppermute(value, axis, [(j, (j + shift) % count) for j in range(count)])]
    transpose x0 -> x1, local copies, waits for them, and re-layouts: none -> 13.7 us  [on_device(): got.transpose(1, 2, 0, 3, 4, 5)]
  transfers between devices with their start and end apart: 9 -> 9, of which waited for: 5 -> 3; matrix products, arithmetic and copies ran while one was open for 14% -> 23% of each run, Pallas kernels for 0% -> 0%
where the time goes in v2:
time: 411 us; the launch traced here: 403 us
  waiting for transfers between devices  150 us (36%)
  blocking collectives  89.7 us (22%)
  local copies, waits for them, and re-layouts  71 us (17%)
  matrix products  42.9 us (10%)
  other arithmetic  25.7 us (6%)
  starting transfers between devices  22.5 us (5%)
    psum x1, blocking collectives, on_device(): all_counts = lax.psum(count_rows, ('half', 'inner'))  89.7 us
    ppermute x7, waiting for transfers between devices, shifted(): lax.ppermute(value, axis, [(j, (j + shift) % count) for j in range(count)])  79 us
    all_to_all x1, waiting for transfers between devices, on_device(): lax.all_to_all(back, 'inner', split_axis=0, concat_axis=0, tiled=True)  71.1 us
    transpose x1, local copies, waits for them, and re-layouts, on_device(): got.transpose(1, 2, 0, 3, 4, 5)  13.7 us
    unnamed x49, local copies, waits for them, and re-layouts  12.7 us
    ppermute x7, starting transfers between devices, shifted(): lax.ppermute(value, axis, [(j, (j + shift) % count) for j in range(count)])  12.5 us
    slice x1, local copies, waits for them, and re-layouts, on_device(): rows_in = got[:, 0]  12.5 us
  transfers between devices with their start and end apart: 9, of which 3 were waited for; matrix products, arithmetic and copies ran while one was open for 23% of the time, Pallas kernels for 0%

profile of v2, /device:TPU:0, one launch (start us, length us, event | category | flops | bytes accessed | tf_op | source)
XLA Modules:
  0.0 403.4 jit_solution(16201613550079711618)
XLA Ops:
  2.8 4.1 %collective-permute-start.2 = (bf16[128,4096]{1,0:T(8,128)(2,1)S(1)}, bf16[128,4096]{1,0:T(8,128)(2,1)S(1)}, u32[]{:S(2)}, u32[]{:S(2)}) collective-permute-start(bf16[128,4096]{1,0:T(8,128)(2,1)S(1)} %constant_dynamic-update-slice_fusion.2), channel_id=1, source_target_pairs={{0,16},{16,0},{1,17},{17,1},{2,18},{18,2},{3,19},{19,3},{4,20},{20... | collective-permute-start | bytes 3145736 | tf_op jit(solution)/shard_map/ppermute | solution.py:10
  11.1 2.9 collective-permute-start.1
  15.1 37.8 %collective-permute-done = s32[128,6]{0,1:T(8,128)S(1)} collective-permute-done((s32[128,6]{0,1:T(8,128)S(1)}, s32[128,6]{0,1:T(8,128)S(1)}, u32[]{:S(2)}, u32[]{:S(2)}) %collective-permute-start) | collective-permute-done | bytes 3104 | tf_op jit(solution)/shard_map/ppermute | solution.py:10
  54.2 6.2 %scatter_custom_fusion = s32[960]{0:T(1024)S(1)} fusion(s32[1536]{0:T(1024)S(1)} %fusion.56, s32[1536]{0:T(1024)S(1)} %reshape.471, s32[]{:T(128)} %constant.22.clone.1), kind=kCustom, calls=%fused_computation.119 | custom fusion | bytes 3844 | tf_op jit(solution)/shard_map/scatter | solution.py:62
  60.4 6.2 %scatter_custom_fusion.1 = f32[960]{0:T(1024)S(1)} fusion(s32[1536]{0:T(1024)S(1)} %fusion.56, f32[1536]{0:T(1024)S(1)} %reshape.479, f32[]{:T(128)} %constant.33.clone.1), kind=kCustom, calls=%fused_computation.117 | custom fusion | bytes 3844 | tf_op jit(solution)/shard_map/scatter | solution.py:65
  66.6 2.2 fusion.23
  69.9 3.8 pad_maximum_fusion.1
  73.8 5.0 %all-to-all-start = ((bf16[8,2,120,2048]{3,2,1,0:T(8,128)(2,1)}), bf16[8,2,120,2048]{3,2,1,0:T(8,128)(2,1)}, u32[]{:S(2)}, u32[]{:S(2)}) async-start(bf16[8,2,120,2048]{3,2,1,0:T(8,128)(2,1)} %pad_maximum_fusion.1), calls=%async_computation | async-start | bytes 15728640 | tf_op jit(solution)/shard_map/all_to_all | solution.py:78
  83.6 89.7 %psum.7 = s32[16,16]{1,0:T(8,128)S(1)} all-reduce(s32[16,16]{1,0:T(8,128)S(1)} %broadcast_select_fusion), channel_id=1, replica_groups=mesh['half'=2,'inner'=8,'dp'=2] {'half','inner'}, use_global_device_ids=true, to_apply=%region_4.5 | all-reduce | flops 256 | bytes 2048 | tf_op jit(solution)/shard_map/psum | solution.py:49
  175.5 7.6 %copy.96 = bf16[8,2,120,2048]{3,0,2,1:T(8,128)(2,1)S(1)} copy(bf16[8,2,120,2048]{3,2,1,0:T(8,128)(2,1)} %all-to-all-done) | data formatting | bytes 15728640 | tf_op jit(solution)/shard_map/all_to_all | solution.py:78
  183.1 3.7 select_bitcast_fusion
  186.8 13.7 %copy.97 = bf16[1,2,8,2,60,2048]{5,1,4,3,2,0:T(2,128)(2,1)S(1)} copy(bf16[1,2,8,2,60,2048]{5,2,4,3,1,0:T(8,128)(2,1)} %select_bitcast_fusion) | data formatting | bytes 15728640 | tf_op jit(solution)/shard_map/transpose | solution.py:90
  200.5 12.5 %fusion.74 = (bf16[1,1,960,2048]{3,1,2,0:T(2,128)(2,1)S(1)}, bf16[1,1,960,2048]{3,1,2,0:T(2,128)(2,1)}) fusion(bf16[1,2,960,2048]{3,1,2,0:T(2,128)(2,1)S(1)} %bitcast.96), kind=kLoop, calls=%fused_computation.131 | loop fusion | bytes 15728640 | tf_op jit(solution)/shard_map/slice | solution.py:91
  213.0 2.6 copy.100
  216.2 4.5 %fusion.4 = f32[960,384]{1,0:T(8,128)S(1)} fusion(bf16[1,1,960,2048]{3,1,2,0:T(2,128)(2,1)S(1)} %copy-done.3, bf16[3,192,2048]{2,1,0:T(8,128)(2,1)} %collective-permute-done.3, bf16[3,192,2048]{2,1,0:T(8,128)(2,1)} %constant_dynamic-update-slice_fusion.4), kind=kOutput, calls=%fused_computation.24 | convolution fusion | flops 1513095168 | bytes 10125312 | tf_op jit(solution)/shard_map/erd,efd->erf/dot_general | solution.py:107
  220.8 3.6 fusion.12
  224.4 4.0 multiply_convert_fusion.2
  228.4 6.1 %convolution_convert_fusion = bf16[960,2048]{1,0:T(8,128)(2,1)} fusion(bf16[960,384]{1,0:T(8,128)(2,1)S(1)} %get-tuple-element.37, bf16[3,192,2048]{2,1,0:T(8,128)(2,1)} %collective-permute-done.3, bf16[3,192,2048]{2,1,0:T(8,128)(2,1)} %constant_dynamic-update-slice_fusion.4), kind=kOutput, calls=%fused_computation.34 | convolution fusion | flops 1515061248 | bytes 9388032 | tf_op jit(solution)/shard_map/erf,efd->erd/dot_general | solution.py:104
  234.5 3.6 fusion.70
  238.1 3.8 add_convert_fusion
  241.9 5.9 %maximum_bitcast_fusion = bf16[8,2,120,2048]{3,2,1,0:T(8,128)(2,1)} fusion(bf16[1,1,8,120,2048]{4,3,1,2,0:T(8,128)(2,1)S(1)} %bitcast.102, bf16[1,1,8,120,2048]{4,3,1,2,0:T(8,128)(2,1)} %bitcast.108), kind=kLoop, calls=%fused_computation.8 | loop fusion | flops 3932160 | bytes 15728640 | tf_op jit(solution)/shard_map/reshape | solution.py:122
  247.8 4.9 %all-to-all-start.1 = ((bf16[8,2,120,2048]{3,2,1,0:T(8,128)(2,1)}), bf16[8,2,120,2048]{3,2,1,0:T(8,128)(2,1)}, u32[]{:S(2)}, u32[]{:S(2)}) async-start(bf16[8,2,120,2048]{3,2,1,0:T(8,128)(2,1)} %maximum_bitcast_fusion), calls=%async_computation.1 | async-start | bytes 15728640 | tf_op jit(solution)/shard_map/all_to_all | solution.py:123
  252.7 4.1 %fusion.14 = f32[1,384,2048]{2,1,0:T(8,128)S(1)} fusion(bf16[960,384]{1,0:T(8,128)(2,1)S(1)} %get-tuple-element.38, bf16[1,1,960,2048]{3,2,1,0:T(8,128)(2,1)} %copy-done), kind=kOutput, calls=%fused_computation.35 | convolution fusion | flops 1509949440 | bytes 7815168 | tf_op jit(solution)/shard_map/erf,erd->efd/dot_general | solution.py:117
  256.9 1.8 fusion.17
  259.2 3.1 fusion.20
  263.5 3.7 copy-done.2
  269.1 71.1 %all-to-all-done.1 = bf16[8,2,120,2048]{3,2,1,0:T(8,128)(2,1)} async-done(((bf16[8,2,120,2048]{3,2,1,0:T(8,128)(2,1)}), bf16[8,2,120,2048]{3,2,1,0:T(8,128)(2,1)}, u32[]{:S(2)}, u32[]{:S(2)}) %all-to-all-start.1) | async-done | bytes 7864352 | tf_op jit(solution)/shard_map/all_to_all | solution.py:123
  340.2 3.9 fusion.73
  345.4 1.9 select_reduce_fusion
  347.5 3.5 fusion.34
  354.8 2.6 fusion.1
  360.1 41.2 %collective-permute-done.5 = f32[128,6]{0,1:T(8,128)S(1)} collective-permute-done((f32[128,6]{0,1:T(8,128)S(1)}, f32[128,6]{0,1:T(8,128)S(1)}, u32[]{:S(2)}, u32[]{:S(2)}) %collective-permute-start.5) | collective-permute-done | bytes 3104 | tf_op jit(solution)/shard_map/ppermute | solution.py:10
  (118 shorter events, 30.7 us)
Async XLA Ops:
  2.8 66.0 %copy-start.6 = (bf16[128,4096]{1,0:T(8,128)(2,1)}, bf16[128,4096]{1,0:T(8,128)(2,1)S(1)}, u32[]{:S(2)}) copy-start(bf16[128,4096]{1,0:T(8,128)(2,1)S(1)} %constant_dynamic-update-slice_fusion.2) | copy-start | bytes 3145732
  2.8 63.7 %collective-permute-start.2 = (bf16[128,4096]{1,0:T(8,128)(2,1)S(1)}, bf16[128,4096]{1,0:T(8,128)(2,1)S(1)}, u32[]{:S(2)}, u32[]{:S(2)}) collective-permute-start(bf16[128,4096]{1,0:T(8,128)(2,1)S(1)} %constant_dynamic-update-slice_fusion.2), channel_id=1, source_target_pairs={{0,16},{16,0},{1,17},{17,1},{2,18},{18,2},{3,19},{19,3},{4,20},{20... | collective-permute-start | bytes 3145736 | tf_op jit(solution)/shard_map/ppermute | solution.py:10
  11.0 41.8 %collective-permute-start = (s32[128,6]{0,1:T(8,128)S(1)}, s32[128,6]{0,1:T(8,128)S(1)}, u32[]{:S(2)}, u32[]{:S(2)}) collective-permute-start(s32[128,6]{0,1:T(8,128)S(1)} %multiply_add_fusion), channel_id=1, source_target_pairs={{0,16},{16,0},{1,17},{17,1},{2,18},{18,2},{3,19},{19,3},{4,20},{20... | collective-permute-start | bytes 9224 | tf_op jit(solution)/shard_map/ppermute | solution.py:10
  11.1 42.7 %collective-permute-start.1 = (f32[128,6]{0,1:T(8,128)}, f32[128,6]{0,1:T(8,128)S(1)}, u32[]{:S(2)}, u32[]{:S(2)}) collective-permute-start(f32[128,6]{0,1:T(8,128)} %param.11), channel_id=1, source_target_pairs={{0,16},{16,0},{1,17},{17,1},{2,18},{18,2},{3,19},{19,3},{4,20},{20... | collective-permute-start | bytes 9224 | tf_op jit(solution)/shard_map/ppermute | solution.py:10
  66.6 2.3 copy-start.8
  73.7 5.0 %copy-start.10 = (bf16[1,192,2048]{2,1,0:T(8,128)(2,1)S(1)}, bf16[1,192,2048]{2,1,0:T(8,128)(2,1)}, u32[]{:S(2)}) copy-start(bf16[1,192,2048]{2,1,0:T(8,128)(2,1)} %param.13) | copy-start | bytes 2359300
  73.8 6.0 %copy-start.11 = (bf16[1,192,2048]{2,1,0:T(8,128)(2,1)S(1)}, bf16[1,192,2048]{2,1,0:T(8,128)(2,1)}, u32[]{:S(2)}) copy-start(bf16[1,192,2048]{2,1,0:T(8,128)(2,1)} %param.14) | copy-start | bytes 2359300
  73.8 101.8 %all-to-all-start = ((bf16[8,2,120,2048]{3,2,1,0:T(8,128)(2,1)}), bf16[8,2,120,2048]{3,2,1,0:T(8,128)(2,1)}, u32[]{:S(2)}, u32[]{:S(2)}) async-start(bf16[8,2,120,2048]{3,2,1,0:T(8,128)(2,1)} %pad_maximum_fusion.1), calls=%async_computation | async-start | bytes 15728640 | tf_op jit(solution)/shard_map/all_to_all | solution.py:78
  78.8 1.9 copy-start.12
  78.8 95.4 %copy-start.15 = (s32[16]{0:T(128)S(1)}, s32[16]{0:T(128)}, u32[]{:S(2)}) copy-start(s32[16]{0:T(128)} %param.12) | copy-start | bytes 196
  81.7 133.9 %collective-permute-start.3 = (bf16[3,192,2048]{2,1,0:T(8,128)(2,1)}, bf16[3,192,2048]{2,1,0:T(8,128)(2,1)}, u32[]{:S(2)}, u32[]{:S(2)}) collective-permute-start(bf16[3,192,2048]{2,1,0:T(8,128)(2,1)} %constant_dynamic-update-slice_fusion.4), channel_id=1, source_target_pairs={{0,1},{1,0},{2,3},{3,2},{4,5},{5,4},{6,7},{7,6},{8,9},{9,8},{10,11... | collective-permute-start | bytes 7077896 | tf_op jit(solution)/shard_map/ppermute | solution.py:10
  213.0 3.2 copy-start.3
  215.6 8.8 %copy-start = (bf16[1,1,960,2048]{3,2,1,0:T(8,128)(2,1)}, bf16[1,1,960,2048]{3,2,1,0:T(8,128)(2,1)S(1)}, u32[]{:S(2)}) copy-start(bf16[1,1,960,2048]{3,2,1,0:T(8,128)(2,1)S(1)} %copy.100) | copy-start | bytes 11796484
  228.4 6.1 %copy-start.13 = (bf16[960,384]{1,0:T(8,128)(2,1)}, bf16[960,384]{1,0:T(8,128)(2,1)S(1)}, u32[]{:S(2)}) copy-start(bf16[960,384]{1,0:T(8,128)(2,1)S(1)} %get-tuple-element.37) | copy-start | bytes 2211844
  228.4 6.1 %copy-start.4 = (bf16[960,384]{1,0:T(8,128)(2,1)}, bf16[960,384]{1,0:T(8,128)(2,1)S(1)}, u32[]{:S(2)}) copy-start(bf16[960,384]{1,0:T(8,128)(2,1)S(1)} %get-tuple-element.39) | copy-start | bytes 2211844
  247.8 92.4 %all-to-all-start.1 = ((bf16[8,2,120,2048]{3,2,1,0:T(8,128)(2,1)}), bf16[8,2,120,2048]{3,2,1,0:T(8,128)(2,1)}, u32[]{:S(2)}, u32[]{:S(2)}) async-start(bf16[8,2,120,2048]{3,2,1,0:T(8,128)(2,1)} %maximum_bitcast_fusion), calls=%async_computation.1 | async-start | bytes 15728640 | tf_op jit(solution)/shard_map/all_to_all | solution.py:123
  252.7 4.1 %copy-start.1 = (bf16[1,1,960,2048]{3,2,1,0:T(8,128)(2,1)S(1)}, bf16[1,1,960,2048]{3,2,1,0:T(8,128)(2,1)}, u32[]{:S(2)}) copy-start(bf16[1,1,960,2048]{3,2,1,0:T(8,128)(2,1)} %copy-done) | copy-start | bytes 11796484
  252.7 4.1 %copy-start.5 = (bf16[960,384]{1,0:T(8,128)(2,1)S(1)}, bf16[960,384]{1,0:T(8,128)(2,1)}, u32[]{:S(2)}) copy-start(bf16[960,384]{1,0:T(8,128)(2,1)} %copy-done.4) | copy-start | bytes 2211844
  252.7 6.0 %slice-start.3 = ((s8[7864320]{0:T(1024)(128)(4,1)}), s8[4194304]{0:T(1024)(128)(4,1)S(1)}, s32[]{:S(2)}) async-start(s8[7864320]{0:T(1024)(128)(4,1)} %bitcast.100), calls=%async_computation.5 | async-start | bytes 8388608
  256.9 2.2 slice-start.4
  256.9 2.3 copy-start.14
  263.5 3.7 copy-start.2
  267.5 76.6 %copy-start.7 = (bf16[128,4096]{1,0:T(8,128)(2,1)S(1)}, bf16[128,4096]{1,0:T(8,128)(2,1)}, u32[]{:S(2)}) copy-start(bf16[128,4096]{1,0:T(8,128)(2,1)} %copy-done.6) | copy-start | bytes 3145732
  267.5 86.5 %collective-permute-start.6 = (bf16[3,192,2048]{2,1,0:T(8,128)(2,1)S(1)}, bf16[3,192,2048]{2,1,0:T(8,128)(2,1)}, u32[]{:S(2)}, u32[]{:S(2)}) collective-permute-start(bf16[3,192,2048]{2,1,0:T(8,128)(2,1)S(1)} %slice.215), channel_id=1, source_target_pairs={{0,1},{1,0},{2,3},{3,2},{4,5},{5,4},{6,7},{7,6},{8,9},{9,8},{10,11... | collective-permute-start | bytes 7077896 | tf_op jit(solution)/shard_map/ppermute | solution.py:10
  340.2 3.9 copy-start.9
  350.9 3.1 slice-start
  351.0 3.5 slice-start.1
  351.6 3.2 slice-start.2
  353.0 48.9 %collective-permute-start.4 = (bf16[128,4096]{1,0:T(8,128)(2,1)S(1)}, bf16[128,4096]{1,0:T(8,128)(2,1)S(1)}, u32[]{:S(2)}, u32[]{:S(2)}) collective-permute-start(bf16[128,4096]{1,0:T(8,128)(2,1)S(1)} %pad_maximum_fusion.3), channel_id=1, source_target_pairs={{0,16},{16,0},{1,17},{17,1},{2,18},{18,2},{3,19},{19,3},{4,20},{20... | collective-permute-start | bytes 3145736 | tf_op jit(solution)/shard_map/ppermute | solution.py:10
  357.4 43.9 %collective-permute-start.5 = (f32[128,6]{0,1:T(8,128)S(1)}, f32[128,6]{0,1:T(8,128)S(1)}, u32[]{:S(2)}, u32[]{:S(2)}) collective-permute-start(f32[128,6]{0,1:T(8,128)S(1)} %slice.158), channel_id=1, source_target_pairs={{0,16},{16,0},{1,17},{17,1},{2,18},{18,2},{3,19},{19,3},{4,20},{20... | collective-permute-start | bytes 9224 | tf_op jit(solution)/shard_map/ppermute | solution.py:10

commit v3 on v2

--- a/solution.py
+++ b/solution.py
@@ -46,7 +46,7 @@
     local_rank = jnp.sum(running * one_hot, axis=1) - 1
     counts = running[-1]
     count_rows = jnp.where(jnp.arange(n_src, dtype=jnp.int32)[:, None] == source, counts[None, :], 0)
-    all_counts = lax.psum(count_rows, ("half", "inner"))
+    all_counts = lax.psum(count_rows.astype(jnp.float32), ("half", "inner")).astype(jnp.int32)
     code = (flat_ids * slots + local_rank).reshape(tok_rows, top_count)
     partner_code = shifted(code, "half", 2, 1)
 
@@ -71,12 +71,9 @@
     picked = jnp.dot(pick, all_rows, preferred_element_type=jnp.float32)
     send_x = picked[:, :width].astype(jnp.bfloat16)
     send_c = (slot_gate[:, None] * picked[:, width:]).astype(jnp.bfloat16)
-    send = jnp.stack(
-        [send_x.reshape(half_experts, 2 * slots, width), send_c.reshape(half_experts, 2 * slots, width)],
-        axis=1,
-    )
+    send = jnp.concatenate([send_x, send_c], axis=1).reshape(half_experts, 2 * slots, 2 * width)
     got = lax.all_to_all(send, "inner", split_axis=0, concat_axis=0, tiled=True)
-    got = got.reshape(n_in, local_experts, 2, 2, slots, width)
+    got = got.reshape(n_in, local_experts, 2, slots, 2 * width)
 
     earlier = jnp.cumsum(all_counts, axis=0) - all_counts
     holders = jnp.arange(n_in, dtype=jnp.int32)[:, None]
@@ -86,10 +83,10 @@
     before = earlier[sources][:, :, mine].transpose(0, 2, 1)
     ranks = jnp.arange(slots, dtype=jnp.int32)
     keep = before[..., None] + ranks < capacity[mine][None, :, None, None]
-    got = jnp.where(keep[:, :, None, :, :, None], got, jnp.zeros((), got.dtype))
-    got = got.transpose(1, 2, 0, 3, 4, 5).reshape(local_experts, 2, n_in * 2 * slots, width)
-    rows_in = got[:, 0]
-    rows_cot = got[:, 1]
+    got = jnp.where(keep[..., None], got, jnp.zeros((), got.dtype))
+    got = got.transpose(1, 0, 2, 3, 4).reshape(local_experts, n_in * 2 * slots, 2 * width)
+    rows_in = got[:, :, :width]
+    rows_cot = got[:, :, width:]
 
     full = jnp.concatenate(pieces, axis=1)
     full_gate = full[:local_experts]
@@ -117,10 +114,13 @@
     part_gate = jnp.einsum("erf,erd->efd", d_gate, rows_in, preferred_element_type=jnp.float32)
     part_up = jnp.einsum("erf,erd->efd", d_up, rows_in, preferred_element_type=jnp.float32)
 
-    back = jnp.stack([out_rows, dx_rows], axis=1)
-    back = back.reshape(local_experts, 2, n_in, 2 * slots, width).transpose(2, 0, 1, 3, 4)
-    back = back.reshape(half_experts, 2, 2 * slots, width)
-    back = lax.all_to_all(back, "inner", split_axis=0, concat_axis=0, tiled=True)
+    out_rows = out_rows.reshape(local_experts, n_in, 2, slots, width)
+    dx_rows = dx_rows.reshape(local_experts, n_in, 2, slots, width)
+
+    def returning(which):
+        back = jnp.stack([out_rows[:, :, which], dx_rows[:, :, which]], axis=2)
+        back = back.transpose(1, 0, 2, 3, 4).reshape(half_experts, 2, slots, width)
+        return lax.all_to_all(back, "inner", split_axis=0, concat_axis=0, tiled=True)
 
     parts = jnp.concatenate([part_gate, part_up, part_down], axis=0)
     summed = parts[:, :hidden_part]
@@ -132,28 +132,33 @@
     grad_up_w = summed[local_experts : 2 * local_experts]
     grad_down_w = summed[2 * local_experts :]
 
-    out_part = back[:, 0].reshape(2 * half_rows, width)
-    dx_part = back[:, 1].reshape(2 * half_rows, width)
-    hit = dest[:, :, None] == jnp.arange(2 * half_rows, dtype=jnp.int32)[None, None, :]
-    weight = jnp.sum(jnp.where(hit, all_gates[:, :, None], 0.0), axis=1)
-    ones = jnp.sum(hit.astype(jnp.float32), axis=1).astype(jnp.bfloat16)
-    layer = jnp.dot(in_three(weight), out_part, preferred_element_type=jnp.float32)
-    n_all = 2 * tok_rows
-    layer = layer[:n_all] + layer[n_all : 2 * n_all] + layer[2 * n_all :]
-    grads = jnp.dot(ones, dx_part, preferred_element_type=jnp.float32)
-    scores = jnp.dot(all_rows[:, width:], out_part.T, preferred_element_type=jnp.float32)
-    gg = jnp.sum(jnp.where(hit, scores[:, None, :], 0.0), axis=2)
+    place = jnp.where(inside, local * slots + all_code % slots, half_rows)
+    columns = jnp.arange(half_rows, dtype=jnp.int32)
 
+    def combine(which):
+        back = returning(which)
+        out_part = back[:, 0].reshape(half_rows, width)
+        dx_part = back[:, 1].reshape(half_rows, width)
+        rows = slice(which * tok_rows, (which + 1) * tok_rows)
+        hit = place[rows][:, :, None] == columns[None, None, :]
+        weight = jnp.sum(jnp.where(hit, all_gates[rows][:, :, None], 0.0), axis=1)
+        ones = jnp.sum(hit.astype(jnp.float32), axis=1).astype(jnp.bfloat16)
+        layer = jnp.dot(in_three(weight), out_part, preferred_element_type=jnp.float32)
+        layer = layer[:tok_rows] + layer[tok_rows : 2 * tok_rows] + layer[2 * tok_rows :]
+        grads = jnp.dot(ones, dx_part, preferred_element_type=jnp.float32)
+        scores = jnp.dot(all_rows[rows, width:], out_part.T, preferred_element_type=jnp.float32)
+        gg = jnp.sum(jnp.where(hit, scores[:, None, :], 0.0), axis=2)
+        return layer, grads, gg
+
+    partner_layer, partner_grads, partner_gg = combine(1)
     returned = shifted(
-        jnp.concatenate([layer[tok_rows:], grads[tok_rows:]], axis=1).astype(jnp.bfloat16),
-        "half",
-        2,
-        1,
+        jnp.concatenate([partner_layer, partner_grads], axis=1).astype(jnp.bfloat16), "half", 2, 1
     )
-    returned_gg = shifted(gg[tok_rows:], "half", 2, 1)
-    layer_out = (layer[:tok_rows] + returned[:, :width].astype(jnp.float32)).astype(jnp.bfloat16)
-    grad_tokens = (grads[:tok_rows] + returned[:, width:].astype(jnp.float32)).astype(jnp.bfloat16)
-    grad_gates = gg[:tok_rows] + returned_gg
+    returned_gg = shifted(partner_gg, "half", 2, 1)
+    own_layer, own_grads, own_gg = combine(0)
+    layer_out = (own_layer + returned[:, :width].astype(jnp.float32)).astype(jnp.bfloat16)
+    grad_tokens = (own_grads + returned[:, width:].astype(jnp.float32)).astype(jnp.bfloat16)
+    grad_gates = own_gg + returned_gg
     return (layer_out, grad_tokens, grad_gates, grad_gate_w, grad_up_w, grad_down_w)
 
 

time: 411 us -> 495 us (1.20)
  local copies, waits for them, and re-layouts: 71 us -> 103 us
  blocking collectives: 89.7 us -> 110 us
  waiting for transfers between devices: 150 us -> 167 us
  matrix products: 42.9 us -> 50.3 us
  starting transfers between devices: 22.5 us -> 27.7 us
    ppermute x7, waiting for transfers between devices: 79 us -> 129 us  [shifted(): lax.ppermute(value, axis, [(j, (j + shift) % count) for j in range(count)])]
    all_to_all x1 -> x2, waiting for transfers between devices: 71.1 us -> 37.3 us  [returning(): lax.all_to_all(back, 'inner', split_axis=0, concat_axis=0, tiled=True)]
    slice x6 -> x5, local copies, waits for them, and re-layouts: 16.8 us -> 46.4 us  [the longest x1 20.8 us: combine(): dx_part = back[:, 1].reshape(half_rows, width)]
    another operation x0 -> x6, local copies, waits for them, and re-layouts: none -> 21.2 us  [the longest x2 12.1 us: returning(): back = back.transpose(1, 0, 2, 3, 4).reshape(half_experts, 2, slots, width)]
    psum x1, blocking collectives: 89.7 us -> 110 us  [on_device(): lax.psum(count_rows.astype(jnp.float32), ('half', 'inner'))]
    transpose x1 -> x0, local copies, waits for them, and re-layouts: 13.7 us -> none  [on_device(): got.transpose(1, 2, 0, 3, 4, 5)]
    reshape x0 -> x2, local copies, waits for them, and re-layouts: none -> 9.95 us  [the longest x1 5.04 us: on_device(): dx_rows = dx_rows.reshape(local_experts, n_in, 2, slots, width)]
    unnamed x49 -> x39, local copies, waits for them, and re-layouts: 12.7 us -> 3.4 us
  transfers between devices with their start and end apart: 9 -> 10, of which waited for: 3 -> 4; matrix products, arithmetic and copies ran while one was open for 23% -> 23% of each run, Pallas kernels for 0% -> 0%
where the time goes in v3:
time: 495 us; the launch traced here: 488 us
  waiting for transfers between devices  167 us (34%)
  blocking collectives  110 us (22%)
  local copies, waits for them, and re-layouts  103 us (21%)
  matrix products  50.3 us (10%)
  other arithmetic  29.1 us (6%)
  starting transfers between devices  27.7 us (6%)
    ppermute x7, waiting for transfers between devices, shifted(): lax.ppermute(value, axis, [(j, (j + shift) % count) for j in range(count)])  129 us
    psum x1, blocking collectives, on_device(): lax.psum(count_rows.astype(jnp.float32), ('half', 'inner'))  110 us
    all_to_all x2, waiting for transfers between devices, returning(): lax.all_to_all(back, 'inner', split_axis=0, concat_axis=0, tiled=True)  37.3 us
    slice x1, local copies, waits for them, and re-layouts, combine(): dx_part = back[:, 1].reshape(half_rows, width)  20.8 us
    slice x1, local copies, waits for them, and re-layouts, combine(): out_part = back[:, 0].reshape(half_rows, width)  20.6 us
    ppermute x7, starting transfers between devices, shifted(): lax.ppermute(value, axis, [(j, (j + shift) % count) for j in range(count)])  13.3 us
    another operation x2, local copies, waits for them, and re-layouts, returning(): back = back.transpose(1, 0, 2, 3, 4).reshape(half_experts, 2, slots, width)  12.1 us
  transfers between devices with their start and end apart: 10, of which 4 were waited for; matrix products, arithmetic and copies ran while one was open for 23% of the time, Pallas kernels for 0%

profile of v3, /device:TPU:0, one launch (start us, length us, event | category | flops | bytes accessed | tf_op | source)
XLA Modules:
  0.0 487.9 jit_solution(17768026236895901356)
XLA Ops:
  2.8 4.1 collective-permute-start.1
  10.4 2.9 collective-permute-start.2
  13.7 39.1 %collective-permute-done = s32[128,6]{0,1:T(8,128)S(1)} collective-permute-done((s32[128,6]{0,1:T(8,128)S(1)}, s32[128,6]{0,1:T(8,128)S(1)}, u32[]{:S(2)}, u32[]{:S(2)}) %collective-permute-start) | collective-permute-done | bytes 3104 | tf_op jit(solution)/shard_map/ppermute | solution.py:10
  54.2 6.2 %scatter_custom_fusion = s32[960]{0:T(1024)S(1)} fusion(s32[1536]{0:T(1024)S(1)} %fusion.47, s32[1536]{0:T(1024)S(1)} %reshape.415, s32[]{:T(128)} %constant.25.clone.1), kind=kCustom, calls=%fused_computation.128 | custom fusion | bytes 3844 | tf_op jit(solution)/shard_map/scatter | solution.py:62
  60.4 6.2 %scatter_custom_fusion.1 = f32[960]{0:T(1024)S(1)} fusion(s32[1536]{0:T(1024)S(1)} %fusion.47, f32[1536]{0:T(1024)S(1)} %reshape.423, f32[]{:T(128)} %constant.34.clone.1), kind=kCustom, calls=%fused_computation.126 | custom fusion | bytes 3844 | tf_op jit(solution)/shard_map/scatter | solution.py:65
  73.9 7.4 %pad_maximum_fusion.1 = bf16[960,4096]{1,0:T(8,128)(2,1)} fusion(bf16[960,2048]{1,0:T(8,128)(2,1)} %fusion, bf16[960,2048]{1,0:T(8,128)(2,1)} %slice.256), kind=kLoop, calls=%fused_computation.7 | loop fusion | flops 15728640 | bytes 15728640 | tf_op jit(solution)/shard_map/concatenate | solution.py:74
  81.3 5.1 %all-to-all-start = ((bf16[8,120,4096]{2,1,0:T(8,128)(2,1)}), bf16[8,120,4096]{2,1,0:T(8,128)(2,1)}, u32[]{:S(2)}, u32[]{:S(2)}) async-start(bf16[8,120,4096]{2,1,0:T(8,128)(2,1)} %bitcast.83), calls=%async_computation | async-start | bytes 15728640 | tf_op jit(solution)/shard_map/all_to_all | solution.py:75
  89.8 109.9 %psum.7 = f32[16,16]{1,0:T(8,128)S(1)} all-reduce(f32[16,16]{1,0:T(8,128)S(1)} %select_convert_fusion), channel_id=1, replica_groups=mesh['half'=2,'inner'=8,'dp'=2] {'half','inner'}, use_global_device_ids=true, to_apply=%region_4.5 | all-reduce | flops 256 | bytes 2048 | tf_op jit(solution)/shard_map/psum | solution.py:49
  202.2 6.9 %bitcast_select_fusion = bf16[1,960,4096]{2,1,0:T(8,128)(2,1)} fusion(pred[960]{0:T(1024)(128)(4,1)S(1)} %lt.80, bf16[1,960,4096]{2,1,0:T(8,128)(2,1)} %bitcast.81), kind=kLoop, calls=%fused_computation.8 | loop fusion | flops 3932160 | bytes 15729600 | tf_op jit(solution)/shard_map/jit(_where)/select_n | solution.py:86
  209.1 4.7 fusion.3
  213.8 3.3 fusion.6
  217.2 4.7 multiply_convert_fusion.2
  221.8 3.6 fusion.61
  225.4 5.3 %add_convert_fusion = bf16[960,2048]{1,0:T(8,128)(2,1)} fusion(f32[960,2048]{1,0:T(8,128)S(1)} %fusion.61, bf16[960,384]{1,0:T(8,128)(2,1)S(1)} %get-tuple-element.45, bf16[3,192,2048]{2,1,0:T(8,128)(2,1)S(1)} %constant_dynamic-update-slice_fusion.2, bf16[3,192,2048]{2,1,0:T(8,128)(2,1)} %collective-permute-done.3), kind=kOutput, calls=%fused_computation.9 | convolution fusion | flops 1517027328 | bytes 17252352 | tf_op jit(solution)/shard_map/erf,efd->erd/dot_general | solution.py:109
  230.7 5.0 %reshape.356 = bf16[1,8,2,60,2048]{4,3,2,1,0:T(8,128)(2,1)} reshape(bf16[960,2048]{1,0:T(8,128)(2,1)} %add_convert_fusion) | data formatting | bytes 7864320 | tf_op jit(solution)/shard_map/reshape | solution.py:118
  235.8 5.4 %convolution_convert_fusion = bf16[960,2048]{1,0:T(8,128)(2,1)} fusion(bf16[960,384]{1,0:T(8,128)(2,1)} %get-tuple-element.44, bf16[3,192,2048]{2,1,0:T(8,128)(2,1)} %collective-permute-done.3, bf16[3,192,2048]{2,1,0:T(8,128)(2,1)S(1)} %constant_dynamic-update-slice_fusion.2), kind=kOutput, calls=%fused_computation.25 | convolution fusion | flops 1515061248 | bytes 9388032 | tf_op jit(solution)/shard_map/erf,efd->erd/dot_general | solution.py:101
  241.2 4.9 %reshape.354 = bf16[1,8,2,60,2048]{4,3,2,1,0:T(8,128)(2,1)} reshape(bf16[960,2048]{1,0:T(8,128)(2,1)} %convolution_convert_fusion) | data formatting | bytes 7864320 | tf_op jit(solution)/shard_map/reshape | solution.py:117
  246.1 4.8 fusion.64
  251.3 6.0 %copy.93 = bf16[8,2,60,2048]{3,1,2,0:T(2,128)(2,1)} copy(bf16[8,2,60,2048]{3,2,1,0:T(8,128)(2,1)S(1)} %maximum_bitcast_fusion.1) | data formatting | bytes 7864320 | tf_op jit(solution)/shard_map/reshape;transpose | solution.py:122
  257.3 4.5 all-to-all-start.2
  263.8 6.0 %copy.92 = bf16[8,2,60,2048]{3,1,2,0:T(2,128)(2,1)} copy(bf16[8,2,60,2048]{3,2,1,0:T(8,128)(2,1)S(1)} %maximum_bitcast_fusion) | data formatting | bytes 7864320 | tf_op jit(solution)/shard_map/reshape;transpose | solution.py:122
  269.8 37.3 %all-to-all-done.2 = bf16[8,2,60,2048]{3,1,2,0:T(2,128)(2,1)} async-done(((bf16[8,2,60,2048]{3,1,2,0:T(2,128)(2,1)}), bf16[8,2,60,2048]{3,1,2,0:T(2,128)(2,1)}, u32[]{:S(2)}, u32[]{:S(2)}) %all-to-all-start.2) | async-done | bytes 3932192 | tf_op jit(solution)/shard_map/all_to_all | solution.py:123
  307.2 4.7 all-to-all-start.1
  312.0 4.1 convolution_bitcast_fusion
  316.1 4.1 convolution_bitcast_fusion.1
  325.2 52.0 %collective-permute-done.6 = bf16[3,192,2048]{2,1,0:T(8,128)(2,1)S(1)} collective-permute-done((bf16[3,192,2048]{2,1,0:T(8,128)(2,1)S(1)}, bf16[3,192,2048]{2,1,0:T(8,128)(2,1)S(1)}, u32[]{:S(2)}, u32[]{:S(2)}) %collective-permute-start.6) | collective-permute-done | bytes 2359328 | tf_op jit(solution)/shard_map/ppermute | solution.py:10
  379.6 20.6 %slice_reduce_fusion.2 = (bf16[8,60,2048]{2,1,0:T(8,128)(2,1)}, bf16[8,60,2048]{2,1,0:T(8,128)(2,1)}) fusion(bf16[8,2,60,2048]{3,1,2,0:T(2,128)(2,1)} %all-to-all-done.2), kind=kLoop, calls=%fused_computation.21 | loop fusion | bytes 7864320 | tf_op jit(solution)/shard_map/slice | solution.py:140
  403.3 20.8 %slice_reduce_fusion = (bf16[8,60,2048]{2,1,0:T(8,128)(2,1)}, bf16[8,60,2048]{2,1,0:T(8,128)(2,1)}) fusion(bf16[8,2,60,2048]{3,1,2,0:T(2,128)(2,1)} %all-to-all-done.1), kind=kLoop, calls=%fused_computation.19 | loop fusion | bytes 7864320 | tf_op jit(solution)/shard_map/slice | solution.py:141
  428.6 2.7 reshape_squeeze.14
  434.6 2.9 collective-permute-start.4
  441.4 2.9 reshape_squeeze.15
  444.8 38.1 %collective-permute-done.4 = bf16[128,4096]{1,0:T(8,128)(2,1)} collective-permute-done((bf16[128,4096]{1,0:T(8,128)(2,1)}, bf16[128,4096]{1,0:T(8,128)(2,1)}, u32[]{:S(2)}, u32[]{:S(2)}) %collective-permute-start.4) | collective-permute-done | bytes 1048608 | tf_op jit(solution)/shard_map/ppermute | solution.py:10
  (123 shorter events, 49.7 us)
Async XLA Ops:
  0.6 9.7 %copy-start.12 = (s32[128,6]{0,1:T(8,128)S(1)}, s32[128,6]{0,1:T(8,128)}, u32[]{:S(2)}) copy-start(s32[128,6]{0,1:T(8,128)} %param.10) | copy-start | bytes 9220
  0.6 9.8 %copy-start.11 = (f32[128,6]{0,1:T(8,128)S(1)}, f32[128,6]{0,1:T(8,128)}, u32[]{:S(2)}) copy-start(f32[128,6]{0,1:T(8,128)} %param.11) | copy-start | bytes 9220
  2.8 63.7 %collective-permute-start.1 = (bf16[128,4096]{1,0:T(8,128)(2,1)S(1)}, bf16[128,4096]{1,0:T(8,128)(2,1)S(1)}, u32[]{:S(2)}, u32[]{:S(2)}) collective-permute-start(bf16[128,4096]{1,0:T(8,128)(2,1)S(1)} %constant_dynamic-update-slice_fusion), channel_id=1, source_target_pairs={{0,16},{16,0},{1,17},{17,1},{2,18},{18,2},{3,19},{19,3},{4,20},{20... | collective-permute-start | bytes 3145736 | tf_op jit(solution)/shard_map/ppermute | solution.py:10
  10.3 42.5 %collective-permute-start = (s32[128,6]{0,1:T(8,128)S(1)}, s32[128,6]{0,1:T(8,128)S(1)}, u32[]{:S(2)}, u32[]{:S(2)}) collective-permute-start(s32[128,6]{0,1:T(8,128)S(1)} %multiply_add_fusion), channel_id=1, source_target_pairs={{0,16},{16,0},{1,17},{17,1},{2,18},{18,2},{3,19},{19,3},{4,20},{20... | collective-permute-start | bytes 9224 | tf_op jit(solution)/shard_map/ppermute | solution.py:10
  10.4 43.4 %collective-permute-start.2 = (f32[128,6]{0,1:T(8,128)S(1)}, f32[128,6]{0,1:T(8,128)S(1)}, u32[]{:S(2)}, u32[]{:S(2)}) collective-permute-start(f32[128,6]{0,1:T(8,128)S(1)} %copy-done.11), channel_id=1, source_target_pairs={{0,16},{16,0},{1,17},{17,1},{2,18},{18,2},{3,19},{19,3},{4,20},{20... | collective-permute-start | bytes 9224 | tf_op jit(solution)/shard_map/ppermute | solution.py:10
  66.6 2.3 copy-start.4
  81.3 5.1 %copy-start.7 = (bf16[1,192,2048]{2,1,0:T(8,128)(2,1)S(1)}, bf16[1,192,2048]{2,1,0:T(8,128)(2,1)}, u32[]{:S(2)}) copy-start(bf16[1,192,2048]{2,1,0:T(8,128)(2,1)} %param.13) | copy-start | bytes 2359300
  81.3 120.9 %all-to-all-start = ((bf16[8,120,4096]{2,1,0:T(8,128)(2,1)}), bf16[8,120,4096]{2,1,0:T(8,128)(2,1)}, u32[]{:S(2)}, u32[]{:S(2)}) async-start(bf16[8,120,4096]{2,1,0:T(8,128)(2,1)} %bitcast.83), calls=%async_computation | async-start | bytes 15728640 | tf_op jit(solution)/shard_map/all_to_all | solution.py:75
  86.4 1.4 copy-start.8
  86.4 114.3 %copy-start.13 = (s32[16]{0:T(128)S(1)}, s32[16]{0:T(128)}, u32[]{:S(2)}) copy-start(s32[16]{0:T(128)} %param.12) | copy-start | bytes 196
  87.9 121.2 %collective-permute-start.3 = (bf16[3,192,2048]{2,1,0:T(8,128)(2,1)S(1)}, bf16[3,192,2048]{2,1,0:T(8,128)(2,1)}, u32[]{:S(2)}, u32[]{:S(2)}) collective-permute-start(bf16[3,192,2048]{2,1,0:T(8,128)(2,1)S(1)} %constant_dynamic-update-slice_fusion.2), channel_id=1, source_target_pairs={{0,1},{1,0},{2,3},{3,2},{4,5},{5,4},{6,7},{7,6},{8,9},{9,8},{10,11... | collective-permute-start | bytes 7077896 | tf_op jit(solution)/shard_map/ppermute | solution.py:10
  209.1 4.7 copy-start.2
  221.8 3.6 copy-start.9
  257.3 49.9 %all-to-all-start.2 = ((bf16[8,2,60,2048]{3,1,2,0:T(2,128)(2,1)}), bf16[8,2,60,2048]{3,1,2,0:T(2,128)(2,1)}, u32[]{:S(2)}, u32[]{:S(2)}) async-start(bf16[8,2,60,2048]{3,1,2,0:T(2,128)(2,1)} %copy.93), calls=%async_computation.2 | async-start | bytes 7864320 | tf_op jit(solution)/shard_map/all_to_all | solution.py:123
  307.2 96.1 %all-to-all-start.1 = ((bf16[8,2,60,2048]{3,1,2,0:T(2,128)(2,1)}), bf16[8,2,60,2048]{3,1,2,0:T(2,128)(2,1)}, u32[]{:S(2)}, u32[]{:S(2)}) async-start(bf16[8,2,60,2048]{3,1,2,0:T(2,128)(2,1)} %copy.92), calls=%async_computation.1 | async-start | bytes 7864320 | tf_op jit(solution)/shard_map/all_to_all | solution.py:123
  311.9 4.1 copy-start.10
  312.0 8.3 %slice-start = ((s8[7864320]{0:T(1024)(128)(4,1)}), s8[4194304]{0:T(1024)(128)(4,1)S(1)}, s32[]{:S(2)}) async-start(s8[7864320]{0:T(1024)(128)(4,1)} %bitcast.84), calls=%async_computation.3 | async-start | bytes 8388608
  316.1 4.2 slice-start.1
  316.1 4.2 copy-start.14
  323.6 53.7 %collective-permute-start.6 = (bf16[3,192,2048]{2,1,0:T(8,128)(2,1)S(1)}, bf16[3,192,2048]{2,1,0:T(8,128)(2,1)S(1)}, u32[]{:S(2)}, u32[]{:S(2)}) collective-permute-start(bf16[3,192,2048]{2,1,0:T(8,128)(2,1)S(1)} %slice.257), channel_id=1, source_target_pairs={{0,1},{1,0},{2,3},{3,2},{4,5},{5,4},{6,7},{7,6},{8,9},{9,8},{10,11... | collective-permute-start | bytes 7077896 | tf_op jit(solution)/shard_map/ppermute | solution.py:10
  400.2 1.9 copy-start.5
  402.1 22.0 %copy-start = (bf16[480,2048]{1,0:T(8,128)(2,1)}, bf16[480,2048]{1,0:T(8,128)(2,1)S(1)}, u32[]{:S(2)}) copy-start(bf16[480,2048]{1,0:T(8,128)(2,1)S(1)} %reshape_squeeze.13) | copy-start | bytes 5898244
  403.2 41.0 %collective-permute-start.5 = (f32[128,6]{0,1:T(8,128)S(1)}, f32[128,6]{0,1:T(8,128)S(1)}, u32[]{:S(2)}, u32[]{:S(2)}) collective-permute-start(f32[128,6]{0,1:T(8,128)S(1)} %get-tuple-element.32), channel_id=1, source_target_pairs={{0,16},{16,0},{1,17},{17,1},{2,18},{18,2},{3,19},{19,3},{4,20},{20... | collective-permute-start | bytes 9224 | tf_op jit(solution)/shard_map/ppermute | solution.py:10
  431.4 6.1 %copy-start.6 = (bf16[128,2048]{1,0:T(8,128)(2,1)S(1)}, bf16[128,2048]{1,0:T(8,128)(2,1)}, u32[]{:S(2)}) copy-start(bf16[128,2048]{1,0:T(8,128)(2,1)} %param.9) | copy-start | bytes 1572868
  434.6 48.4 %collective-permute-start.4 = (bf16[128,4096]{1,0:T(8,128)(2,1)}, bf16[128,4096]{1,0:T(8,128)(2,1)}, u32[]{:S(2)}, u32[]{:S(2)}) collective-permute-start(bf16[128,4096]{1,0:T(8,128)(2,1)} %pad_maximum_fusion.3), channel_id=1, source_target_pairs={{0,16},{16,0},{1,17},{17,1},{2,18},{18,2},{3,19},{19,3},{4,20},{20... | collective-permute-start | bytes 3145736 | tf_op jit(solution)/shard_map/ppermute | solution.py:10
  441.4 41.6 %copy-start.1 = (f32[384,2048]{1,0:T(8,128)S(1)}, f32[384,2048]{1,0:T(8,128)}, u32[]{:S(2)}) copy-start(f32[384,2048]{1,0:T(8,128)} %fusion.23) | copy-start | bytes 9437188
  444.2 40.9 %copy-start.3 = (bf16[480,2048]{1,0:T(8,128)(2,1)S(1)}, bf16[480,2048]{1,0:T(8,128)(2,1)}, u32[]{:S(2)}) copy-start(bf16[480,2048]{1,0:T(8,128)(2,1)} %reshape_squeeze.15) | copy-start | bytes 5898244

commit v4 on v2

--- a/solution.py
+++ b/solution.py
@@ -71,12 +71,9 @@
     picked = jnp.dot(pick, all_rows, preferred_element_type=jnp.float32)
     send_x = picked[:, :width].astype(jnp.bfloat16)
     send_c = (slot_gate[:, None] * picked[:, width:]).astype(jnp.bfloat16)
-    send = jnp.stack(
-        [send_x.reshape(half_experts, 2 * slots, width), send_c.reshape(half_experts, 2 * slots, width)],
-        axis=1,
-    )
+    send = jnp.concatenate([send_x, send_c], axis=1).reshape(half_experts, 2 * slots, 2 * width)
     got = lax.all_to_all(send, "inner", split_axis=0, concat_axis=0, tiled=True)
-    got = got.reshape(n_in, local_experts, 2, 2, slots, width)
+    got = got.reshape(n_in, local_experts, 2, slots, 2 * width)
 
     earlier = jnp.cumsum(all_counts, axis=0) - all_counts
     holders = jnp.arange(n_in, dtype=jnp.int32)[:, None]
@@ -86,10 +83,13 @@
     before = earlier[sources][:, :, mine].transpose(0, 2, 1)
     ranks = jnp.arange(slots, dtype=jnp.int32)
     keep = before[..., None] + ranks < capacity[mine][None, :, None, None]
-    got = jnp.where(keep[:, :, None, :, :, None], got, jnp.zeros((), got.dtype))
-    got = got.transpose(1, 2, 0, 3, 4, 5).reshape(local_experts, 2, n_in * 2 * slots, width)
-    rows_in = got[:, 0]
-    rows_cot = got[:, 1]
+    got = jnp.where(keep[..., None], got, jnp.zeros((), got.dtype))
+    if local_experts == 1:
+        got = got.reshape(1, n_in * 2 * slots, 2 * width)
+    else:
+        got = got.transpose(1, 0, 2, 3, 4).reshape(local_experts, n_in * 2 * slots, 2 * width)
+    rows_in = got[:, :, :width]
+    rows_cot = got[:, :, width:]
 
     full = jnp.concatenate(pieces, axis=1)
     full_gate = full[:local_experts]

time: 411 us -> 376 us (0.915); the launches traced: 403 us -> 375 us
  local copies, waits for them, and re-layouts: 71 us -> 33.8 us
  other arithmetic: 25.7 us -> 34.6 us
    transpose x1 -> x0, local copies, waits for them, and re-layouts: 13.7 us -> none  [on_device(): got.transpose(1, 2, 0, 3, 4, 5)]
    slice x2 -> x1, local copies, waits for them, and re-layouts: 12.7 us -> 0.25 us  [the longest x1 12.5 us: on_device(): rows_in = got[:, 0]]
    all_to_all x1 -> x0, local copies, waits for them, and re-layouts: 7.56 us -> none  [on_device(): got = lax.all_to_all(send, 'inner', split_axis=0, concat_axis=0, tiled=True)]
    concatenate x0 -> x1, other arithmetic: none -> 7.4 us  [on_device(): jnp.concatenate([send_x, send_c], axis=1)]
    select_n x0 -> x1, other arithmetic: none -> 6.89 us  [on_device(): got = jnp.where(keep[..., None], got, jnp.zeros((), got.dtype))]
    unnamed x49 -> x42, local copies, waits for them, and re-layouts: 12.7 us -> 8.17 us
  transfers between devices with their start and end apart: 9 -> 9, of which waited for: 3 -> 3; matrix products, arithmetic and copies ran while one was open for 23% -> 16% of each run, Pallas kernels for 0% -> 0%
where the time goes in v4:
time: 376 us; the launch traced here: 375 us
  waiting for transfers between devices  149 us (40%)
  blocking collectives  90.8 us (24%)
  matrix products  42.6 us (11%)
  other arithmetic  34.6 us (9%)
  local copies, waits for them, and re-layouts  33.8 us (9%)
  starting transfers between devices  23.1 us (6%)
    psum x1, blocking collectives, on_device(): all_counts = lax.psum(count_rows, ('half', 'inner'))  90.8 us
    ppermute x7, waiting for transfers between devices, shifted(): lax.ppermute(value, axis, [(j, (j + shift) % count) for j in range(count)])  78.8 us
    all_to_all x1, waiting for transfers between devices, on_device(): lax.all_to_all(back, 'inner', split_axis=0, concat_axis=0, tiled=True)  70.4 us
    ppermute x7, starting transfers between devices, shifted(): lax.ppermute(value, axis, [(j, (j + shift) % count) for j in range(count)])  12.8 us
    unnamed x42, local copies, waits for them, and re-layouts  8.17 us
  transfers between devices with their start and end apart: 9, of which 3 were waited for; matrix products, arithmetic and copies ran while one was open for 16% of the time, Pallas kernels for 0%

profile of v4, /device:TPU:0, one launch (start us, length us, event | category | flops | bytes accessed | tf_op | source)
XLA Modules:
  0.0 375.3 jit_solution(2328853660076526013)
XLA Ops:
  2.8 4.1 %collective-permute-start.2 = (bf16[128,4096]{1,0:T(8,128)(2,1)S(1)}, bf16[128,4096]{1,0:T(8,128)(2,1)S(1)}, u32[]{:S(2)}, u32[]{:S(2)}) collective-permute-start(bf16[128,4096]{1,0:T(8,128)(2,1)S(1)} %constant_dynamic-update-slice_fusion.2), channel_id=1, source_target_pairs={{0,16},{16,0},{1,17},{17,1},{2,18},{18,2},{3,19},{19,3},{4,20},{20... | collective-permute-start | bytes 3145736 | tf_op jit(solution)/shard_map/ppermute | solution.py:10
  8.0 1.7 reduce-window.6
  11.1 2.9 collective-permute-start.1
  15.1 37.8 %collective-permute-done = s32[128,6]{0,1:T(8,128)S(1)} collective-permute-done((s32[128,6]{0,1:T(8,128)S(1)}, s32[128,6]{0,1:T(8,128)S(1)}, u32[]{:S(2)}, u32[]{:S(2)}) %collective-permute-start) | collective-permute-done | bytes 3104 | tf_op jit(solution)/shard_map/ppermute | solution.py:10
  54.2 6.2 %scatter_custom_fusion = s32[960]{0:T(1024)S(1)} fusion(s32[1536]{0:T(1024)S(1)} %fusion.38, s32[1536]{0:T(1024)S(1)} %reshape.486, s32[]{:T(128)} %constant.22.clone.1), kind=kCustom, calls=%fused_computation.111 | custom fusion | bytes 3844 | tf_op jit(solution)/shard_map/scatter | solution.py:62
  60.4 6.2 %scatter_custom_fusion.1 = f32[960]{0:T(1024)S(1)} fusion(s32[1536]{0:T(1024)S(1)} %fusion.38, f32[1536]{0:T(1024)S(1)} %reshape.494, f32[]{:T(128)} %constant.33.clone.1), kind=kCustom, calls=%fused_computation.109 | custom fusion | bytes 3844 | tf_op jit(solution)/shard_map/scatter | solution.py:65
  66.6 2.2 fusion.7
  68.8 2.5 slice.224
  71.4 2.5 fusion
  73.8 7.4 %pad_maximum_fusion.1 = bf16[960,4096]{1,0:T(8,128)(2,1)} fusion(bf16[960,2048]{1,0:T(8,128)(2,1)} %fusion, bf16[960,2048]{1,0:T(8,128)(2,1)} %slice.224), kind=kLoop, calls=%fused_computation.7 | loop fusion | flops 15728640 | bytes 15728640 | tf_op jit(solution)/shard_map/concatenate | solution.py:74
  81.2 5.1 %all-to-all-start = ((bf16[8,120,4096]{2,1,0:T(8,128)(2,1)}), bf16[8,120,4096]{2,1,0:T(8,128)(2,1)}, u32[]{:S(2)}, u32[]{:S(2)}) async-start(bf16[8,120,4096]{2,1,0:T(8,128)(2,1)} %bitcast.84), calls=%async_computation | async-start | bytes 15728640 | tf_op jit(solution)/shard_map/all_to_all | solution.py:75
  87.8 1.6 collective-permute-start.3
  89.8 90.8 %psum.7 = s32[16,16]{1,0:T(8,128)S(1)} all-reduce(s32[16,16]{1,0:T(8,128)S(1)} %broadcast_select_fusion), channel_id=1, replica_groups=mesh['half'=2,'inner'=8,'dp'=2] {'half','inner'}, use_global_device_ids=true, to_apply=%region_4.5 | all-reduce | flops 256 | bytes 2048 | tf_op jit(solution)/shard_map/psum | solution.py:49
  183.1 6.9 %bitcast_select_fusion = bf16[1,960,4096]{2,1,0:T(8,128)(2,1)} fusion(pred[960]{0:T(1024)(128)(4,1)S(1)} %lt.82, bf16[1,960,4096]{2,1,0:T(8,128)(2,1)} %bitcast.82), kind=kLoop, calls=%fused_computation.9 | loop fusion | flops 3932160 | bytes 15729600 | tf_op jit(solution)/shard_map/jit(_where)/select_n | solution.py:86
  190.0 4.7 %fusion.3 = f32[960,384]{1,0:T(8,128)S(1)} fusion(bf16[1,960,4096]{2,1,0:T(8,128)(2,1)} %bitcast_select_fusion, bf16[3,192,2048]{2,1,0:T(8,128)(2,1)} %collective-permute-done.3, bf16[3,192,2048]{2,1,0:T(8,128)(2,1)S(1)} %constant_dynamic-update-slice_fusion.4), kind=kOutput, calls=%fused_computation.26 | convolution fusion | flops 1513095168 | bytes 10125312 | tf_op jit(solution)/shard_map/erd,efd->erf/dot_general | solution.py:107
  194.7 3.3 fusion.6
  198.0 3.8 %multiply_convert_fusion.2 = (bf16[960,384]{1,0:T(8,128)(2,1)S(1)}, bf16[960,384]{1,0:T(8,128)(2,1)S(1)}, bf16[960,384]{1,0:T(8,128)(2,1)S(1)}) fusion(f32[960,384]{1,0:T(8,128)S(1)} %fusion.6, f32[960,384]{1,0:T(8,128)S(1)} %fusion.3, bf16[3,192,2048]{2,1,0:T(8,128)(2,1)S(1)} %constant_dynamic-update-slice_fusion.4, ...), kind=kOutput, calls=%fused_computation.52 | convolution fusion | flops 1518256128 | bytes 13811712 | tf_op jit(solution)/shard_map/erd,efd->erf/dot_general | solution.py:100
  201.8 5.7 %convolution_convert_fusion = bf16[960,2048]{1,0:T(8,128)(2,1)} fusion(bf16[960,384]{1,0:T(8,128)(2,1)S(1)} %get-tuple-element.35, bf16[3,192,2048]{2,1,0:T(8,128)(2,1)} %collective-permute-done.3, bf16[3,192,2048]{2,1,0:T(8,128)(2,1)S(1)} %constant_dynamic-update-slice_fusion.4), kind=kOutput, calls=%fused_computation.24 | convolution fusion | flops 1515061248 | bytes 9388032 | tf_op jit(solution)/shard_map/erf,efd->erd/dot_general | solution.py:104
  207.6 3.3 fusion.52
  210.9 3.4 add_convert_fusion
  214.3 5.9 %maximum_bitcast_fusion = bf16[8,2,120,2048]{3,2,1,0:T(8,128)(2,1)} fusion(bf16[1,1,8,120,2048]{4,3,1,2,0:T(8,128)(2,1)S(1)} %bitcast.87, bf16[1,1,8,120,2048]{4,3,1,2,0:T(8,128)(2,1)} %bitcast.93), kind=kLoop, calls=%fused_computation.8 | loop fusion | flops 3932160 | bytes 15728640 | tf_op jit(solution)/shard_map/reshape | solution.py:122
  220.3 5.1 %all-to-all-start.1 = ((bf16[8,2,120,2048]{3,2,1,0:T(8,128)(2,1)}), bf16[8,2,120,2048]{3,2,1,0:T(8,128)(2,1)}, u32[]{:S(2)}, u32[]{:S(2)}) async-start(bf16[8,2,120,2048]{3,2,1,0:T(8,128)(2,1)} %maximum_bitcast_fusion), calls=%async_computation.1 | async-start | bytes 15728640 | tf_op jit(solution)/shard_map/all_to_all | solution.py:123
  225.4 4.1 %convolution_bitcast_fusion = f32[1,384,2048]{2,1,0:T(8,128)S(1)} fusion(bf16[960,384]{1,0:T(8,128)(2,1)S(1)} %get-tuple-element.37, bf16[1,960,4096]{2,1,0:T(8,128)(2,1)} %bitcast_select_fusion), kind=kOutput, calls=%fused_computation.28 | convolution fusion | flops 1509949440 | bytes 7815168 | tf_op jit(solution)/shard_map/erf,erd->efd/dot_general | solution.py:118
  229.6 4.1 %convolution_bitcast_fusion.1 = f32[1,384,2048]{2,1,0:T(8,128)S(1)} fusion(bf16[960,384]{1,0:T(8,128)(2,1)S(1)} %copy-done.9, bf16[1,960,4096]{2,1,0:T(8,128)(2,1)} %bitcast_select_fusion), kind=kOutput, calls=%fused_computation.29 | convolution fusion | flops 1509949440 | bytes 7815168 | tf_op jit(solution)/shard_map/erf,erd->efd/dot_general | solution.py:117
  233.7 1.8 fusion.4
  236.7 3.6 copy-done
  242.3 70.4 %all-to-all-done.1 = bf16[8,2,120,2048]{3,2,1,0:T(8,128)(2,1)} async-done(((bf16[8,2,120,2048]{3,2,1,0:T(8,128)(2,1)}), bf16[8,2,120,2048]{3,2,1,0:T(8,128)(2,1)}, u32[]{:S(2)}, u32[]{:S(2)}) %all-to-all-start.1) | async-done | bytes 7864352 | tf_op jit(solution)/shard_map/all_to_all | solution.py:123
  312.7 3.7 fusion.55
  317.7 1.9 select_reduce_fusion
  319.7 3.5 fusion.16
  327.1 2.6 fusion.1
  332.4 41.0 %collective-permute-done.5 = f32[128,6]{0,1:T(8,128)S(1)} collective-permute-done((f32[128,6]{0,1:T(8,128)S(1)}, f32[128,6]{0,1:T(8,128)S(1)}, u32[]{:S(2)}, u32[]{:S(2)}) %collective-permute-start.5) | collective-permute-done | bytes 3104 | tf_op jit(solution)/shard_map/ppermute | solution.py:10
  (110 shorter events, 24.0 us)
Async XLA Ops:
  2.8 66.0 %copy-start.2 = (bf16[128,4096]{1,0:T(8,128)(2,1)}, bf16[128,4096]{1,0:T(8,128)(2,1)S(1)}, u32[]{:S(2)}) copy-start(bf16[128,4096]{1,0:T(8,128)(2,1)S(1)} %constant_dynamic-update-slice_fusion.2) | copy-start | bytes 3145732
  2.8 63.7 %collective-permute-start.2 = (bf16[128,4096]{1,0:T(8,128)(2,1)S(1)}, bf16[128,4096]{1,0:T(8,128)(2,1)S(1)}, u32[]{:S(2)}, u32[]{:S(2)}) collective-permute-start(bf16[128,4096]{1,0:T(8,128)(2,1)S(1)} %constant_dynamic-update-slice_fusion.2), channel_id=1, source_target_pairs={{0,16},{16,0},{1,17},{17,1},{2,18},{18,2},{3,19},{19,3},{4,20},{20... | collective-permute-start | bytes 3145736 | tf_op jit(solution)/shard_map/ppermute | solution.py:10
  11.0 41.8 %collective-permute-start = (s32[128,6]{0,1:T(8,128)S(1)}, s32[128,6]{0,1:T(8,128)S(1)}, u32[]{:S(2)}, u32[]{:S(2)}) collective-permute-start(s32[128,6]{0,1:T(8,128)S(1)} %multiply_add_fusion), channel_id=1, source_target_pairs={{0,16},{16,0},{1,17},{17,1},{2,18},{18,2},{3,19},{19,3},{4,20},{20... | collective-permute-start | bytes 9224 | tf_op jit(solution)/shard_map/ppermute | solution.py:10
  11.1 42.7 %collective-permute-start.1 = (f32[128,6]{0,1:T(8,128)}, f32[128,6]{0,1:T(8,128)S(1)}, u32[]{:S(2)}, u32[]{:S(2)}) collective-permute-start(f32[128,6]{0,1:T(8,128)} %param.11), channel_id=1, source_target_pairs={{0,16},{16,0},{1,17},{17,1},{2,18},{18,2},{3,19},{19,3},{4,20},{20... | collective-permute-start | bytes 9224 | tf_op jit(solution)/shard_map/ppermute | solution.py:10
  66.6 2.3 copy-start.4
  81.2 5.1 %copy-start.6 = (bf16[1,192,2048]{2,1,0:T(8,128)(2,1)S(1)}, bf16[1,192,2048]{2,1,0:T(8,128)(2,1)}, u32[]{:S(2)}) copy-start(bf16[1,192,2048]{2,1,0:T(8,128)(2,1)} %param.13) | copy-start | bytes 2359300
  81.2 101.8 %all-to-all-start = ((bf16[8,120,4096]{2,1,0:T(8,128)(2,1)}), bf16[8,120,4096]{2,1,0:T(8,128)(2,1)}, u32[]{:S(2)}, u32[]{:S(2)}) async-start(bf16[8,120,4096]{2,1,0:T(8,128)(2,1)} %bitcast.84), calls=%async_computation | async-start | bytes 15728640 | tf_op jit(solution)/shard_map/all_to_all | solution.py:75
  86.4 1.4 copy-start.7
  86.4 95.2 %copy-start.10 = (s32[16]{0:T(128)S(1)}, s32[16]{0:T(128)}, u32[]{:S(2)}) copy-start(s32[16]{0:T(128)} %param.12) | copy-start | bytes 196
  87.8 102.1 %collective-permute-start.3 = (bf16[3,192,2048]{2,1,0:T(8,128)(2,1)S(1)}, bf16[3,192,2048]{2,1,0:T(8,128)(2,1)}, u32[]{:S(2)}, u32[]{:S(2)}) collective-permute-start(bf16[3,192,2048]{2,1,0:T(8,128)(2,1)S(1)} %constant_dynamic-update-slice_fusion.4), channel_id=1, source_target_pairs={{0,1},{1,0},{2,3},{3,2},{4,5},{5,4},{6,7},{7,6},{8,9},{9,8},{10,11... | collective-permute-start | bytes 7077896 | tf_op jit(solution)/shard_map/ppermute | solution.py:10
  190.0 4.7 %copy-start.1 = (bf16[1,960,4096]{2,1,0:T(8,128)(2,1)S(1)}, bf16[1,960,4096]{2,1,0:T(8,128)(2,1)}, u32[]{:S(2)}) copy-start(bf16[1,960,4096]{2,1,0:T(8,128)(2,1)} %bitcast_select_fusion) | copy-start | bytes 23592964
  201.8 5.8 %copy-start.11 = (bf16[960,384]{1,0:T(8,128)(2,1)}, bf16[960,384]{1,0:T(8,128)(2,1)S(1)}, u32[]{:S(2)}) copy-start(bf16[960,384]{1,0:T(8,128)(2,1)S(1)} %get-tuple-element.35) | copy-start | bytes 2211844
  201.8 9.1 %copy-start.8 = (bf16[960,384]{1,0:T(8,128)(2,1)}, bf16[960,384]{1,0:T(8,128)(2,1)S(1)}, u32[]{:S(2)}) copy-start(bf16[960,384]{1,0:T(8,128)(2,1)S(1)} %get-tuple-element.36) | copy-start | bytes 2211844
  220.3 92.4 %all-to-all-start.1 = ((bf16[8,2,120,2048]{3,2,1,0:T(8,128)(2,1)}), bf16[8,2,120,2048]{3,2,1,0:T(8,128)(2,1)}, u32[]{:S(2)}, u32[]{:S(2)}) async-start(bf16[8,2,120,2048]{3,2,1,0:T(8,128)(2,1)} %maximum_bitcast_fusion), calls=%async_computation.1 | async-start | bytes 15728640 | tf_op jit(solution)/shard_map/all_to_all | solution.py:123
  225.4 4.1 %copy-start.9 = (bf16[960,384]{1,0:T(8,128)(2,1)S(1)}, bf16[960,384]{1,0:T(8,128)(2,1)}, u32[]{:S(2)}) copy-start(bf16[960,384]{1,0:T(8,128)(2,1)} %copy-done.8) | copy-start | bytes 2211844
  225.4 8.3 %slice-start.3 = ((s8[7864320]{0:T(1024)(128)(4,1)}), s8[4194304]{0:T(1024)(128)(4,1)S(1)}, s32[]{:S(2)}) async-start(s8[7864320]{0:T(1024)(128)(4,1)} %bitcast.88), calls=%async_computation.5 | async-start | bytes 8388608
  229.5 4.2 %slice-start.4 = ((s8[7864320]{0:T(1024)(128)(4,1)}), s8[3670016]{0:T(1024)(128)(4,1)S(1)}, s32[]{:S(2)}) async-start(s8[7864320]{0:T(1024)(128)(4,1)} %bitcast.88), calls=%async_computation.6 | async-start | bytes 7340032
  229.5 4.2 %copy-start.12 = (bf16[960,384]{1,0:T(8,128)(2,1)S(1)}, bf16[960,384]{1,0:T(8,128)(2,1)}, u32[]{:S(2)}) copy-start(bf16[960,384]{1,0:T(8,128)(2,1)} %copy-done.11) | copy-start | bytes 2211844
  236.7 3.6 copy-start
  240.7 75.7 %copy-start.3 = (bf16[128,4096]{1,0:T(8,128)(2,1)S(1)}, bf16[128,4096]{1,0:T(8,128)(2,1)}, u32[]{:S(2)}) copy-start(bf16[128,4096]{1,0:T(8,128)(2,1)} %copy-done.2) | copy-start | bytes 3145732
  240.7 85.9 %collective-permute-start.6 = (bf16[3,192,2048]{2,1,0:T(8,128)(2,1)S(1)}, bf16[3,192,2048]{2,1,0:T(8,128)(2,1)}, u32[]{:S(2)}, u32[]{:S(2)}) collective-permute-start(bf16[3,192,2048]{2,1,0:T(8,128)(2,1)S(1)} %slice.225), channel_id=1, source_target_pairs={{0,1},{1,0},{2,3},{3,2},{4,5},{5,4},{6,7},{7,6},{8,9},{9,8},{10,11... | collective-permute-start | bytes 7077896 | tf_op jit(solution)/shard_map/ppermute | solution.py:10
  312.7 3.7 copy-start.5
  323.2 3.4 slice-start
  323.2 3.5 slice-start.1
  323.8 3.2 slice-start.2
  325.3 48.8 %collective-permute-start.4 = (bf16[128,4096]{1,0:T(8,128)(2,1)S(1)}, bf16[128,4096]{1,0:T(8,128)(2,1)S(1)}, u32[]{:S(2)}, u32[]{:S(2)}) collective-permute-start(bf16[128,4096]{1,0:T(8,128)(2,1)S(1)} %pad_maximum_fusion.3), channel_id=1, source_target_pairs={{0,16},{16,0},{1,17},{17,1},{2,18},{18,2},{3,19},{19,3},{4,20},{20... | collective-permute-start | bytes 3145736 | tf_op jit(solution)/shard_map/ppermute | solution.py:10
  329.7 43.8 %collective-permute-start.5 = (f32[128,6]{0,1:T(8,128)S(1)}, f32[128,6]{0,1:T(8,128)S(1)}, u32[]{:S(2)}, u32[]{:S(2)}) collective-permute-start(f32[128,6]{0,1:T(8,128)S(1)} %slice.158), channel_id=1, source_target_pairs={{0,16},{16,0},{1,17},{17,1},{2,18},{18,2},{3,19},{19,3},{4,20},{20... | collective-permute-start | bytes 9224 | tf_op jit(solution)/shard_map/ppermute | solution.py:10

commit v5 on v4

--- a/solution.py
+++ b/solution.py
@@ -58,20 +58,14 @@
     side = (jnp.arange(2 * tok_rows, dtype=jnp.int32) >= tok_rows).astype(jnp.int32)[:, None]
     dest = jnp.where(inside, (local * 2 + side) * slots + all_code % slots, 2 * half_rows)
 
-    row_of = jnp.broadcast_to(jnp.arange(2 * tok_rows, dtype=jnp.int32)[:, None], dest.shape)
-    filled_by = jnp.full((2 * half_rows,), -1, jnp.int32).at[dest.reshape(-1)].set(
-        row_of.reshape(-1), mode="drop"
-    )
-    slot_gate = jnp.zeros((2 * half_rows,), jnp.float32).at[dest.reshape(-1)].set(
-        all_gates.reshape(-1), mode="drop"
-    )
-    pick = (filled_by[:, None] == jnp.arange(2 * tok_rows, dtype=jnp.int32)[None, :]).astype(
-        jnp.bfloat16
-    )
+    slot_ids = jnp.arange(2 * half_rows, dtype=jnp.int32)[:, None, None]
+    lands = dest[None, :, :] == slot_ids
+    pick = jnp.any(lands, axis=2).astype(jnp.bfloat16)
+    slot_gate = jnp.sum(jnp.where(lands, all_gates[None, :, :], 0.0), axis=(1, 2))
     picked = jnp.dot(pick, all_rows, preferred_element_type=jnp.float32)
-    send_x = picked[:, :width].astype(jnp.bfloat16)
-    send_c = (slot_gate[:, None] * picked[:, width:]).astype(jnp.bfloat16)
-    send = jnp.concatenate([send_x, send_c], axis=1).reshape(half_experts, 2 * slots, 2 * width)
+    lane = jnp.arange(2 * width, dtype=jnp.int32)[None, :]
+    scale = jnp.where(lane < width, 1.0, slot_gate[:, None])
+    send = (picked * scale).astype(jnp.bfloat16).reshape(half_experts, 2 * slots, 2 * width)
     got = lax.all_to_all(send, "inner", split_axis=0, concat_axis=0, tiled=True)
     got = got.reshape(n_in, local_experts, 2, slots, 2 * width)
 

time: 376 us -> 359 us (0.955)
  local copies, waits for them, and re-layouts: 33.8 us -> 16.8 us
  other arithmetic: 34.6 us -> 26.5 us
  waiting for transfers between devices: 149 us -> 154 us
    scatter x2 -> x0, local copies, waits for them, and re-layouts: 12.4 us -> none  [the longest x1 6.18 us: on_device(): jnp.full((2 * half_rows,), -1, jnp.int32).at[dest.reshape(-1)]]
    concatenate x1 -> x0, other arithmetic: 7.4 us -> none  [on_device(): jnp.concatenate([send_x, send_c], axis=1)]
    ppermute x7, waiting for transfers between devices: 78.8 us -> 83.8 us  [shifted(): lax.ppermute(value, axis, [(j, (j + shift) % count) for j in range(count)])]
  transfers between devices with their start and end apart: 9 -> 9, of which waited for: 3 -> 3; matrix products, arithmetic and copies ran while one was open for 16% -> 14% of each run, Pallas kernels for 0% -> 0%
where the time goes in v5:
time: 359 us; the launch traced here: 358 us
  waiting for transfers between devices  154 us (43%)
  blocking collectives  90.6 us (25%)
  matrix products  44.8 us (12%)
  other arithmetic  26.5 us (7%)
  starting transfers between devices  23.7 us (7%)
  local copies, waits for them, and re-layouts  16.8 us (5%)
    psum x1, blocking collectives, on_device(): all_counts = lax.psum(count_rows, ('half', 'inner'))  90.6 us
    ppermute x7, waiting for transfers between devices, shifted(): lax.ppermute(value, axis, [(j, (j + shift) % count) for j in range(count)])  83.8 us
    all_to_all x1, waiting for transfers between devices, on_device(): lax.all_to_all(back, 'inner', split_axis=0, concat_axis=0, tiled=True)  70.4 us
    ppermute x7, starting transfers between devices, shifted(): lax.ppermute(value, axis, [(j, (j + shift) % count) for j in range(count)])  13.3 us
    unnamed x42, local copies, waits for them, and re-layouts  7.68 us
  transfers between devices with their start and end apart: 9, of which 3 were waited for; matrix products, arithmetic and copies ran while one was open for 14% of the time, Pallas kernels for 0%

profile of v5, /device:TPU:0, one launch (start us, length us, event | category | flops | bytes accessed | tf_op | source)
XLA Modules:
  0.0 357.7 jit_solution(1905141854798472884)
XLA Ops:
  0.6 4.1 %collective-permute-start.1 = (f32[128,6]{0,1:T(8,128)}, f32[128,6]{0,1:T(8,128)S(1)}, u32[]{:S(2)}, u32[]{:S(2)}) collective-permute-start(f32[128,6]{0,1:T(8,128)} %param.11), channel_id=1, source_target_pairs={{0,16},{16,0},{1,17},{17,1},{2,18},{18,2},{3,19},{19,3},{4,20},{20... | collective-permute-start | bytes 9224 | tf_op jit(solution)/shard_map/ppermute | solution.py:10
  5.8 1.7 reduce-window.6
  11.0 3.0 collective-permute-start.2
  16.4 42.7 %collective-permute-done.2 = bf16[128,4096]{1,0:T(8,128)(2,1)S(1)} collective-permute-done((bf16[128,4096]{1,0:T(8,128)(2,1)S(1)}, bf16[128,4096]{1,0:T(8,128)(2,1)S(1)}, u32[]{:S(2)}, u32[]{:S(2)}) %collective-permute-start.2) | collective-permute-done | bytes 1048608 | tf_op jit(solution)/shard_map/ppermute | solution.py:10
  59.1 4.4 %multiply_convert_fusion = bf16[960,4096]{1,0:T(8,128)(2,1)} fusion(pred[960,256]{1,0:T(8,128)(4,1)S(1)} %fusion, f32[960]{0:T(1024)S(1)} %select_reduce_fusion.1, pred[4096]{0:T(1024)(128)(4,1)S(1)} %iota_compare_fusion.4, bf16[128,4096]{1,0:T(8,128)(2,1)S(1)} %collective-permute-done.2, bf16[128,4096]{1,0:T(8,128)(2,1)S(1)} %constant_dynamic-update-slice_fusion.2), kind=kOutput, calls=%fused_computation.1 | convolution fusion | flops 2029256704 | bytes 10215168 | tf_op jit(solution)/shard_map/dot_general | solution.py:65
  63.5 5.1 %all-to-all-start = ((bf16[8,120,4096]{2,1,0:T(8,128)(2,1)}), bf16[8,120,4096]{2,1,0:T(8,128)(2,1)}, u32[]{:S(2)}, u32[]{:S(2)}) async-start(bf16[8,120,4096]{2,1,0:T(8,128)(2,1)} %bitcast.88), calls=%async_computation | async-start | bytes 15728640 | tf_op jit(solution)/shard_map/all_to_all | solution.py:69
  70.1 1.6 collective-permute-start.3
  72.2 90.6 %psum.7 = s32[16,16]{1,0:T(8,128)S(1)} all-reduce(s32[16,16]{1,0:T(8,128)S(1)} %broadcast_select_fusion), channel_id=1, replica_groups=mesh['half'=2,'inner'=8,'dp'=2] {'half','inner'}, use_global_device_ids=true, to_apply=%region_4.5 | all-reduce | flops 256 | bytes 2048 | tf_op jit(solution)/shard_map/psum | solution.py:49
  165.2 6.9 %bitcast_select_fusion = bf16[1,960,4096]{2,1,0:T(8,128)(2,1)} fusion(pred[960]{0:T(1024)(128)(4,1)S(1)} %lt.72, bf16[1,960,4096]{2,1,0:T(8,128)(2,1)} %bitcast.83), kind=kLoop, calls=%fused_computation.4 | loop fusion | flops 3932160 | bytes 15729600 | tf_op jit(solution)/shard_map/jit(_where)/select_n | solution.py:80
  172.1 4.7 %fusion.3 = f32[960,384]{1,0:T(8,128)S(1)} fusion(bf16[1,960,4096]{2,1,0:T(8,128)(2,1)} %bitcast_select_fusion, bf16[3,192,2048]{2,1,0:T(8,128)(2,1)} %collective-permute-done.3, bf16[3,192,2048]{2,1,0:T(8,128)(2,1)S(1)} %constant_dynamic-update-slice_fusion.4), kind=kOutput, calls=%fused_computation.24 | convolution fusion | flops 1513095168 | bytes 10125312 | tf_op jit(solution)/shard_map/erd,efd->erf/dot_general | solution.py:101
  176.7 3.3 fusion.6
  180.1 3.8 %multiply_convert_fusion.3 = (bf16[960,384]{1,0:T(8,128)(2,1)S(1)}, bf16[960,384]{1,0:T(8,128)(2,1)S(1)}, bf16[960,384]{1,0:T(8,128)(2,1)S(1)}) fusion(f32[960,384]{1,0:T(8,128)S(1)} %fusion.6, f32[960,384]{1,0:T(8,128)S(1)} %fusion.3, bf16[3,192,2048]{2,1,0:T(8,128)(2,1)S(1)} %constant_dynamic-update-slice_fusion.4, ...), kind=kOutput, calls=%fused_computation.49 | convolution fusion | flops 1518256128 | bytes 13811712 | tf_op jit(solution)/shard_map/erd,efd->erf/dot_general | solution.py:94
  183.9 5.7 %convolution_convert_fusion = bf16[960,2048]{1,0:T(8,128)(2,1)} fusion(bf16[960,384]{1,0:T(8,128)(2,1)S(1)} %get-tuple-element.33, bf16[3,192,2048]{2,1,0:T(8,128)(2,1)} %collective-permute-done.3, bf16[3,192,2048]{2,1,0:T(8,128)(2,1)S(1)} %constant_dynamic-update-slice_fusion.4), kind=kOutput, calls=%fused_computation.22 | convolution fusion | flops 1515061248 | bytes 9388032 | tf_op jit(solution)/shard_map/erf,efd->erd/dot_general | solution.py:98
  189.7 3.3 fusion.43
  193.0 3.4 add_convert_fusion
  196.4 5.9 %maximum_bitcast_fusion = bf16[8,2,120,2048]{3,2,1,0:T(8,128)(2,1)} fusion(bf16[1,1,8,120,2048]{4,3,1,2,0:T(8,128)(2,1)S(1)} %bitcast.87, bf16[1,1,8,120,2048]{4,3,1,2,0:T(8,128)(2,1)} %bitcast.94), kind=kLoop, calls=%fused_computation.3 | loop fusion | flops 3932160 | bytes 15728640 | tf_op jit(solution)/shard_map/reshape | solution.py:116
  202.4 5.3 %all-to-all-start.1 = ((bf16[8,2,120,2048]{3,2,1,0:T(8,128)(2,1)}), bf16[8,2,120,2048]{3,2,1,0:T(8,128)(2,1)}, u32[]{:S(2)}, u32[]{:S(2)}) async-start(bf16[8,2,120,2048]{3,2,1,0:T(8,128)(2,1)} %maximum_bitcast_fusion), calls=%async_computation.1 | async-start | bytes 15728640 | tf_op jit(solution)/shard_map/all_to_all | solution.py:117
  207.6 4.1 %fusion.4 = f32[1,384,2048]{2,1,0:T(8,128)S(1)} fusion(bf16[960,384]{1,0:T(8,128)(2,1)S(1)} %copy-done.12, bf16[1,960,4096]{2,1,0:T(8,128)(2,1)} %bitcast_select_fusion), kind=kOutput, calls=%fused_computation.25 | convolution fusion | flops 1509949440 | bytes 7815168 | tf_op jit(solution)/shard_map/erf,erd->efd/dot_general | solution.py:110
  211.8 4.1 %convolution_bitcast_fusion.1 = f32[1,384,2048]{2,1,0:T(8,128)S(1)} fusion(bf16[960,384]{1,0:T(8,128)(2,1)S(1)} %get-tuple-element.34, bf16[1,960,4096]{2,1,0:T(8,128)(2,1)} %bitcast_select_fusion), kind=kOutput, calls=%fused_computation.27 | convolution fusion | flops 1509949440 | bytes 7815168 | tf_op jit(solution)/shard_map/erf,erd->efd/dot_general | solution.py:111
  215.9 1.8 convolution_bitcast_fusion
  218.9 3.6 %copy-done = f32[3,384,2048]{2,1,0:T(8,128)} copy-done((f32[3,384,2048]{2,1,0:T(8,128)}, f32[3,384,2048]{2,1,0:T(8,128)S(1)}, u32[]{:S(2)}) %copy-start) | copy-done | bytes 9437208
  222.9 1.5 collective-permute-start.6
  224.5 70.4 %all-to-all-done.1 = bf16[8,2,120,2048]{3,2,1,0:T(8,128)(2,1)} async-done(((bf16[8,2,120,2048]{3,2,1,0:T(8,128)(2,1)}), bf16[8,2,120,2048]{3,2,1,0:T(8,128)(2,1)}, u32[]{:S(2)}, u32[]{:S(2)}) %all-to-all-start.1) | async-done | bytes 7864352 | tf_op jit(solution)/shard_map/all_to_all | solution.py:117
  294.9 3.7 %fusion.46 = (bf16[8,1,120,2048]{3,2,1,0:T(8,128)(2,1)S(1)}, bf16[8,1,120,2048]{3,2,1,0:T(8,128)(2,1)S(1)}) fusion(bf16[8,2,120,2048]{3,2,1,0:T(8,128)(2,1)} %all-to-all-done.1), kind=kLoop, calls=%fused_computation.107 | loop fusion | bytes 15728640 | tf_op jit(solution)/shard_map/slice | solution.py:130
  299.8 1.9 select_reduce_fusion
  301.7 1.3 fusion.49
  303.3 3.6 fusion.15
  307.6 1.3 collective-permute-start.4
  309.0 2.6 fusion.1
  311.6 1.7 collective-permute-start.5
  313.3 1.4 fusion.47
  314.8 41.1 %collective-permute-done.5 = f32[128,6]{0,1:T(8,128)S(1)} collective-permute-done((f32[128,6]{0,1:T(8,128)S(1)}, f32[128,6]{0,1:T(8,128)S(1)}, u32[]{:S(2)}, u32[]{:S(2)}) %collective-permute-start.5) | collective-permute-done | bytes 3104 | tf_op jit(solution)/shard_map/ppermute | solution.py:10
  (95 shorter events, 16.8 us)
Async XLA Ops:
  0.6 14.1 %collective-permute-start.1 = (f32[128,6]{0,1:T(8,128)}, f32[128,6]{0,1:T(8,128)S(1)}, u32[]{:S(2)}, u32[]{:S(2)}) collective-permute-start(f32[128,6]{0,1:T(8,128)} %param.11), channel_id=1, source_target_pairs={{0,16},{16,0},{1,17},{17,1},{2,18},{18,2},{3,19},{19,3},{4,20},{20... | collective-permute-start | bytes 9224 | tf_op jit(solution)/shard_map/ppermute | solution.py:10
  8.8 5.9 %collective-permute-start = (s32[128,6]{0,1:T(8,128)S(1)}, s32[128,6]{0,1:T(8,128)S(1)}, u32[]{:S(2)}, u32[]{:S(2)}) collective-permute-start(s32[128,6]{0,1:T(8,128)S(1)} %multiply_add_fusion), channel_id=1, source_target_pairs={{0,16},{16,0},{1,17},{17,1},{2,18},{18,2},{3,19},{19,3},{4,20},{20... | collective-permute-start | bytes 9224 | tf_op jit(solution)/shard_map/ppermute | solution.py:10
  11.0 52.5 %copy-start.6 = (bf16[128,4096]{1,0:T(8,128)(2,1)}, bf16[128,4096]{1,0:T(8,128)(2,1)S(1)}, u32[]{:S(2)}) copy-start(bf16[128,4096]{1,0:T(8,128)(2,1)S(1)} %constant_dynamic-update-slice_fusion.2) | copy-start | bytes 3145732
  11.0 48.1 %collective-permute-start.2 = (bf16[128,4096]{1,0:T(8,128)(2,1)S(1)}, bf16[128,4096]{1,0:T(8,128)(2,1)S(1)}, u32[]{:S(2)}, u32[]{:S(2)}) collective-permute-start(bf16[128,4096]{1,0:T(8,128)(2,1)S(1)} %constant_dynamic-update-slice_fusion.2), channel_id=1, source_target_pairs={{0,16},{16,0},{1,17},{17,1},{2,18},{18,2},{3,19},{19,3},{4,20},{20... | collective-permute-start | bytes 3145736 | tf_op jit(solution)/shard_map/ppermute | solution.py:10
  59.1 4.4 %copy-start.8 = (bf16[128,4096]{1,0:T(8,128)(2,1)}, bf16[128,4096]{1,0:T(8,128)(2,1)S(1)}, u32[]{:S(2)}) copy-start(bf16[128,4096]{1,0:T(8,128)(2,1)S(1)} %collective-permute-done.2) | copy-start | bytes 3145732
  63.5 5.1 %copy-start.4 = (bf16[1,192,2048]{2,1,0:T(8,128)(2,1)S(1)}, bf16[1,192,2048]{2,1,0:T(8,128)(2,1)}, u32[]{:S(2)}) copy-start(bf16[1,192,2048]{2,1,0:T(8,128)(2,1)} %param.13) | copy-start | bytes 2359300
  63.5 101.6 %all-to-all-start = ((bf16[8,120,4096]{2,1,0:T(8,128)(2,1)}), bf16[8,120,4096]{2,1,0:T(8,128)(2,1)}, u32[]{:S(2)}, u32[]{:S(2)}) async-start(bf16[8,120,4096]{2,1,0:T(8,128)(2,1)} %bitcast.88), calls=%async_computation | async-start | bytes 15728640 | tf_op jit(solution)/shard_map/all_to_all | solution.py:69
  68.7 1.4 copy-start.5
  68.7 94.2 %copy-start.10 = (s32[16]{0:T(128)S(1)}, s32[16]{0:T(128)}, u32[]{:S(2)}) copy-start(s32[16]{0:T(128)} %param.12) | copy-start | bytes 196
  70.1 102.0 %collective-permute-start.3 = (bf16[3,192,2048]{2,1,0:T(8,128)(2,1)S(1)}, bf16[3,192,2048]{2,1,0:T(8,128)(2,1)}, u32[]{:S(2)}, u32[]{:S(2)}) collective-permute-start(bf16[3,192,2048]{2,1,0:T(8,128)(2,1)S(1)} %constant_dynamic-update-slice_fusion.4), channel_id=1, source_target_pairs={{0,1},{1,0},{2,3},{3,2},{4,5},{5,4},{6,7},{7,6},{8,9},{9,8},{10,11... | collective-permute-start | bytes 7077896 | tf_op jit(solution)/shard_map/ppermute | solution.py:10
  172.1 4.7 %copy-start.1 = (bf16[1,960,4096]{2,1,0:T(8,128)(2,1)S(1)}, bf16[1,960,4096]{2,1,0:T(8,128)(2,1)}, u32[]{:S(2)}) copy-start(bf16[1,960,4096]{2,1,0:T(8,128)(2,1)} %bitcast_select_fusion) | copy-start | bytes 23592964
  183.9 5.8 %copy-start.11 = (bf16[960,384]{1,0:T(8,128)(2,1)}, bf16[960,384]{1,0:T(8,128)(2,1)S(1)}, u32[]{:S(2)}) copy-start(bf16[960,384]{1,0:T(8,128)(2,1)S(1)} %get-tuple-element.33) | copy-start | bytes 2211844
  183.9 5.8 %copy-start.2 = (bf16[960,384]{1,0:T(8,128)(2,1)}, bf16[960,384]{1,0:T(8,128)(2,1)S(1)}, u32[]{:S(2)}) copy-start(bf16[960,384]{1,0:T(8,128)(2,1)S(1)} %get-tuple-element.35) | copy-start | bytes 2211844
  202.4 5.3 %copy-start.12 = (bf16[960,384]{1,0:T(8,128)(2,1)S(1)}, bf16[960,384]{1,0:T(8,128)(2,1)}, u32[]{:S(2)}) copy-start(bf16[960,384]{1,0:T(8,128)(2,1)} %copy-done.11) | copy-start | bytes 2211844
  202.4 92.5 %all-to-all-start.1 = ((bf16[8,2,120,2048]{3,2,1,0:T(8,128)(2,1)}), bf16[8,2,120,2048]{3,2,1,0:T(8,128)(2,1)}, u32[]{:S(2)}, u32[]{:S(2)}) async-start(bf16[8,2,120,2048]{3,2,1,0:T(8,128)(2,1)} %maximum_bitcast_fusion), calls=%async_computation.1 | async-start | bytes 15728640 | tf_op jit(solution)/shard_map/all_to_all | solution.py:117
  207.6 8.3 %slice-start.3 = ((s8[7864320]{0:T(1024)(128)(4,1)}), s8[4194304]{0:T(1024)(128)(4,1)S(1)}, s32[]{:S(2)}) async-start(s8[7864320]{0:T(1024)(128)(4,1)} %bitcast.89), calls=%async_computation.5 | async-start | bytes 8388608
  211.7 4.1 %slice-start.4 = ((s8[7864320]{0:T(1024)(128)(4,1)}), s8[3670016]{0:T(1024)(128)(4,1)S(1)}, s32[]{:S(2)}) async-start(s8[7864320]{0:T(1024)(128)(4,1)} %bitcast.89), calls=%async_computation.6 | async-start | bytes 7340032
  211.8 4.1 %copy-start.3 = (bf16[960,384]{1,0:T(8,128)(2,1)S(1)}, bf16[960,384]{1,0:T(8,128)(2,1)}, u32[]{:S(2)}) copy-start(bf16[960,384]{1,0:T(8,128)(2,1)} %copy-done.2) | copy-start | bytes 2211844
  218.9 3.6 %copy-start = (f32[3,384,2048]{2,1,0:T(8,128)}, f32[3,384,2048]{2,1,0:T(8,128)S(1)}, u32[]{:S(2)}) copy-start(f32[3,384,2048]{2,1,0:T(8,128)S(1)} %pad_maximum_fusion) | copy-start | bytes 28311556
  222.9 75.7 %copy-start.7 = (bf16[128,4096]{1,0:T(8,128)(2,1)S(1)}, bf16[128,4096]{1,0:T(8,128)(2,1)}, u32[]{:S(2)}) copy-start(bf16[128,4096]{1,0:T(8,128)(2,1)} %copy-done.6) | copy-start | bytes 3145732
  222.9 86.1 %collective-permute-start.6 = (bf16[3,192,2048]{2,1,0:T(8,128)(2,1)S(1)}, bf16[3,192,2048]{2,1,0:T(8,128)(2,1)}, u32[]{:S(2)}, u32[]{:S(2)}) collective-permute-start(bf16[3,192,2048]{2,1,0:T(8,128)(2,1)S(1)} %slice.209), channel_id=1, source_target_pairs={{0,1},{1,0},{2,3},{3,2},{4,5},{5,4},{6,7},{7,6},{8,9},{9,8},{10,11... | collective-permute-start | bytes 7077896 | tf_op jit(solution)/shard_map/ppermute | solution.py:10
  294.9 3.7 %copy-start.9 = (bf16[128,4096]{1,0:T(8,128)(2,1)S(1)}, bf16[128,4096]{1,0:T(8,128)(2,1)}, u32[]{:S(2)}) copy-start(bf16[128,4096]{1,0:T(8,128)(2,1)} %copy-done.8) | copy-start | bytes 3145732
  303.2 5.7 %slice-start = ((s8[9437184]{0:T(1024)(128)(4,1)}), s8[4194304]{0:T(1024)(128)(4,1)S(1)}, s32[]{:S(2)}) async-start(s8[9437184]{0:T(1024)(128)(4,1)} %bitcast.85), calls=%async_computation.2 | async-start | bytes 8388608
  303.3 5.7 %slice-start.1 = ((s8[9437184]{0:T(1024)(128)(4,1)}), s8[4194304]{0:T(1024)(128)(4,1)S(1)}, s32[]{:S(2)}) async-start(s8[9437184]{0:T(1024)(128)(4,1)} %bitcast.85), calls=%async_computation.3 | async-start | bytes 8388608
  306.8 2.1 slice-start.2
  307.6 48.8 %collective-permute-start.4 = (bf16[128,4096]{1,0:T(8,128)(2,1)S(1)}, bf16[128,4096]{1,0:T(8,128)(2,1)S(1)}, u32[]{:S(2)}, u32[]{:S(2)}) collective-permute-start(bf16[128,4096]{1,0:T(8,128)(2,1)S(1)} %pad_maximum_fusion.2), channel_id=1, source_target_pairs={{0,16},{16,0},{1,17},{17,1},{2,18},{18,2},{3,19},{19,3},{4,20},{20... | collective-permute-start | bytes 3145736 | tf_op jit(solution)/shard_map/ppermute | solution.py:10
  311.6 44.2 %collective-permute-start.5 = (f32[128,6]{0,1:T(8,128)S(1)}, f32[128,6]{0,1:T(8,128)S(1)}, u32[]{:S(2)}, u32[]{:S(2)}) collective-permute-start(f32[128,6]{0,1:T(8,128)S(1)} %slice.147), channel_id=1, source_target_pairs={{0,16},{16,0},{1,17},{17,1},{2,18},{18,2},{3,19},{19,3},{4,20},{20... | collective-permute-start | bytes 9224 | tf_op jit(solution)/shard_map/ppermute | solution.py:10

commit v6 on v5

--- a/solution.py
+++ b/solution.py
@@ -45,8 +45,7 @@
     running = jnp.cumsum(one_hot, axis=0)
     local_rank = jnp.sum(running * one_hot, axis=1) - 1
     counts = running[-1]
-    count_rows = jnp.where(jnp.arange(n_src, dtype=jnp.int32)[:, None] == source, counts[None, :], 0)
-    all_counts = lax.psum(count_rows, ("half", "inner"))
+    all_counts = lax.all_gather(counts, ("half", "inner"))
     code = (flat_ids * slots + local_rank).reshape(tok_rows, top_count)
     partner_code = shifted(code, "half", 2, 1)
 
@@ -66,6 +65,7 @@
     lane = jnp.arange(2 * width, dtype=jnp.int32)[None, :]
     scale = jnp.where(lane < width, 1.0, slot_gate[:, None])
     send = (picked * scale).astype(jnp.bfloat16).reshape(half_experts, 2 * slots, 2 * width)
+    send = jnp.where(all_counts[0, 0] >= 0, send, jnp.zeros((), send.dtype))
     got = lax.all_to_all(send, "inner", split_axis=0, concat_axis=0, tiled=True)
     got = got.reshape(n_in, local_experts, 2, slots, 2 * width)
 

time: 359 us -> 362 us (level)
  blocking collectives: 90.6 us -> 36.3 us
  waiting for transfers between devices: 154 us -> 197 us
  starting transfers between devices: 23.7 us -> 35.7 us
    psum x1 -> x0, blocking collectives: 90.6 us -> none  [on_device(): all_counts = lax.psum(count_rows, ('half', 'inner'))]
    all_to_all x1, waiting for transfers between devices: 0.01 us -> 82.2 us  [on_device(): got = lax.all_to_all(send, 'inner', split_axis=0, concat_axis=0, tiled=True)]
    ppermute x7, waiting for transfers between devices: 83.8 us -> 46 us  [shifted(): lax.ppermute(value, axis, [(j, (j + shift) % count) for j in range(count)])]
    all_gather x0 -> x1, blocking collectives: none -> 36.3 us  [on_device(): all_counts = lax.all_gather(counts, ('half', 'inner'))]
    all_to_all x1, starting transfers between devices: 5.13 us -> 16.8 us  [on_device(): got = lax.all_to_all(send, 'inner', split_axis=0, concat_axis=0, tiled=True)]
    unnamed x42 -> x38, local copies, waits for them, and re-layouts: 7.68 us -> 7.68 us
  transfers between devices with their start and end apart: 9 -> 9, of which waited for: 3 -> 4; matrix products, arithmetic and copies ran while one was open for 14% -> 14% of each run, Pallas kernels for 0% -> 0%
where the time goes in v6:
time: 362 us; the launch traced here: 361 us
  waiting for transfers between devices  197 us (54%)
  matrix products  46.6 us (13%)
  blocking collectives  36.3 us (10%)
  starting transfers between devices  35.7 us (10%)
  other arithmetic  26.4 us (7%)
  local copies, waits for them, and re-layouts  17.3 us (5%)
    all_to_all x1, waiting for transfers between devices, on_device(): got = lax.all_to_all(send, 'inner', split_axis=0, concat_axis=0, tiled=True)  82.2 us
    all_to_all x1, waiting for transfers between devices, on_device(): lax.all_to_all(back, 'inner', split_axis=0, concat_axis=0, tiled=True)  68.8 us
    ppermute x7, waiting for transfers between devices, shifted(): lax.ppermute(value, axis, [(j, (j + shift) % count) for j in range(count)])  46 us
    all_gather x1, blocking collectives, on_device(): all_counts = lax.all_gather(counts, ('half', 'inner'))  36.3 us
    all_to_all x1, starting transfers between devices, on_device(): got = lax.all_to_all(send, 'inner', split_axis=0, concat_axis=0, tiled=True)  16.8 us
    ppermute x7, starting transfers between devices, shifted(): lax.ppermute(value, axis, [(j, (j + shift) % count) for j in range(count)])  13.7 us
    unnamed x38, local copies, waits for them, and re-layouts  7.68 us
  transfers between devices with their start and end apart: 9, of which 4 were waited for; matrix products, arithmetic and copies ran while one was open for 14% of the time, Pallas kernels for 0%

profile of v6, /device:TPU:0, one launch (start us, length us, event | category | flops | bytes accessed | tf_op | source)
XLA Modules:
  0.0 361.0 jit_solution(5562804122494176741)
XLA Ops:
  0.6 4.1 %collective-permute-start.1 = (f32[128,6]{0,1:T(8,128)}, f32[128,6]{0,1:T(8,128)S(1)}, u32[]{:S(2)}, u32[]{:S(2)}) collective-permute-start(f32[128,6]{0,1:T(8,128)} %param.11), channel_id=1, source_target_pairs={{0,16},{16,0},{1,17},{17,1},{2,18},{18,2},{3,19},{19,3},{4,20},{20... | collective-permute-start | bytes 9224 | tf_op jit(solution)/shard_map/ppermute | solution.py:10
  5.8 1.7 reduce-window.6
  11.0 3.0 collective-permute-start.2
  15.0 36.3 %all-gather = s32[16,1,16]{2,1,0:T(1,128)S(1)} all-gather(s32[1,1,16]{2,1,0:T(1,128)S(1)} %bitcast.103), channel_id=1, replica_groups=mesh['half'=2,'inner'=8,'dp'=2] {'half','inner'}, dimensions={0}, use_global_device_ids=true | all-gather | bytes 1088 | tf_op jit(solution)/shard_map/all_gather | solution.py:48
  54.2 5.0 %collective-permute-done.2 = bf16[128,4096]{1,0:T(8,128)(2,1)S(1)} collective-permute-done((bf16[128,4096]{1,0:T(8,128)(2,1)S(1)}, bf16[128,4096]{1,0:T(8,128)(2,1)S(1)}, u32[]{:S(2)}, u32[]{:S(2)}) %collective-permute-start.2) | collective-permute-done | bytes 1048608 | tf_op jit(solution)/shard_map/ppermute | solution.py:10
  59.2 4.3 %broadcast_select_fusion = bf16[960,4096]{1,0:T(8,128)(2,1)} fusion(pred[]{:T(512)} %bitcast.9, f32[960]{0:T(1024)S(1)} %select_reduce_fusion.1, pred[4096]{0:T(1024)(128)(4,1)S(1)} %iota_compare_fusion.4, pred[960,256]{1,0:T(8,128)(4,1)S(1)} %fusion, bf16[128,4096]{1,0:T(8,128)(2,1)S(1)} %collective-permute-done.2, ...), kind=kOutput, calls=%fused_computation.6 | convolution fusion | flops 2033188864 | bytes 10215169 | tf_op jit(solution)/shard_map/dot_general | solution.py:64
  63.5 16.8 %all-to-all-start = ((bf16[8,120,4096]{2,1,0:T(8,128)(2,1)}), bf16[8,120,4096]{2,1,0:T(8,128)(2,1)}, u32[]{:S(2)}, u32[]{:S(2)}) async-start(bf16[8,120,4096]{2,1,0:T(8,128)(2,1)} %bitcast.91), calls=%async_computation | async-start | bytes 15728640 | tf_op jit(solution)/shard_map/all_to_all | solution.py:69
  81.7 1.5 collective-permute-start.3
  85.7 82.2 %all-to-all-done = bf16[8,120,4096]{2,1,0:T(8,128)(2,1)} async-done(((bf16[8,120,4096]{2,1,0:T(8,128)(2,1)}), bf16[8,120,4096]{2,1,0:T(8,128)(2,1)}, u32[]{:S(2)}, u32[]{:S(2)}) %all-to-all-start) | async-done | bytes 7864352 | tf_op jit(solution)/shard_map/all_to_all | solution.py:69
  167.9 6.9 %bitcast_select_fusion = bf16[1,960,4096]{2,1,0:T(8,128)(2,1)} fusion(pred[960]{0:T(1024)(128)(4,1)S(1)} %lt.72, bf16[1,960,4096]{2,1,0:T(8,128)(2,1)} %bitcast.86), kind=kLoop, calls=%fused_computation.4 | loop fusion | flops 3932160 | bytes 15729600 | tf_op jit(solution)/shard_map/jit(_where)/select_n | solution.py:80
  174.8 4.7 %fusion.3 = f32[960,384]{1,0:T(8,128)S(1)} fusion(bf16[1,960,4096]{2,1,0:T(8,128)(2,1)} %bitcast_select_fusion, bf16[3,192,2048]{2,1,0:T(8,128)(2,1)} %collective-permute-done.3, bf16[3,192,2048]{2,1,0:T(8,128)(2,1)S(1)} %constant_dynamic-update-slice_fusion.4), kind=kOutput, calls=%fused_computation.25 | convolution fusion | flops 1513095168 | bytes 10125312 | tf_op jit(solution)/shard_map/erd,efd->erf/dot_general | solution.py:101
  179.4 3.3 fusion.6
  182.8 3.8 %multiply_convert_fusion.3 = (bf16[960,384]{1,0:T(8,128)(2,1)S(1)}, bf16[960,384]{1,0:T(8,128)(2,1)S(1)}, bf16[960,384]{1,0:T(8,128)(2,1)S(1)}) fusion(f32[960,384]{1,0:T(8,128)S(1)} %fusion.6, f32[960,384]{1,0:T(8,128)S(1)} %fusion.3, bf16[3,192,2048]{2,1,0:T(8,128)(2,1)S(1)} %constant_dynamic-update-slice_fusion.4, ...), kind=kOutput, calls=%fused_computation.50 | convolution fusion | flops 1518256128 | bytes 13811712 | tf_op jit(solution)/shard_map/erd,efd->erf/dot_general | solution.py:94
  186.6 5.7 %convolution_convert_fusion = bf16[960,2048]{1,0:T(8,128)(2,1)} fusion(bf16[960,384]{1,0:T(8,128)(2,1)S(1)} %get-tuple-element.33, bf16[3,192,2048]{2,1,0:T(8,128)(2,1)} %collective-permute-done.3, bf16[3,192,2048]{2,1,0:T(8,128)(2,1)S(1)} %constant_dynamic-update-slice_fusion.4), kind=kOutput, calls=%fused_computation.23 | convolution fusion | flops 1515061248 | bytes 9388032 | tf_op jit(solution)/shard_map/erf,efd->erd/dot_general | solution.py:98
  192.4 3.3 fusion.43
  195.7 3.4 add_convert_fusion
  199.1 5.9 %maximum_bitcast_fusion = bf16[8,2,120,2048]{3,2,1,0:T(8,128)(2,1)} fusion(bf16[1,1,8,120,2048]{4,3,1,2,0:T(8,128)(2,1)S(1)} %bitcast.90, bf16[1,1,8,120,2048]{4,3,1,2,0:T(8,128)(2,1)} %bitcast.95), kind=kLoop, calls=%fused_computation.3 | loop fusion | flops 3932160 | bytes 15728640 | tf_op jit(solution)/shard_map/reshape | solution.py:116
  205.0 5.3 %all-to-all-start.1 = ((bf16[8,2,120,2048]{3,2,1,0:T(8,128)(2,1)}), bf16[8,2,120,2048]{3,2,1,0:T(8,128)(2,1)}, u32[]{:S(2)}, u32[]{:S(2)}) async-start(bf16[8,2,120,2048]{3,2,1,0:T(8,128)(2,1)} %maximum_bitcast_fusion), calls=%async_computation.1 | async-start | bytes 15728640 | tf_op jit(solution)/shard_map/all_to_all | solution.py:117
  210.3 4.0 %fusion.4 = f32[1,384,2048]{2,1,0:T(8,128)S(1)} fusion(bf16[960,384]{1,0:T(8,128)(2,1)S(1)} %copy-done.12, bf16[1,960,4096]{2,1,0:T(8,128)(2,1)} %bitcast_select_fusion), kind=kOutput, calls=%fused_computation.26 | convolution fusion | flops 1509949440 | bytes 7815168 | tf_op jit(solution)/shard_map/erf,erd->efd/dot_general | solution.py:110
  214.3 4.0 %convolution_bitcast_fusion.1 = f32[1,384,2048]{2,1,0:T(8,128)S(1)} fusion(bf16[960,384]{1,0:T(8,128)(2,1)S(1)} %get-tuple-element.34, bf16[1,960,4096]{2,1,0:T(8,128)(2,1)} %bitcast_select_fusion), kind=kOutput, calls=%fused_computation.28 | convolution fusion | flops 1509949440 | bytes 7815168 | tf_op jit(solution)/shard_map/erf,erd->efd/dot_general | solution.py:111
  218.3 4.0 %convolution_bitcast_fusion = f32[1,384,2048]{2,1,0:T(8,128)S(1)} fusion(bf16[960,384]{1,0:T(8,128)(2,1)S(1)} %copy-done.3, bf16[1,960,4096]{2,1,0:T(8,128)(2,1)} %bitcast_select_fusion), kind=kOutput, calls=%fused_computation.27 | convolution fusion | flops 1509949440 | bytes 7815168 | tf_op jit(solution)/shard_map/erf,erd->efd/dot_general | solution.py:112
  223.5 3.6 %copy-done = f32[3,384,2048]{2,1,0:T(8,128)} copy-done((f32[3,384,2048]{2,1,0:T(8,128)}, f32[3,384,2048]{2,1,0:T(8,128)S(1)}, u32[]{:S(2)}) %copy-start) | copy-done | bytes 9437208
  227.5 1.5 collective-permute-start.6
  229.0 68.8 %all-to-all-done.1 = bf16[8,2,120,2048]{3,2,1,0:T(8,128)(2,1)} async-done(((bf16[8,2,120,2048]{3,2,1,0:T(8,128)(2,1)}), bf16[8,2,120,2048]{3,2,1,0:T(8,128)(2,1)}, u32[]{:S(2)}, u32[]{:S(2)}) %all-to-all-start.1) | async-done | bytes 7864352 | tf_op jit(solution)/shard_map/all_to_all | solution.py:117
  297.8 3.7 %fusion.46 = (bf16[8,1,120,2048]{3,2,1,0:T(8,128)(2,1)S(1)}, bf16[8,1,120,2048]{3,2,1,0:T(8,128)(2,1)S(1)}) fusion(bf16[8,2,120,2048]{3,2,1,0:T(8,128)(2,1)} %all-to-all-done.1), kind=kLoop, calls=%fused_computation.106 | loop fusion | bytes 15728640 | tf_op jit(solution)/shard_map/slice | solution.py:130
  302.8 1.9 select_reduce_fusion
  304.7 1.3 fusion.49
  306.2 3.6 fusion.15
  310.6 3.1 collective-permute-start.4
  313.7 2.6 fusion.1
  316.7 1.4 fusion.47
  318.2 41.0 %collective-permute-done.5 = f32[128,6]{0,1:T(8,128)S(1)} collective-permute-done((f32[128,6]{0,1:T(8,128)S(1)}, f32[128,6]{0,1:T(8,128)S(1)}, u32[]{:S(2)}, u32[]{:S(2)}) %collective-permute-start.5) | collective-permute-done | bytes 3104 | tf_op jit(solution)/shard_map/ppermute | solution.py:10
  (89 shorter events, 17.6 us)
Async XLA Ops:
  0.6 51.8 %collective-permute-start.1 = (f32[128,6]{0,1:T(8,128)}, f32[128,6]{0,1:T(8,128)S(1)}, u32[]{:S(2)}, u32[]{:S(2)}) collective-permute-start(f32[128,6]{0,1:T(8,128)} %param.11), channel_id=1, source_target_pairs={{0,16},{16,0},{1,17},{17,1},{2,18},{18,2},{3,19},{19,3},{4,20},{20... | collective-permute-start | bytes 9224 | tf_op jit(solution)/shard_map/ppermute | solution.py:10
  8.8 43.6 %collective-permute-start = (s32[128,6]{0,1:T(8,128)S(1)}, s32[128,6]{0,1:T(8,128)S(1)}, u32[]{:S(2)}, u32[]{:S(2)}) collective-permute-start(s32[128,6]{0,1:T(8,128)S(1)} %multiply_add_fusion), channel_id=1, source_target_pairs={{0,16},{16,0},{1,17},{17,1},{2,18},{18,2},{3,19},{19,3},{4,20},{20... | collective-permute-start | bytes 9224 | tf_op jit(solution)/shard_map/ppermute | solution.py:10
  11.0 52.5 %copy-start.6 = (bf16[128,4096]{1,0:T(8,128)(2,1)}, bf16[128,4096]{1,0:T(8,128)(2,1)S(1)}, u32[]{:S(2)}) copy-start(bf16[128,4096]{1,0:T(8,128)(2,1)S(1)} %constant_dynamic-update-slice_fusion.2) | copy-start | bytes 3145732
  11.0 48.1 %collective-permute-start.2 = (bf16[128,4096]{1,0:T(8,128)(2,1)S(1)}, bf16[128,4096]{1,0:T(8,128)(2,1)S(1)}, u32[]{:S(2)}, u32[]{:S(2)}) collective-permute-start(bf16[128,4096]{1,0:T(8,128)(2,1)S(1)} %constant_dynamic-update-slice_fusion.2), channel_id=1, source_target_pairs={{0,16},{16,0},{1,17},{17,1},{2,18},{18,2},{3,19},{19,3},{4,20},{20... | collective-permute-start | bytes 3145736 | tf_op jit(solution)/shard_map/ppermute | solution.py:10
  59.2 4.3 %copy-start.8 = (bf16[128,4096]{1,0:T(8,128)(2,1)}, bf16[128,4096]{1,0:T(8,128)(2,1)S(1)}, u32[]{:S(2)}) copy-start(bf16[128,4096]{1,0:T(8,128)(2,1)S(1)} %collective-permute-done.2) | copy-start | bytes 3145732
  63.5 16.8 %copy-start.4 = (bf16[1,192,2048]{2,1,0:T(8,128)(2,1)S(1)}, bf16[1,192,2048]{2,1,0:T(8,128)(2,1)}, u32[]{:S(2)}) copy-start(bf16[1,192,2048]{2,1,0:T(8,128)(2,1)} %param.13) | copy-start | bytes 2359300
  63.5 104.4 %all-to-all-start = ((bf16[8,120,4096]{2,1,0:T(8,128)(2,1)}), bf16[8,120,4096]{2,1,0:T(8,128)(2,1)}, u32[]{:S(2)}, u32[]{:S(2)}) async-start(bf16[8,120,4096]{2,1,0:T(8,128)(2,1)} %bitcast.91), calls=%async_computation | async-start | bytes 15728640 | tf_op jit(solution)/shard_map/all_to_all | solution.py:69
  80.3 1.4 copy-start.5
  80.3 3.2 copy-start.10
  81.7 93.1 %collective-permute-start.3 = (bf16[3,192,2048]{2,1,0:T(8,128)(2,1)S(1)}, bf16[3,192,2048]{2,1,0:T(8,128)(2,1)}, u32[]{:S(2)}, u32[]{:S(2)}) collective-permute-start(bf16[3,192,2048]{2,1,0:T(8,128)(2,1)S(1)} %constant_dynamic-update-slice_fusion.4), channel_id=1, source_target_pairs={{0,1},{1,0},{2,3},{3,2},{4,5},{5,4},{6,7},{7,6},{8,9},{9,8},{10,11... | collective-permute-start | bytes 7077896 | tf_op jit(solution)/shard_map/ppermute | solution.py:10
  174.7 4.7 %copy-start.1 = (bf16[1,960,4096]{2,1,0:T(8,128)(2,1)S(1)}, bf16[1,960,4096]{2,1,0:T(8,128)(2,1)}, u32[]{:S(2)}) copy-start(bf16[1,960,4096]{2,1,0:T(8,128)(2,1)} %bitcast_select_fusion) | copy-start | bytes 23592964
  186.6 5.8 %copy-start.11 = (bf16[960,384]{1,0:T(8,128)(2,1)}, bf16[960,384]{1,0:T(8,128)(2,1)S(1)}, u32[]{:S(2)}) copy-start(bf16[960,384]{1,0:T(8,128)(2,1)S(1)} %get-tuple-element.33) | copy-start | bytes 2211844
  186.6 5.8 %copy-start.2 = (bf16[960,384]{1,0:T(8,128)(2,1)}, bf16[960,384]{1,0:T(8,128)(2,1)S(1)}, u32[]{:S(2)}) copy-start(bf16[960,384]{1,0:T(8,128)(2,1)S(1)} %get-tuple-element.35) | copy-start | bytes 2211844
  205.0 5.3 %copy-start.12 = (bf16[960,384]{1,0:T(8,128)(2,1)S(1)}, bf16[960,384]{1,0:T(8,128)(2,1)}, u32[]{:S(2)}) copy-start(bf16[960,384]{1,0:T(8,128)(2,1)} %copy-done.11) | copy-start | bytes 2211844
  205.0 92.8 %all-to-all-start.1 = ((bf16[8,2,120,2048]{3,2,1,0:T(8,128)(2,1)}), bf16[8,2,120,2048]{3,2,1,0:T(8,128)(2,1)}, u32[]{:S(2)}, u32[]{:S(2)}) async-start(bf16[8,2,120,2048]{3,2,1,0:T(8,128)(2,1)} %maximum_bitcast_fusion), calls=%async_computation.1 | async-start | bytes 15728640 | tf_op jit(solution)/shard_map/all_to_all | solution.py:117
  214.3 4.0 %copy-start.3 = (bf16[960,384]{1,0:T(8,128)(2,1)S(1)}, bf16[960,384]{1,0:T(8,128)(2,1)}, u32[]{:S(2)}) copy-start(bf16[960,384]{1,0:T(8,128)(2,1)} %copy-done.2) | copy-start | bytes 2211844
  223.5 3.6 %copy-start = (f32[3,384,2048]{2,1,0:T(8,128)}, f32[3,384,2048]{2,1,0:T(8,128)S(1)}, u32[]{:S(2)}) copy-start(f32[3,384,2048]{2,1,0:T(8,128)S(1)} %pad_maximum_fusion) | copy-start | bytes 28311556
  227.4 74.1 %copy-start.7 = (bf16[128,4096]{1,0:T(8,128)(2,1)S(1)}, bf16[128,4096]{1,0:T(8,128)(2,1)}, u32[]{:S(2)}) copy-start(bf16[128,4096]{1,0:T(8,128)(2,1)} %copy-done.6) | copy-start | bytes 3145732
  227.5 86.2 %collective-permute-start.6 = (bf16[3,192,2048]{2,1,0:T(8,128)(2,1)S(1)}, bf16[3,192,2048]{2,1,0:T(8,128)(2,1)}, u32[]{:S(2)}, u32[]{:S(2)}) collective-permute-start(bf16[3,192,2048]{2,1,0:T(8,128)(2,1)S(1)} %slice.214), channel_id=1, source_target_pairs={{0,1},{1,0},{2,3},{3,2},{4,5},{5,4},{6,7},{7,6},{8,9},{9,8},{10,11... | collective-permute-start | bytes 7077896 | tf_op jit(solution)/shard_map/ppermute | solution.py:10
  297.8 3.7 %copy-start.9 = (bf16[128,4096]{1,0:T(8,128)(2,1)S(1)}, bf16[128,4096]{1,0:T(8,128)(2,1)}, u32[]{:S(2)}) copy-start(bf16[128,4096]{1,0:T(8,128)(2,1)} %copy-done.8) | copy-start | bytes 3145732
  306.2 7.5 %slice-start = ((s8[9437184]{0:T(1024)(128)(4,1)}), s8[4194304]{0:T(1024)(128)(4,1)S(1)}, s32[]{:S(2)}) async-start(s8[9437184]{0:T(1024)(128)(4,1)} %bitcast.88), calls=%async_computation.2 | async-start | bytes 8388608
  306.2 7.5 %slice-start.1 = ((s8[9437184]{0:T(1024)(128)(4,1)}), s8[4194304]{0:T(1024)(128)(4,1)S(1)}, s32[]{:S(2)}) async-start(s8[9437184]{0:T(1024)(128)(4,1)} %bitcast.88), calls=%async_computation.3 | async-start | bytes 8388608
  309.8 3.9 %slice-start.2 = ((s8[9437184]{0:T(1024)(128)(4,1)}), s8[1048576]{0:T(1024)(128)(4,1)S(1)}, s32[]{:S(2)}) async-start(s8[9437184]{0:T(1024)(128)(4,1)} %bitcast.88), calls=%async_computation.4 | async-start | bytes 2097152
  310.6 49.2 %collective-permute-start.4 = (bf16[128,4096]{1,0:T(8,128)(2,1)S(1)}, bf16[128,4096]{1,0:T(8,128)(2,1)S(1)}, u32[]{:S(2)}, u32[]{:S(2)}) collective-permute-start(bf16[128,4096]{1,0:T(8,128)(2,1)S(1)} %pad_maximum_fusion.2), channel_id=1, source_target_pairs={{0,16},{16,0},{1,17},{17,1},{2,18},{18,2},{3,19},{19,3},{4,20},{20... | collective-permute-start | bytes 3145736 | tf_op jit(solution)/shard_map/ppermute | solution.py:10
  316.3 42.9 %collective-permute-start.5 = (f32[128,6]{0,1:T(8,128)S(1)}, f32[128,6]{0,1:T(8,128)S(1)}, u32[]{:S(2)}, u32[]{:S(2)}) collective-permute-start(f32[128,6]{0,1:T(8,128)S(1)} %slice.152), channel_id=1, source_target_pairs={{0,16},{16,0},{1,17},{17,1},{2,18},{18,2},{3,19},{19,3},{4,20},{20... | collective-permute-start | bytes 9224 | tf_op jit(solution)/shard_map/ppermute | solution.py:10

commit v7 on v5

--- a/solution.py
+++ b/solution.py
@@ -111,9 +111,12 @@
     part_gate = jnp.einsum("erf,erd->efd", d_gate, rows_in, preferred_element_type=jnp.float32)
     part_up = jnp.einsum("erf,erd->efd", d_up, rows_in, preferred_element_type=jnp.float32)
 
-    back = jnp.stack([out_rows, dx_rows], axis=1)
-    back = back.reshape(local_experts, 2, n_in, 2 * slots, width).transpose(2, 0, 1, 3, 4)
-    back = back.reshape(half_experts, 2, 2 * slots, width)
+    back = jnp.concatenate([out_rows, dx_rows], axis=-1)
+    if local_experts == 1:
+        back = back.reshape(half_experts, 2 * slots, 2 * width)
+    else:
+        back = back.reshape(local_experts, n_in, 2 * slots, 2 * width).transpose(1, 0, 2, 3)
+        back = back.reshape(half_experts, 2 * slots, 2 * width)
     back = lax.all_to_all(back, "inner", split_axis=0, concat_axis=0, tiled=True)
 
     parts = jnp.concatenate([part_gate, part_up, part_down], axis=0)
@@ -126,28 +129,32 @@
     grad_up_w = summed[local_experts : 2 * local_experts]
     grad_down_w = summed[2 * local_experts :]
 
-    out_part = back[:, 0].reshape(2 * half_rows, width)
-    dx_part = back[:, 1].reshape(2 * half_rows, width)
-    hit = dest[:, :, None] == jnp.arange(2 * half_rows, dtype=jnp.int32)[None, None, :]
-    weight = jnp.sum(jnp.where(hit, all_gates[:, :, None], 0.0), axis=1)
-    ones = jnp.sum(hit.astype(jnp.float32), axis=1).astype(jnp.bfloat16)
-    layer = jnp.dot(in_three(weight), out_part, preferred_element_type=jnp.float32)
-    n_all = 2 * tok_rows
-    layer = layer[:n_all] + layer[n_all : 2 * n_all] + layer[2 * n_all :]
-    grads = jnp.dot(ones, dx_part, preferred_element_type=jnp.float32)
-    scores = jnp.dot(all_rows[:, width:], out_part.T, preferred_element_type=jnp.float32)
-    gg = jnp.sum(jnp.where(hit, scores[:, None, :], 0.0), axis=2)
+    back = back.reshape(2 * half_rows, 2 * width)
+    out_part = back[:, :width]
+    dx_part = back[:, width:]
+    columns = jnp.arange(2 * half_rows, dtype=jnp.int32)
 
+    def combine(which):
+        rows = slice(which * tok_rows, (which + 1) * tok_rows)
+        hit = dest[rows][:, :, None] == columns[None, None, :]
+        weight = jnp.sum(jnp.where(hit, all_gates[rows][:, :, None], 0.0), axis=1)
+        ones = jnp.sum(hit.astype(jnp.float32), axis=1).astype(jnp.bfloat16)
+        layer = jnp.dot(in_three(weight), out_part, preferred_element_type=jnp.float32)
+        layer = layer[:tok_rows] + layer[tok_rows : 2 * tok_rows] + layer[2 * tok_rows :]
+        grads = jnp.dot(ones, dx_part, preferred_element_type=jnp.float32)
+        scores = jnp.dot(all_rows[rows, width:], out_part.T, preferred_element_type=jnp.float32)
+        gg = jnp.sum(jnp.where(hit, scores[:, None, :], 0.0), axis=2)
+        return layer, grads, gg
+
+    partner_layer, partner_grads, partner_gg = combine(1)
     returned = shifted(
-        jnp.concatenate([layer[tok_rows:], grads[tok_rows:]], axis=1).astype(jnp.bfloat16),
-        "half",
-        2,
-        1,
+        jnp.concatenate([partner_layer, partner_grads], axis=1).astype(jnp.bfloat16), "half", 2, 1
     )
-    returned_gg = shifted(gg[tok_rows:], "half", 2, 1)
-    layer_out = (layer[:tok_rows] + returned[:, :width].astype(jnp.float32)).astype(jnp.bfloat16)
-    grad_tokens = (grads[:tok_rows] + returned[:, width:].astype(jnp.float32)).astype(jnp.bfloat16)
-    grad_gates = gg[:tok_rows] + returned_gg
+    returned_gg = shifted(partner_gg, "half", 2, 1)
+    own_layer, own_grads, own_gg = combine(0)
+    layer_out = (own_layer + returned[:, :width].astype(jnp.float32)).astype(jnp.bfloat16)
+    grad_tokens = (own_grads + returned[:, width:].astype(jnp.float32)).astype(jnp.bfloat16)
+    grad_gates = own_gg + returned_gg
     return (layer_out, grad_tokens, grad_gates, grad_gate_w, grad_up_w, grad_down_w)
 
 

time: 359 us -> 360 us (level)
  matrix products: 44.8 us -> 61.6 us
  local copies, waits for them, and re-layouts: 16.8 us -> 8.67 us
  waiting for transfers between devices: 154 us -> 149 us
    all_to_all x1, waiting for transfers between devices: 70.4 us -> 19.9 us  [on_device(): lax.all_to_all(back, 'inner', split_axis=0, concat_axis=0, tiled=True)]
    ppermute x7, waiting for transfers between devices: 83.8 us -> 129 us  [shifted(): lax.ppermute(value, axis, [(j, (j + shift) % count) for j in range(count)])]
    dot_general x3 -> x6, matrix products: 6.07 us -> 21 us  [the longest x2 7.92 us: combine(): jnp.dot(in_three(weight), out_part, preferred_element_type=jnp.float32)]
    concatenate x1 -> x3, other arithmetic: 0.07 us -> 8.17 us  [the longest x1 7.39 us: on_device(): back = jnp.concatenate([out_rows, dx_rows], axis=-1)]
    reshape x1 -> x0, other arithmetic: 5.94 us -> none  [on_device(): back = back.reshape(half_experts, 2, 2 * slots, width)]
    unnamed x42 -> x33, local copies, waits for them, and re-layouts: 7.68 us -> 3.37 us
    slice x5 -> x2, local copies, waits for them, and re-layouts: 4.07 us -> 0.25 us  [the longest x1 3.7 us: on_device(): dx_part = back[:, 1].reshape(2 * half_rows, width)]
  transfers between devices with their start and end apart: 9 -> 9, of which waited for: 3 -> 4; matrix products, arithmetic and copies ran while one was open for 14% -> 12% of each run, Pallas kernels for 0% -> 0%
where the time goes in v7:
time: 360 us; the launch traced here: 359 us
  waiting for transfers between devices  149 us (41%)
  blocking collectives  88.6 us (25%)
  matrix products  61.6 us (17%)
  other arithmetic  26.2 us (7%)
  starting transfers between devices  24.7 us (7%)
  local copies, waits for them, and re-layouts  8.67 us (2%)
    ppermute x7, waiting for transfers between devices, shifted(): lax.ppermute(value, axis, [(j, (j + shift) % count) for j in range(count)])  129 us
    psum x1, blocking collectives, on_device(): all_counts = lax.psum(count_rows, ('half', 'inner'))  88.6 us
    all_to_all x1, waiting for transfers between devices, on_device(): lax.all_to_all(back, 'inner', split_axis=0, concat_axis=0, tiled=True)  19.9 us
    ppermute x7, starting transfers between devices, shifted(): lax.ppermute(value, axis, [(j, (j + shift) % count) for j in range(count)])  14.4 us
    dot_general x2, matrix products, combine(): jnp.dot(in_three(weight), out_part, preferred_element_type=jnp.float32)  7.92 us
    concatenate x1, other arithmetic, on_device(): back = jnp.concatenate([out_rows, dx_rows], axis=-1)  7.39 us
  transfers between devices with their start and end apart: 9, of which 4 were waited for; matrix products, arithmetic and copies ran while one was open for 12% of the time, Pallas kernels for 0%

profile of v7, /device:TPU:0, one launch (start us, length us, event | category | flops | bytes accessed | tf_op | source)
XLA Modules:
  0.0 359.4 jit_solution(4669083174209403513)
XLA Ops:
  0.6 4.1 %collective-permute-start.2 = (f32[128,6]{0,1:T(8,128)}, f32[128,6]{0,1:T(8,128)S(1)}, u32[]{:S(2)}, u32[]{:S(2)}) collective-permute-start(f32[128,6]{0,1:T(8,128)} %param.11), channel_id=1, source_target_pairs={{0,16},{16,0},{1,17},{17,1},{2,18},{18,2},{3,19},{19,3},{4,20},{20... | collective-permute-start | bytes 9224 | tf_op jit(solution)/shard_map/ppermute | solution.py:10
  8.1 1.7 reduce-window.6
  11.1 2.9 collective-permute-start
  14.7 40.4 %collective-permute-done = s32[128,6]{0,1:T(8,128)S(1)} collective-permute-done((s32[128,6]{0,1:T(8,128)S(1)}, s32[128,6]{0,1:T(8,128)S(1)}, u32[]{:S(2)}, u32[]{:S(2)}) %collective-permute-start) | collective-permute-done | bytes 3104 | tf_op jit(solution)/shard_map/ppermute | solution.py:10
  56.8 4.4 %multiply_convert_fusion = bf16[960,4096]{1,0:T(8,128)(2,1)} fusion(pred[960,256]{1,0:T(8,128)(4,1)S(1)} %fusion, f32[960]{0:T(1024)S(1)} %select_reduce_fusion, pred[4096]{0:T(1024)(128)(4,1)S(1)} %iota_compare_fusion.5, bf16[128,4096]{1,0:T(8,128)(2,1)S(1)} %collective-permute-done.1, bf16[128,4096]{1,0:T(8,128)(2,1)S(1)} %constant_dynamic-update-slice_fusion), kind=kOutput, calls=%fused_computation.1 | convolution fusion | flops 2029256704 | bytes 10215168 | tf_op jit(solution)/shard_map/dot_general | solution.py:65
  61.2 5.0 %all-to-all-start = ((bf16[8,120,4096]{2,1,0:T(8,128)(2,1)}), bf16[8,120,4096]{2,1,0:T(8,128)(2,1)}, u32[]{:S(2)}, u32[]{:S(2)}) async-start(bf16[8,120,4096]{2,1,0:T(8,128)(2,1)} %bitcast.78), calls=%async_computation | async-start | bytes 15728640 | tf_op jit(solution)/shard_map/all_to_all | solution.py:69
  67.7 1.6 collective-permute-start.3
  69.8 88.6 %psum.7 = s32[16,16]{1,0:T(8,128)S(1)} all-reduce(s32[16,16]{1,0:T(8,128)S(1)} %broadcast_select_fusion), channel_id=1, replica_groups=mesh['half'=2,'inner'=8,'dp'=2] {'half','inner'}, use_global_device_ids=true, to_apply=%region_4.5 | all-reduce | flops 256 | bytes 2048 | tf_op jit(solution)/shard_map/psum | solution.py:49
  160.6 6.9 %bitcast_select_fusion = bf16[1,960,4096]{2,1,0:T(8,128)(2,1)} fusion(pred[960]{0:T(1024)(128)(4,1)S(1)} %lt.68, bf16[1,960,4096]{2,1,0:T(8,128)(2,1)} %bitcast.75), kind=kLoop, calls=%fused_computation.4 | loop fusion | flops 3932160 | bytes 15729600 | tf_op jit(solution)/shard_map/jit(_where)/select_n | solution.py:80
  167.6 4.7 %fusion.3 = f32[960,384]{1,0:T(8,128)S(1)} fusion(bf16[1,960,4096]{2,1,0:T(8,128)(2,1)} %bitcast_select_fusion, bf16[3,192,2048]{2,1,0:T(8,128)(2,1)} %collective-permute-done.3, bf16[3,192,2048]{2,1,0:T(8,128)(2,1)S(1)} %constant_dynamic-update-slice_fusion.2), kind=kOutput, calls=%fused_computation.20 | convolution fusion | flops 1513095168 | bytes 10125312 | tf_op jit(solution)/shard_map/erd,efd->erf/dot_general | solution.py:101
  172.3 3.3 fusion.10
  175.6 3.8 %multiply_convert_fusion.3 = (bf16[960,384]{1,0:T(8,128)(2,1)S(1)}, bf16[960,384]{1,0:T(8,128)(2,1)S(1)}, bf16[960,384]{1,0:T(8,128)(2,1)S(1)}) fusion(f32[960,384]{1,0:T(8,128)S(1)} %fusion.10, f32[960,384]{1,0:T(8,128)S(1)} %fusion.3, bf16[3,192,2048]{2,1,0:T(8,128)(2,1)S(1)} %constant_dynamic-update-slice_fusion.2, ...), kind=kOutput, calls=%fused_computation.58 | convolution fusion | flops 1518256128 | bytes 13811712 | tf_op jit(solution)/shard_map/erd,efd->erf/dot_general | solution.py:94
  179.4 5.8 %convolution_convert_fusion = bf16[960,2048]{1,0:T(8,128)(2,1)} fusion(bf16[960,384]{1,0:T(8,128)(2,1)S(1)} %get-tuple-element.34, bf16[3,192,2048]{2,1,0:T(8,128)(2,1)} %collective-permute-done.3, bf16[3,192,2048]{2,1,0:T(8,128)(2,1)S(1)} %constant_dynamic-update-slice_fusion.2), kind=kOutput, calls=%fused_computation.18 | convolution fusion | flops 1515061248 | bytes 9388032 | tf_op jit(solution)/shard_map/erf,efd->erd/dot_general | solution.py:98
  185.2 3.3 fusion.68
  188.6 5.3 %add_convert_fusion = bf16[960,2048]{1,0:T(8,128)(2,1)} fusion(f32[960,2048]{1,0:T(8,128)S(1)} %fusion.68, bf16[960,384]{1,0:T(8,128)(2,1)S(1)} %get-tuple-element.35, bf16[3,192,2048]{2,1,0:T(8,128)(2,1)S(1)} %constant_dynamic-update-slice_fusion.2, bf16[3,192,2048]{2,1,0:T(8,128)(2,1)} %collective-permute-done.3), kind=kOutput, calls=%fused_computation.5 | convolution fusion | flops 1517027328 | bytes 17252352 | tf_op jit(solution)/shard_map/erf,efd->erd/dot_general | solution.py:106
  193.8 7.4 %pad_maximum_fusion.1 = bf16[8,120,4096]{2,1,0:T(8,128)(2,1)} fusion(bf16[8,120,2048]{2,1,0:T(8,128)(2,1)} %bitcast.77, bf16[8,120,2048]{2,1,0:T(8,128)(2,1)} %bitcast.81), kind=kLoop, calls=%fused_computation.3 | loop fusion | flops 15728640 | bytes 15728640 | tf_op jit(solution)/shard_map/concatenate | solution.py:114
  201.2 5.3 %all-to-all-start.1 = ((bf16[8,120,4096]{2,1,0:T(8,128)(2,1)}), bf16[8,120,4096]{2,1,0:T(8,128)(2,1)}, u32[]{:S(2)}, u32[]{:S(2)}) async-start(bf16[8,120,4096]{2,1,0:T(8,128)(2,1)} %pad_maximum_fusion.1), calls=%async_computation.1 | async-start | bytes 15728640 | tf_op jit(solution)/shard_map/all_to_all | solution.py:120
  206.5 4.1 %fusion.8 = f32[1,384,2048]{2,1,0:T(8,128)S(1)} fusion(bf16[960,384]{1,0:T(8,128)(2,1)S(1)} %copy-done.11, bf16[1,960,4096]{2,1,0:T(8,128)(2,1)} %bitcast_select_fusion), kind=kOutput, calls=%fused_computation.25 | convolution fusion | flops 1509949440 | bytes 7815168 | tf_op jit(solution)/shard_map/erf,erd->efd/dot_general | solution.py:110
  210.6 4.1 %convolution_bitcast_fusion.1 = f32[1,384,2048]{2,1,0:T(8,128)S(1)} fusion(bf16[960,384]{1,0:T(8,128)(2,1)S(1)} %get-tuple-element.35, bf16[1,960,4096]{2,1,0:T(8,128)(2,1)} %bitcast_select_fusion), kind=kOutput, calls=%fused_computation.27 | convolution fusion | flops 1509949440 | bytes 7815168 | tf_op jit(solution)/shard_map/erf,erd->efd/dot_general | solution.py:111
  214.8 1.8 convolution_bitcast_fusion
  218.2 1.6 collective-permute-start.6
  219.7 51.8 %collective-permute-done.6 = bf16[3,192,2048]{2,1,0:T(8,128)(2,1)S(1)} collective-permute-done((bf16[3,192,2048]{2,1,0:T(8,128)(2,1)S(1)}, bf16[3,192,2048]{2,1,0:T(8,128)(2,1)S(1)}, u32[]{:S(2)}, u32[]{:S(2)}) %collective-permute-start.6) | collective-permute-done | bytes 2359328 | tf_op jit(solution)/shard_map/ppermute | solution.py:10
  272.4 1.4 fusion.71
  273.8 19.9 %all-to-all-done.1 = bf16[8,120,4096]{2,1,0:T(8,128)(2,1)} async-done(((bf16[8,120,4096]{2,1,0:T(8,128)(2,1)}), bf16[8,120,4096]{2,1,0:T(8,128)(2,1)}, u32[]{:S(2)}, u32[]{:S(2)}) %all-to-all-start.1) | async-done | bytes 7864352 | tf_op jit(solution)/shard_map/all_to_all | solution.py:120
  293.8 3.3 fusion.11
  297.9 2.9 fusion.19
  300.9 4.0 %fusion.15 = f32[384,2048]{1,0:T(8,128)S(1)} fusion(bf16[960,4096]{1,0:T(8,128)(2,1)} %bitcast.17, bf16[128,960]{0,1:T(8,128)(2,1)S(1)} %get-tuple-element.41, bf16[128,960]{0,1:T(8,128)(2,1)S(1)} %get-tuple-element.42, bf16[128,960]{0,1:T(8,128)(2,1)S(1)} %get-tuple-element.40), kind=kOutput, calls=%fused_computation.42 | convolution fusion | flops 1512161280 | bytes 7815168 | tf_op jit(solution)/shard_map/dot_general | solution.py:142
  305.2 3.4 collective-permute-start.4
  308.6 3.3 fusion.30
  313.6 4.0 %fusion.17 = f32[384,2048]{1,0:T(8,128)S(1)} fusion(bf16[960,4096]{1,0:T(8,128)(2,1)} %bitcast.17, bf16[128,960]{0,1:T(8,128)(2,1)S(1)} %get-tuple-element.44, bf16[128,960]{0,1:T(8,128)(2,1)S(1)} %get-tuple-element.45, bf16[128,960]{0,1:T(8,128)(2,1)S(1)} %get-tuple-element.43), kind=kOutput, calls=%fused_computation.44 | convolution fusion | flops 1512161280 | bytes 7815168 | tf_op jit(solution)/shard_map/dot_general | solution.py:142
  317.6 36.5 %collective-permute-done.5 = f32[128,6]{0,1:T(8,128)S(1)} collective-permute-done((f32[128,6]{0,1:T(8,128)S(1)}, f32[128,6]{0,1:T(8,128)S(1)}, u32[]{:S(2)}, u32[]{:S(2)}) %collective-permute-start.5) | collective-permute-done | bytes 3104 | tf_op jit(solution)/shard_map/ppermute | solution.py:10
  354.7 3.7 %add_convert_fusion.1 = bf16[128,2048]{1,0:T(8,128)(2,1)} fusion(bf16[128,4096]{1,0:T(8,128)(2,1)S(1)} %collective-permute-done.4, bf16[960,4096]{1,0:T(8,128)(2,1)} %bitcast.17, bf16[128,960]{0,1:T(8,128)(2,1)S(1)} %get-tuple-element.32), kind=kOutput, calls=%fused_computation.70 | convolution fusion | flops 504102912 | bytes 5226496 | tf_op jit(solution)/shard_map/dot_general | solution.py:144
  (87 shorter events, 18.2 us)
Async XLA Ops:
  0.6 13.4 %collective-permute-start.2 = (f32[128,6]{0,1:T(8,128)}, f32[128,6]{0,1:T(8,128)S(1)}, u32[]{:S(2)}, u32[]{:S(2)}) collective-permute-start(f32[128,6]{0,1:T(8,128)} %param.11), channel_id=1, source_target_pairs={{0,16},{16,0},{1,17},{17,1},{2,18},{18,2},{3,19},{19,3},{4,20},{20... | collective-permute-start | bytes 9224 | tf_op jit(solution)/shard_map/ppermute | solution.py:10
  6.9 49.9 %collective-permute-start.1 = (bf16[128,4096]{1,0:T(8,128)(2,1)S(1)}, bf16[128,4096]{1,0:T(8,128)(2,1)S(1)}, u32[]{:S(2)}, u32[]{:S(2)}) collective-permute-start(bf16[128,4096]{1,0:T(8,128)(2,1)S(1)} %constant_dynamic-update-slice_fusion), channel_id=1, source_target_pairs={{0,16},{16,0},{1,17},{17,1},{2,18},{18,2},{3,19},{19,3},{4,20},{20... | collective-permute-start | bytes 3145736 | tf_op jit(solution)/shard_map/ppermute | solution.py:10
  11.1 44.0 %collective-permute-start = (s32[128,6]{0,1:T(8,128)S(1)}, s32[128,6]{0,1:T(8,128)S(1)}, u32[]{:S(2)}, u32[]{:S(2)}) collective-permute-start(s32[128,6]{0,1:T(8,128)S(1)} %multiply_add_fusion), channel_id=1, source_target_pairs={{0,16},{16,0},{1,17},{17,1},{2,18},{18,2},{3,19},{19,3},{4,20},{20... | collective-permute-start | bytes 9224 | tf_op jit(solution)/shard_map/ppermute | solution.py:10
  56.8 4.4 %copy-start.7 = (bf16[128,4096]{1,0:T(8,128)(2,1)}, bf16[128,4096]{1,0:T(8,128)(2,1)S(1)}, u32[]{:S(2)}) copy-start(bf16[128,4096]{1,0:T(8,128)(2,1)S(1)} %collective-permute-done.1) | copy-start | bytes 3145732
  61.2 5.0 %copy-start.3 = (bf16[1,192,2048]{2,1,0:T(8,128)(2,1)S(1)}, bf16[1,192,2048]{2,1,0:T(8,128)(2,1)}, u32[]{:S(2)}) copy-start(bf16[1,192,2048]{2,1,0:T(8,128)(2,1)} %param.13) | copy-start | bytes 2359300
  61.2 99.4 %all-to-all-start = ((bf16[8,120,4096]{2,1,0:T(8,128)(2,1)}), bf16[8,120,4096]{2,1,0:T(8,128)(2,1)}, u32[]{:S(2)}, u32[]{:S(2)}) async-start(bf16[8,120,4096]{2,1,0:T(8,128)(2,1)} %bitcast.78), calls=%async_computation | async-start | bytes 15728640 | tf_op jit(solution)/shard_map/all_to_all | solution.py:69
  66.3 1.4 copy-start.4
  66.3 92.1 %copy-start.9 = (s32[16]{0:T(128)S(1)}, s32[16]{0:T(128)}, u32[]{:S(2)}) copy-start(s32[16]{0:T(128)} %param.12) | copy-start | bytes 196
  67.7 99.9 %collective-permute-start.3 = (bf16[3,192,2048]{2,1,0:T(8,128)(2,1)S(1)}, bf16[3,192,2048]{2,1,0:T(8,128)(2,1)}, u32[]{:S(2)}, u32[]{:S(2)}) collective-permute-start(bf16[3,192,2048]{2,1,0:T(8,128)(2,1)S(1)} %constant_dynamic-update-slice_fusion.2), channel_id=1, source_target_pairs={{0,1},{1,0},{2,3},{3,2},{4,5},{5,4},{6,7},{7,6},{8,9},{9,8},{10,11... | collective-permute-start | bytes 7077896 | tf_op jit(solution)/shard_map/ppermute | solution.py:10
  167.6 4.7 %copy-start = (bf16[1,960,4096]{2,1,0:T(8,128)(2,1)S(1)}, bf16[1,960,4096]{2,1,0:T(8,128)(2,1)}, u32[]{:S(2)}) copy-start(bf16[1,960,4096]{2,1,0:T(8,128)(2,1)} %bitcast_select_fusion) | copy-start | bytes 23592964
  179.4 5.8 %copy-start.10 = (bf16[960,384]{1,0:T(8,128)(2,1)}, bf16[960,384]{1,0:T(8,128)(2,1)S(1)}, u32[]{:S(2)}) copy-start(bf16[960,384]{1,0:T(8,128)(2,1)S(1)} %get-tuple-element.34) | copy-start | bytes 2211844
  179.4 5.8 %copy-start.1 = (bf16[960,384]{1,0:T(8,128)(2,1)}, bf16[960,384]{1,0:T(8,128)(2,1)S(1)}, u32[]{:S(2)}) copy-start(bf16[960,384]{1,0:T(8,128)(2,1)S(1)} %get-tuple-element.36) | copy-start | bytes 2211844
  201.2 5.3 %copy-start.11 = (bf16[960,384]{1,0:T(8,128)(2,1)S(1)}, bf16[960,384]{1,0:T(8,128)(2,1)}, u32[]{:S(2)}) copy-start(bf16[960,384]{1,0:T(8,128)(2,1)} %copy-done.10) | copy-start | bytes 2211844
  201.2 92.5 %all-to-all-start.1 = ((bf16[8,120,4096]{2,1,0:T(8,128)(2,1)}), bf16[8,120,4096]{2,1,0:T(8,128)(2,1)}, u32[]{:S(2)}, u32[]{:S(2)}) async-start(bf16[8,120,4096]{2,1,0:T(8,128)(2,1)} %pad_maximum_fusion.1), calls=%async_computation.1 | async-start | bytes 15728640 | tf_op jit(solution)/shard_map/all_to_all | solution.py:120
  206.5 8.3 %slice-start = ((s8[7864320]{0:T(1024)(128)(4,1)}), s8[4194304]{0:T(1024)(128)(4,1)S(1)}, s32[]{:S(2)}) async-start(s8[7864320]{0:T(1024)(128)(4,1)} %bitcast.79), calls=%async_computation.2 | async-start | bytes 8388608
  210.6 4.1 %slice-start.1 = ((s8[7864320]{0:T(1024)(128)(4,1)}), s8[3670016]{0:T(1024)(128)(4,1)S(1)}, s32[]{:S(2)}) async-start(s8[7864320]{0:T(1024)(128)(4,1)} %bitcast.79), calls=%async_computation.3 | async-start | bytes 7340032
  210.6 4.1 %copy-start.2 = (bf16[960,384]{1,0:T(8,128)(2,1)S(1)}, bf16[960,384]{1,0:T(8,128)(2,1)}, u32[]{:S(2)}) copy-start(bf16[960,384]{1,0:T(8,128)(2,1)} %copy-done.1) | copy-start | bytes 2211844
  218.2 53.4 %collective-permute-start.6 = (bf16[3,192,2048]{2,1,0:T(8,128)(2,1)S(1)}, bf16[3,192,2048]{2,1,0:T(8,128)(2,1)S(1)}, u32[]{:S(2)}, u32[]{:S(2)}) collective-permute-start(bf16[3,192,2048]{2,1,0:T(8,128)(2,1)S(1)} %slice.225), channel_id=1, source_target_pairs={{0,1},{1,0},{2,3},{3,2},{4,5},{5,4},{6,7},{7,6},{8,9},{9,8},{10,11... | collective-permute-start | bytes 7077896 | tf_op jit(solution)/shard_map/ppermute | solution.py:10
  272.4 21.4 %copy-start.8 = (bf16[128,4096]{1,0:T(8,128)(2,1)S(1)}, bf16[128,4096]{1,0:T(8,128)(2,1)}, u32[]{:S(2)}) copy-start(bf16[128,4096]{1,0:T(8,128)(2,1)} %copy-done.7) | copy-start | bytes 3145732
  304.9 3.7 %copy-start.5 = (bf16[128,2048]{1,0:T(8,128)(2,1)S(1)}, bf16[128,2048]{1,0:T(8,128)(2,1)}, u32[]{:S(2)}) copy-start(bf16[128,2048]{1,0:T(8,128)(2,1)} %param.9) | copy-start | bytes 1572868
  305.1 7.5 %copy-start.6 = (f32[128,6]{0,1:T(8,128)S(1)}, f32[128,6]{0,1:T(8,128)}, u32[]{:S(2)}) copy-start(f32[128,6]{0,1:T(8,128)} %param.11) | copy-start | bytes 9220
  305.2 49.5 %collective-permute-start.4 = (bf16[128,4096]{1,0:T(8,128)(2,1)S(1)}, bf16[128,4096]{1,0:T(8,128)(2,1)S(1)}, u32[]{:S(2)}, u32[]{:S(2)}) collective-permute-start(bf16[128,4096]{1,0:T(8,128)(2,1)S(1)} %pad_maximum_fusion.3), channel_id=1, source_target_pairs={{0,16},{16,0},{1,17},{17,1},{2,18},{18,2},{3,19},{19,3},{4,20},{20... | collective-permute-start | bytes 3145736 | tf_op jit(solution)/shard_map/ppermute | solution.py:10
  311.9 42.2 %collective-permute-start.5 = (f32[128,6]{0,1:T(8,128)S(1)}, f32[128,6]{0,1:T(8,128)S(1)}, u32[]{:S(2)}, u32[]{:S(2)}) collective-permute-start(f32[128,6]{0,1:T(8,128)S(1)} %get-tuple-element.28), channel_id=1, source_target_pairs={{0,16},{16,0},{1,17},{17,1},{2,18},{18,2},{3,19},{19,3},{4,20},{20... | collective-permute-start | bytes 9224 | tf_op jit(solution)/shard_map/ppermute | solution.py:10

commit v8 on v5

--- a/solution.py
+++ b/solution.py
@@ -86,12 +86,17 @@
     rows_cot = got[:, :, width:]
 
     full = jnp.concatenate(pieces, axis=1)
-    full_gate = full[:local_experts]
-    full_up = full[local_experts : 2 * local_experts]
     full_down = full[2 * local_experts :]
 
-    gate_pre = jnp.einsum("erd,efd->erf", rows_in, full_gate, preferred_element_type=jnp.float32)
-    up_pre = jnp.einsum("erd,efd->erf", rows_in, full_up, preferred_element_type=jnp.float32)
+    full_hidden = full.shape[1]
+    if local_experts == 1:
+        gate_up = full[:2].reshape(1, 2 * full_hidden, width)
+    else:
+        gate_up = full[: 2 * local_experts].reshape(2, local_experts, full_hidden, width)
+        gate_up = gate_up.transpose(1, 0, 2, 3).reshape(local_experts, 2 * full_hidden, width)
+    both_pre = jnp.einsum("erd,egd->erg", rows_in, gate_up, preferred_element_type=jnp.float32)
+    gate_pre = both_pre[..., :full_hidden]
+    up_pre = both_pre[..., full_hidden:]
     sigmoid_gate = jax.nn.sigmoid(gate_pre)
     activated = gate_pre * sigmoid_gate
     hidden = (activated * up_pre).astype(jnp.bfloat16)
@@ -103,13 +108,14 @@
         jnp.bfloat16
     )
     d_up = (d_hidden * activated).astype(jnp.bfloat16)
-    dx_rows = jnp.einsum("erf,efd->erd", d_gate, full_gate, preferred_element_type=jnp.float32)
-    dx_rows = (
-        dx_rows + jnp.einsum("erf,efd->erd", d_up, full_up, preferred_element_type=jnp.float32)
+    d_both = jnp.concatenate([d_gate, d_up], axis=-1)
+    dx_rows = jnp.einsum(
+        "erg,egd->erd", d_both, gate_up, preferred_element_type=jnp.float32
     ).astype(jnp.bfloat16)
     part_down = jnp.einsum("erf,erd->efd", hidden, rows_cot, preferred_element_type=jnp.float32)
-    part_gate = jnp.einsum("erf,erd->efd", d_gate, rows_in, preferred_element_type=jnp.float32)
-    part_up = jnp.einsum("erf,erd->efd", d_up, rows_in, preferred_element_type=jnp.float32)
+    part_both = jnp.einsum("erg,erd->egd", d_both, rows_in, preferred_element_type=jnp.float32)
+    part_gate = part_both[:, :full_hidden]
+    part_up = part_both[:, full_hidden:]
 
     back = jnp.stack([out_rows, dx_rows], axis=1)
     back = back.reshape(local_experts, 2, n_in, 2 * slots, width).transpose(2, 0, 1, 3, 4)

time: 359 us -> 351 us (0.978)
  matrix products: 44.8 us -> 38.6 us
  other arithmetic: 26.5 us -> 22.5 us
    dot_general x6 -> x3, matrix products: 19.8 us -> 16.8 us  [the longest x1 7.64 us: on_device(): jnp.einsum('erd,egd->erg', rows_in, gate_up, preferred_element_type=jnp.f...]
    unnamed x42 -> x48, local copies, waits for them, and re-layouts: 7.68 us -> 7.7 us
  transfers between devices with their start and end apart: 9 -> 9, of which waited for: 3 -> 3; matrix products, arithmetic and copies ran while one was open for 14% -> 13% of each run, Pallas kernels for 0% -> 0%
where the time goes in v8:
time: 351 us; the launch traced here: 350 us
  waiting for transfers between devices  154 us (44%)
  blocking collectives  90.7 us (26%)
  matrix products  38.6 us (11%)
  starting transfers between devices  23.5 us (7%)
  other arithmetic  22.5 us (6%)
  local copies, waits for them, and re-layouts  19 us (5%)
    psum x1, blocking collectives, on_device(): all_counts = lax.psum(count_rows, ('half', 'inner'))  90.7 us
    ppermute x7, waiting for transfers between devices, shifted(): lax.ppermute(value, axis, [(j, (j + shift) % count) for j in range(count)])  85.4 us
    all_to_all x1, waiting for transfers between devices, on_device(): lax.all_to_all(back, 'inner', split_axis=0, concat_axis=0, tiled=True)  68.9 us
    ppermute x7, starting transfers between devices, shifted(): lax.ppermute(value, axis, [(j, (j + shift) % count) for j in range(count)])  13.3 us
    unnamed x48, local copies, waits for them, and re-layouts  7.7 us
    dot_general x1, matrix products, on_device(): jnp.einsum('erd,egd->erg', rows_in, gate_up, preferred_element_type=jnp.f...  7.64 us
  transfers between devices with their start and end apart: 9, of which 3 were waited for; matrix products, arithmetic and copies ran while one was open for 13% of the time, Pallas kernels for 0%

profile of v8, /device:TPU:0, one launch (start us, length us, event | category | flops | bytes accessed | tf_op | source)
XLA Modules:
  0.0 349.9 jit_solution(4884660477446778453)
XLA Ops:
  0.6 4.1 %collective-permute-start.1 = (f32[128,6]{0,1:T(8,128)}, f32[128,6]{0,1:T(8,128)S(1)}, u32[]{:S(2)}, u32[]{:S(2)}) collective-permute-start(f32[128,6]{0,1:T(8,128)} %param.11), channel_id=1, source_target_pairs={{0,16},{16,0},{1,17},{17,1},{2,18},{18,2},{3,19},{19,3},{4,20},{20... | collective-permute-start | bytes 9224 | tf_op jit(solution)/shard_map/ppermute | solution.py:10
  5.8 1.7 reduce-window.6
  11.0 3.0 collective-permute-start.2
  16.4 42.7 %collective-permute-done.2 = bf16[128,4096]{1,0:T(8,128)(2,1)S(1)} collective-permute-done((bf16[128,4096]{1,0:T(8,128)(2,1)S(1)}, bf16[128,4096]{1,0:T(8,128)(2,1)S(1)}, u32[]{:S(2)}, u32[]{:S(2)}) %collective-permute-start.2) | collective-permute-done | bytes 1048608 | tf_op jit(solution)/shard_map/ppermute | solution.py:10
  59.1 4.4 %multiply_convert_fusion = bf16[960,4096]{1,0:T(8,128)(2,1)} fusion(pred[960,256]{1,0:T(8,128)(4,1)S(1)} %fusion, f32[960]{0:T(1024)S(1)} %select_reduce_fusion.1, pred[4096]{0:T(1024)(128)(4,1)S(1)} %iota_compare_fusion.4, bf16[128,4096]{1,0:T(8,128)(2,1)S(1)} %collective-permute-done.2, bf16[128,4096]{1,0:T(8,128)(2,1)S(1)} %constant_dynamic-update-slice_fusion.2), kind=kOutput, calls=%fused_computation.1 | convolution fusion | flops 2029256704 | bytes 10215168 | tf_op jit(solution)/shard_map/dot_general | solution.py:65
  63.5 5.0 %all-to-all-start = ((bf16[8,120,4096]{2,1,0:T(8,128)(2,1)}), bf16[8,120,4096]{2,1,0:T(8,128)(2,1)}, u32[]{:S(2)}, u32[]{:S(2)}) async-start(bf16[8,120,4096]{2,1,0:T(8,128)(2,1)} %bitcast.93), calls=%async_computation | async-start | bytes 15728640 | tf_op jit(solution)/shard_map/all_to_all | solution.py:69
  68.7 1.2 constant_dynamic-update-slice_fusion.5
  70.0 1.6 collective-permute-start.3
  72.1 90.7 %psum.7 = s32[16,16]{1,0:T(8,128)S(1)} all-reduce(s32[16,16]{1,0:T(8,128)S(1)} %broadcast_select_fusion), channel_id=1, replica_groups=mesh['half'=2,'inner'=8,'dp'=2] {'half','inner'}, use_global_device_ids=true, to_apply=%region_4.5 | all-reduce | flops 256 | bytes 2048 | tf_op jit(solution)/shard_map/psum | solution.py:49
  165.1 2.9 fusion.5
  168.1 3.8 %bitcast_select_fusion = bf16[1,960,4096]{2,1,0:T(8,128)(2,1)S(1)} fusion(pred[960]{0:T(1024)(128)(4,1)S(1)} %lt.72, bf16[1,960,4096]{2,1,0:T(8,128)(2,1)} %bitcast.89), kind=kLoop, calls=%fused_computation.4 | loop fusion | flops 3932160 | bytes 15729600 | tf_op jit(solution)/shard_map/jit(_where)/select_n | solution.py:80
  172.0 7.6 %fusion.10 = f32[1,960,768]{2,1,0:T(8,128)S(1)} fusion(bf16[768,2048]{1,0:T(8,128)(2,1)} %bitcast.99, bf16[1,960,4096]{2,1,0:T(8,128)(2,1)S(1)} %bitcast_select_fusion), kind=kOutput, calls=%fused_computation.32 | convolution fusion | flops 3019898880 | bytes 10027008 | tf_op jit(solution)/shard_map/erd,egd->erg/dot_general | solution.py:97
  179.6 4.0 %fusion.19 = (bf16[1,960,384]{2,1,0:T(8,128)(2,1)S(1)}, bf16[1,960,384]{2,1,0:T(8,128)(2,1)S(1)}, bf16[960,384]{1,0:T(8,128)(2,1)S(1)}) fusion(f32[1,960,768]{2,1,0:T(8,128)S(1)} %fusion.10, bf16[3,192,2048]{2,1,0:T(8,128)(2,1)} %collective-permute-done.3, bf16[3,192,2048]{2,1,0:T(8,128)(2,1)S(1)} %copy-done.3, bf16[1,960,4096]{2,1,0:T(8,128)(2,1)S(1)} %bitcast_select_fusion), kind=kOutput, calls=%fused_computation.45 | convolution fusion | flops 1518256128 | bytes 13811712 | tf_op jit(solution)/shard_map/erd,efd->erf/dot_general | solution.py:106
  183.6 3.5 convolution_convert_fusion
  187.2 3.3 convolution_convert_fusion.1
  190.5 3.8 %maximum_bitcast_fusion = bf16[8,2,120,2048]{3,2,1,0:T(8,128)(2,1)} fusion(bf16[1,1,8,120,2048]{4,3,1,2,0:T(8,128)(2,1)S(1)} %bitcast.97, bf16[1,1,8,120,2048]{4,3,1,2,0:T(8,128)(2,1)S(1)} %bitcast.98), kind=kLoop, calls=%fused_computation.3 | loop fusion | flops 3932160 | bytes 15728640 | tf_op jit(solution)/shard_map/reshape | solution.py:122
  194.3 5.2 %all-to-all-start.1 = ((bf16[8,2,120,2048]{3,2,1,0:T(8,128)(2,1)}), bf16[8,2,120,2048]{3,2,1,0:T(8,128)(2,1)}, u32[]{:S(2)}, u32[]{:S(2)}) async-start(bf16[8,2,120,2048]{3,2,1,0:T(8,128)(2,1)} %maximum_bitcast_fusion), calls=%async_computation.1 | async-start | bytes 15728640 | tf_op jit(solution)/shard_map/all_to_all | solution.py:123
  199.6 4.1 %fusion.6 = f32[1,384,2048]{2,1,0:T(8,128)S(1)} fusion(bf16[960,384]{1,0:T(8,128)(2,1)S(1)} %copy-done.13, bf16[1,960,4096]{2,1,0:T(8,128)(2,1)} %copy-done.1), kind=kOutput, calls=%fused_computation.26 | convolution fusion | flops 1509949440 | bytes 7815168 | tf_op jit(solution)/shard_map/erf,erd->efd/dot_general | solution.py:115
  203.7 5.7 %convolution_bitcast_fusion = f32[1,768,2048]{2,1,0:T(8,128)S(1)} fusion(bf16[1,960,4096]{2,1,0:T(8,128)(2,1)} %copy-done.1, bf16[1,960,384]{2,1,0:T(8,128)(2,1)S(1)} %copy-done.17, bf16[1,960,384]{2,1,0:T(8,128)(2,1)S(1)} %copy-done.15), kind=kOutput, calls=%fused_computation.19 | convolution fusion | flops 3022848000 | bytes 11698176 | tf_op jit(solution)/shard_map/erg,erd->egd/dot_general | solution.py:116
  211.0 3.6 %copy-done = f32[3,384,2048]{2,1,0:T(8,128)} copy-done((f32[3,384,2048]{2,1,0:T(8,128)}, f32[3,384,2048]{2,1,0:T(8,128)S(1)}, u32[]{:S(2)}) %copy-start) | copy-done | bytes 9437208
  214.6 1.8 slice.223
  216.4 1.5 collective-permute-start.6
  217.9 68.9 %all-to-all-done.1 = bf16[8,2,120,2048]{3,2,1,0:T(8,128)(2,1)} async-done(((bf16[8,2,120,2048]{3,2,1,0:T(8,128)(2,1)}), bf16[8,2,120,2048]{3,2,1,0:T(8,128)(2,1)}, u32[]{:S(2)}, u32[]{:S(2)}) %all-to-all-start.1) | async-done | bytes 7864352 | tf_op jit(solution)/shard_map/all_to_all | solution.py:123
  286.8 4.0 %fusion.43 = (bf16[8,1,120,2048]{3,2,1,0:T(8,128)(2,1)S(1)}, bf16[8,1,120,2048]{3,2,1,0:T(8,128)(2,1)S(1)}) fusion(bf16[8,2,120,2048]{3,2,1,0:T(8,128)(2,1)} %all-to-all-done.1), kind=kLoop, calls=%fused_computation.107 | loop fusion | bytes 15728640 | tf_op jit(solution)/shard_map/slice | solution.py:136
  292.0 1.9 select_reduce_fusion
  293.9 1.3 fusion.49
  295.5 3.6 %fusion.12 = f32[768,2048]{1,0:T(8,128)S(1)} fusion(bf16[960,2048]{1,0:T(8,128)(2,1)S(1)} %bitcast.95, bf16[256,960]{0,1:T(8,128)(2,1)S(1)} %get-tuple-element.44, bf16[256,960]{0,1:T(8,128)(2,1)S(1)} %get-tuple-element.45, bf16[256,960]{0,1:T(8,128)(2,1)S(1)} %get-tuple-element.43), kind=kOutput, calls=%fused_computation.35 | convolution fusion | flops 3024322560 | bytes 11698176 | tf_op jit(solution)/shard_map/dot_general | solution.py:140
  299.8 1.2 collective-permute-start.4
  302.0 1.8 collective-permute-start.5
  303.8 1.4 fusion.45
  305.3 42.7 %collective-permute-done.5 = f32[128,6]{0,1:T(8,128)S(1)} collective-permute-done((f32[128,6]{0,1:T(8,128)S(1)}, f32[128,6]{0,1:T(8,128)S(1)}, u32[]{:S(2)}, u32[]{:S(2)}) %collective-permute-start.5) | collective-permute-done | bytes 3104 | tf_op jit(solution)/shard_map/ppermute | solution.py:10
  348.6 1.3 fusion.25
  (99 shorter events, 15.3 us)
Async XLA Ops:
  0.6 14.1 %collective-permute-start.1 = (f32[128,6]{0,1:T(8,128)}, f32[128,6]{0,1:T(8,128)S(1)}, u32[]{:S(2)}, u32[]{:S(2)}) collective-permute-start(f32[128,6]{0,1:T(8,128)} %param.11), channel_id=1, source_target_pairs={{0,16},{16,0},{1,17},{17,1},{2,18},{18,2},{3,19},{19,3},{4,20},{20... | collective-permute-start | bytes 9224 | tf_op jit(solution)/shard_map/ppermute | solution.py:10
  8.8 5.9 %collective-permute-start = (s32[128,6]{0,1:T(8,128)S(1)}, s32[128,6]{0,1:T(8,128)S(1)}, u32[]{:S(2)}, u32[]{:S(2)}) collective-permute-start(s32[128,6]{0,1:T(8,128)S(1)} %multiply_add_fusion), channel_id=1, source_target_pairs={{0,16},{16,0},{1,17},{17,1},{2,18},{18,2},{3,19},{19,3},{4,20},{20... | collective-permute-start | bytes 9224 | tf_op jit(solution)/shard_map/ppermute | solution.py:10
  11.0 52.5 %copy-start.7 = (bf16[128,4096]{1,0:T(8,128)(2,1)}, bf16[128,4096]{1,0:T(8,128)(2,1)S(1)}, u32[]{:S(2)}) copy-start(bf16[128,4096]{1,0:T(8,128)(2,1)S(1)} %constant_dynamic-update-slice_fusion.2) | copy-start | bytes 3145732
  11.0 48.1 %collective-permute-start.2 = (bf16[128,4096]{1,0:T(8,128)(2,1)S(1)}, bf16[128,4096]{1,0:T(8,128)(2,1)S(1)}, u32[]{:S(2)}, u32[]{:S(2)}) collective-permute-start(bf16[128,4096]{1,0:T(8,128)(2,1)S(1)} %constant_dynamic-update-slice_fusion.2), channel_id=1, source_target_pairs={{0,16},{16,0},{1,17},{17,1},{2,18},{18,2},{3,19},{19,3},{4,20},{20... | collective-permute-start | bytes 3145736 | tf_op jit(solution)/shard_map/ppermute | solution.py:10
  59.1 4.4 %copy-start.9 = (bf16[128,4096]{1,0:T(8,128)(2,1)}, bf16[128,4096]{1,0:T(8,128)(2,1)S(1)}, u32[]{:S(2)}) copy-start(bf16[128,4096]{1,0:T(8,128)(2,1)S(1)} %collective-permute-done.2) | copy-start | bytes 3145732
  63.5 5.0 %copy-start.5 = (bf16[1,192,2048]{2,1,0:T(8,128)(2,1)S(1)}, bf16[1,192,2048]{2,1,0:T(8,128)(2,1)}, u32[]{:S(2)}) copy-start(bf16[1,192,2048]{2,1,0:T(8,128)(2,1)} %param.13) | copy-start | bytes 2359300
  63.5 104.6 %all-to-all-start = ((bf16[8,120,4096]{2,1,0:T(8,128)(2,1)}), bf16[8,120,4096]{2,1,0:T(8,128)(2,1)}, u32[]{:S(2)}, u32[]{:S(2)}) async-start(bf16[8,120,4096]{2,1,0:T(8,128)(2,1)} %bitcast.93), calls=%async_computation | async-start | bytes 15728640 | tf_op jit(solution)/shard_map/all_to_all | solution.py:69
  68.6 1.4 copy-start.6
  68.6 94.3 %copy-start.11 = (s32[16]{0:T(128)S(1)}, s32[16]{0:T(128)}, u32[]{:S(2)}) copy-start(s32[16]{0:T(128)} %param.12) | copy-start | bytes 196
  70.0 98.1 %copy-start.2 = (bf16[3,192,2048]{2,1,0:T(8,128)(2,1)}, bf16[3,192,2048]{2,1,0:T(8,128)(2,1)S(1)}, u32[]{:S(2)}) copy-start(bf16[3,192,2048]{2,1,0:T(8,128)(2,1)S(1)} %constant_dynamic-update-slice_fusion.4) | copy-start | bytes 7077892
  70.0 95.1 %collective-permute-start.3 = (bf16[3,192,2048]{2,1,0:T(8,128)(2,1)S(1)}, bf16[3,192,2048]{2,1,0:T(8,128)(2,1)}, u32[]{:S(2)}, u32[]{:S(2)}) collective-permute-start(bf16[3,192,2048]{2,1,0:T(8,128)(2,1)S(1)} %constant_dynamic-update-slice_fusion.4), channel_id=1, source_target_pairs={{0,1},{1,0},{2,3},{3,2},{4,5},{5,4},{6,7},{7,6},{8,9},{9,8},{10,11... | collective-permute-start | bytes 7077896 | tf_op jit(solution)/shard_map/ppermute | solution.py:10
  171.9 7.7 %copy-start.1 = (bf16[1,960,4096]{2,1,0:T(8,128)(2,1)}, bf16[1,960,4096]{2,1,0:T(8,128)(2,1)S(1)}, u32[]{:S(2)}) copy-start(bf16[1,960,4096]{2,1,0:T(8,128)(2,1)S(1)} %bitcast_select_fusion) | copy-start | bytes 23592964
  171.9 7.7 %copy-start.3 = (bf16[3,192,2048]{2,1,0:T(8,128)(2,1)S(1)}, bf16[3,192,2048]{2,1,0:T(8,128)(2,1)}, u32[]{:S(2)}) copy-start(bf16[3,192,2048]{2,1,0:T(8,128)(2,1)} %copy-done.2) | copy-start | bytes 7077892
  179.6 4.0 %copy-start.4 = (bf16[2,384,2048]{2,1,0:T(8,128)(2,1)S(1)}, bf16[2,384,2048]{2,1,0:T(8,128)(2,1)}, u32[]{:S(2)}) copy-start(bf16[2,384,2048]{2,1,0:T(8,128)(2,1)} %fusion.5) | copy-start | bytes 9437188
  183.6 3.5 %copy-start.14 = (bf16[1,960,384]{2,1,0:T(8,128)(2,1)}, bf16[1,960,384]{2,1,0:T(8,128)(2,1)S(1)}, u32[]{:S(2)}) copy-start(bf16[1,960,384]{2,1,0:T(8,128)(2,1)S(1)} %get-tuple-element.35) | copy-start | bytes 2211844
  183.6 3.5 %copy-start.16 = (bf16[1,960,384]{2,1,0:T(8,128)(2,1)}, bf16[1,960,384]{2,1,0:T(8,128)(2,1)S(1)}, u32[]{:S(2)}) copy-start(bf16[1,960,384]{2,1,0:T(8,128)(2,1)S(1)} %get-tuple-element.36) | copy-start | bytes 2211844
  183.6 3.5 %copy-start.12 = (bf16[960,384]{1,0:T(8,128)(2,1)}, bf16[960,384]{1,0:T(8,128)(2,1)S(1)}, u32[]{:S(2)}) copy-start(bf16[960,384]{1,0:T(8,128)(2,1)S(1)} %get-tuple-element.37) | copy-start | bytes 2211844
  194.3 5.2 %copy-start.13 = (bf16[960,384]{1,0:T(8,128)(2,1)S(1)}, bf16[960,384]{1,0:T(8,128)(2,1)}, u32[]{:S(2)}) copy-start(bf16[960,384]{1,0:T(8,128)(2,1)} %copy-done.12) | copy-start | bytes 2211844
  194.3 92.5 %all-to-all-start.1 = ((bf16[8,2,120,2048]{3,2,1,0:T(8,128)(2,1)}), bf16[8,2,120,2048]{3,2,1,0:T(8,128)(2,1)}, u32[]{:S(2)}, u32[]{:S(2)}) async-start(bf16[8,2,120,2048]{3,2,1,0:T(8,128)(2,1)} %maximum_bitcast_fusion), calls=%async_computation.1 | async-start | bytes 15728640 | tf_op jit(solution)/shard_map/all_to_all | solution.py:123
  199.5 4.1 %copy-start.15 = (bf16[1,960,384]{2,1,0:T(8,128)(2,1)S(1)}, bf16[1,960,384]{2,1,0:T(8,128)(2,1)}, u32[]{:S(2)}) copy-start(bf16[1,960,384]{2,1,0:T(8,128)(2,1)} %copy-done.14) | copy-start | bytes 2211844
  199.6 4.1 %copy-start.17 = (bf16[1,960,384]{2,1,0:T(8,128)(2,1)S(1)}, bf16[1,960,384]{2,1,0:T(8,128)(2,1)}, u32[]{:S(2)}) copy-start(bf16[1,960,384]{2,1,0:T(8,128)(2,1)} %copy-done.16) | copy-start | bytes 2211844
  210.9 3.6 %copy-start = (f32[3,384,2048]{2,1,0:T(8,128)}, f32[3,384,2048]{2,1,0:T(8,128)S(1)}, u32[]{:S(2)}) copy-start(f32[3,384,2048]{2,1,0:T(8,128)S(1)} %pad_maximum_fusion) | copy-start | bytes 28311556
  216.4 74.4 %copy-start.8 = (bf16[128,4096]{1,0:T(8,128)(2,1)S(1)}, bf16[128,4096]{1,0:T(8,128)(2,1)}, u32[]{:S(2)}) copy-start(bf16[128,4096]{1,0:T(8,128)(2,1)} %copy-done.7) | copy-start | bytes 3145732
  216.4 84.7 %collective-permute-start.6 = (bf16[3,192,2048]{2,1,0:T(8,128)(2,1)}, bf16[3,192,2048]{2,1,0:T(8,128)(2,1)S(1)}, u32[]{:S(2)}, u32[]{:S(2)}) collective-permute-start(bf16[3,192,2048]{2,1,0:T(8,128)(2,1)} %slice.223), channel_id=1, source_target_pairs={{0,1},{1,0},{2,3},{3,2},{4,5},{5,4},{6,7},{7,6},{8,9},{9,8},{10,11... | collective-permute-start | bytes 7077896 | tf_op jit(solution)/shard_map/ppermute | solution.py:10
  286.8 4.0 %copy-start.10 = (bf16[128,4096]{1,0:T(8,128)(2,1)S(1)}, bf16[128,4096]{1,0:T(8,128)(2,1)}, u32[]{:S(2)}) copy-start(bf16[128,4096]{1,0:T(8,128)(2,1)} %copy-done.9) | copy-start | bytes 3145732
  295.4 5.6 %slice-start = ((s8[9437184]{0:T(1024)(128)(4,1)}), s8[4194304]{0:T(1024)(128)(4,1)S(1)}, s32[]{:S(2)}) async-start(s8[9437184]{0:T(1024)(128)(4,1)} %bitcast.91), calls=%async_computation.2 | async-start | bytes 8388608
  295.4 5.6 %slice-start.1 = ((s8[9437184]{0:T(1024)(128)(4,1)}), s8[4194304]{0:T(1024)(128)(4,1)S(1)}, s32[]{:S(2)}) async-start(s8[9437184]{0:T(1024)(128)(4,1)} %bitcast.91), calls=%async_computation.3 | async-start | bytes 8388608
  299.0 2.1 slice-start.2
  299.8 48.8 %collective-permute-start.4 = (bf16[128,4096]{1,0:T(8,128)(2,1)S(1)}, bf16[128,4096]{1,0:T(8,128)(2,1)S(1)}, u32[]{:S(2)}, u32[]{:S(2)}) collective-permute-start(bf16[128,4096]{1,0:T(8,128)(2,1)S(1)} %pad_maximum_fusion.2), channel_id=1, source_target_pairs={{0,16},{16,0},{1,17},{17,1},{2,18},{18,2},{3,19},{19,3},{4,20},{20... | collective-permute-start | bytes 3145736 | tf_op jit(solution)/shard_map/ppermute | solution.py:10
  302.0 46.0 %collective-permute-start.5 = (f32[128,6]{0,1:T(8,128)S(1)}, f32[128,6]{0,1:T(8,128)S(1)}, u32[]{:S(2)}, u32[]{:S(2)}) collective-permute-start(f32[128,6]{0,1:T(8,128)S(1)} %slice.159), channel_id=1, source_target_pairs={{0,16},{16,0},{1,17},{17,1},{2,18},{18,2},{3,19},{19,3},{4,20},{20... | collective-permute-start | bytes 9224 | tf_op jit(solution)/shard_map/ppermute | solution.py:10

commit v9 on v8

--- a/solution.py
+++ b/solution.py
@@ -134,26 +134,29 @@
 
     out_part = back[:, 0].reshape(2 * half_rows, width)
     dx_part = back[:, 1].reshape(2 * half_rows, width)
-    hit = dest[:, :, None] == jnp.arange(2 * half_rows, dtype=jnp.int32)[None, None, :]
-    weight = jnp.sum(jnp.where(hit, all_gates[:, :, None], 0.0), axis=1)
-    ones = jnp.sum(hit.astype(jnp.float32), axis=1).astype(jnp.bfloat16)
-    layer = jnp.dot(in_three(weight), out_part, preferred_element_type=jnp.float32)
-    n_all = 2 * tok_rows
-    layer = layer[:n_all] + layer[n_all : 2 * n_all] + layer[2 * n_all :]
-    grads = jnp.dot(ones, dx_part, preferred_element_type=jnp.float32)
-    scores = jnp.dot(all_rows[:, width:], out_part.T, preferred_element_type=jnp.float32)
-    gg = jnp.sum(jnp.where(hit, scores[:, None, :], 0.0), axis=2)
+    columns = jnp.arange(2 * half_rows, dtype=jnp.int32)
 
+    def combine(which):
+        rows = slice(which * tok_rows, (which + 1) * tok_rows)
+        hit = dest[rows][:, :, None] == columns[None, None, :]
+        weight = jnp.sum(jnp.where(hit, all_gates[rows][:, :, None], 0.0), axis=1)
+        ones = jnp.sum(hit.astype(jnp.float32), axis=1).astype(jnp.bfloat16)
+        layer = jnp.dot(in_three(weight), out_part, preferred_element_type=jnp.float32)
+        layer = layer[:tok_rows] + layer[tok_rows : 2 * tok_rows] + layer[2 * tok_rows :]
+        grads = jnp.dot(ones, dx_part, preferred_element_type=jnp.float32)
+        scores = jnp.dot(all_rows[rows, width:], out_part.T, preferred_element_type=jnp.float32)
+        gg = jnp.sum(jnp.where(hit, scores[:, None, :], 0.0), axis=2)
+        return layer, grads, gg
+
+    partner_layer, partner_grads, partner_gg = combine(1)
     returned = shifted(
-        jnp.concatenate([layer[tok_rows:], grads[tok_rows:]], axis=1).astype(jnp.bfloat16),
-        "half",
-        2,
-        1,
+        jnp.concatenate([partner_layer, partner_grads], axis=1).astype(jnp.bfloat16), "half", 2, 1
     )
-    returned_gg = shifted(gg[tok_rows:], "half", 2, 1)
-    layer_out = (layer[:tok_rows] + returned[:, :width].astype(jnp.float32)).astype(jnp.bfloat16)
-    grad_tokens = (grads[:tok_rows] + returned[:, width:].astype(jnp.float32)).astype(jnp.bfloat16)
-    grad_gates = gg[:tok_rows] + returned_gg
+    returned_gg = shifted(partner_gg, "half", 2, 1)
+    own_layer, own_grads, own_gg = combine(0)
+    layer_out = (own_layer + returned[:, :width].astype(jnp.float32)).astype(jnp.bfloat16)
+    grad_tokens = (own_grads + returned[:, width:].astype(jnp.float32)).astype(jnp.bfloat16)
+    grad_gates = own_gg + returned_gg
     return (layer_out, grad_tokens, grad_gates, grad_gate_w, grad_up_w, grad_down_w)
 
 

time: 351 us -> 344 us (0.980)
  local copies, waits for them, and re-layouts: 19 us -> 13 us
    all_to_all x1, waiting for transfers between devices: 68.9 us -> 19.8 us  [on_device(): lax.all_to_all(back, 'inner', split_axis=0, concat_axis=0, tiled=True)]
    ppermute x7, waiting for transfers between devices: 85.4 us -> 134 us  [shifted(): lax.ppermute(value, axis, [(j, (j + shift) % count) for j in range(count)])]
    unnamed x48 -> x39, local copies, waits for them, and re-layouts: 7.7 us -> 3.39 us
    dot_general x3 -> x6, matrix products: 6.07 us -> 8.35 us  [the longest x2 3.71 us: combine(): jnp.dot(in_three(weight), out_part, preferred_element_type=jnp.float32)]
  transfers between devices with their start and end apart: 9 -> 9, of which waited for: 3 -> 4; matrix products, arithmetic and copies ran while one was open for 13% -> 10% of each run, Pallas kernels for 0% -> 0%
where the time goes in v9:
time: 344 us; the launch traced here: 343 us
  waiting for transfers between devices  153 us (44%)
  blocking collectives  88.6 us (26%)
  matrix products  40.8 us (12%)
  starting transfers between devices  24.2 us (7%)
  other arithmetic  22.4 us (7%)
  local copies, waits for them, and re-layouts  13 us (4%)
    ppermute x7, waiting for transfers between devices, shifted(): lax.ppermute(value, axis, [(j, (j + shift) % count) for j in range(count)])  134 us
    psum x1, blocking collectives, on_device(): all_counts = lax.psum(count_rows, ('half', 'inner'))  88.6 us
    all_to_all x1, waiting for transfers between devices, on_device(): lax.all_to_all(back, 'inner', split_axis=0, concat_axis=0, tiled=True)  19.8 us
    ppermute x7, starting transfers between devices, shifted(): lax.ppermute(value, axis, [(j, (j + shift) % count) for j in range(count)])  13.8 us
    dot_general x1, matrix products, on_device(): jnp.einsum('erd,egd->erg', rows_in, gate_up, preferred_element_type=jnp.f...  7.64 us
  transfers between devices with their start and end apart: 9, of which 4 were waited for; matrix products, arithmetic and copies ran while one was open for 10% of the time, Pallas kernels for 0%

profile of v9, /device:TPU:0, one launch (start us, length us, event | category | flops | bytes accessed | tf_op | source)
XLA Modules:
  0.0 343.5 jit_solution(16296641009947971912)
XLA Ops:
  0.6 4.1 %collective-permute-start.2 = (f32[128,6]{0,1:T(8,128)}, f32[128,6]{0,1:T(8,128)S(1)}, u32[]{:S(2)}, u32[]{:S(2)}) collective-permute-start(f32[128,6]{0,1:T(8,128)} %param.11), channel_id=1, source_target_pairs={{0,16},{16,0},{1,17},{17,1},{2,18},{18,2},{3,19},{19,3},{4,20},{20... | collective-permute-start | bytes 9224 | tf_op jit(solution)/shard_map/ppermute | solution.py:10
  8.1 1.7 reduce-window.6
  11.1 2.9 collective-permute-start
  14.7 40.4 %collective-permute-done = s32[128,6]{0,1:T(8,128)S(1)} collective-permute-done((s32[128,6]{0,1:T(8,128)S(1)}, s32[128,6]{0,1:T(8,128)S(1)}, u32[]{:S(2)}, u32[]{:S(2)}) %collective-permute-start) | collective-permute-done | bytes 3104 | tf_op jit(solution)/shard_map/ppermute | solution.py:10
  56.8 4.3 %multiply_convert_fusion = bf16[960,4096]{1,0:T(8,128)(2,1)} fusion(pred[960,256]{1,0:T(8,128)(4,1)S(1)} %fusion, f32[960]{0:T(1024)S(1)} %select_reduce_fusion, pred[4096]{0:T(1024)(128)(4,1)S(1)} %iota_compare_fusion.5, bf16[128,4096]{1,0:T(8,128)(2,1)S(1)} %collective-permute-done.1, bf16[128,4096]{1,0:T(8,128)(2,1)S(1)} %constant_dynamic-update-slice_fusion), kind=kOutput, calls=%fused_computation.1 | convolution fusion | flops 2029256704 | bytes 10215168 | tf_op jit(solution)/shard_map/dot_general | solution.py:65
  61.2 5.0 %all-to-all-start = ((bf16[8,120,4096]{2,1,0:T(8,128)(2,1)}), bf16[8,120,4096]{2,1,0:T(8,128)(2,1)}, u32[]{:S(2)}, u32[]{:S(2)}) async-start(bf16[8,120,4096]{2,1,0:T(8,128)(2,1)} %bitcast.104), calls=%async_computation | async-start | bytes 15728640 | tf_op jit(solution)/shard_map/all_to_all | solution.py:69
  66.3 1.2 constant_dynamic-update-slice_fusion.3
  67.6 1.6 collective-permute-start.3
  69.7 88.6 %psum.7 = s32[16,16]{1,0:T(8,128)S(1)} all-reduce(s32[16,16]{1,0:T(8,128)S(1)} %broadcast_select_fusion), channel_id=1, replica_groups=mesh['half'=2,'inner'=8,'dp'=2] {'half','inner'}, use_global_device_ids=true, to_apply=%region_4.5 | all-reduce | flops 256 | bytes 2048 | tf_op jit(solution)/shard_map/psum | solution.py:49
  160.6 2.9 fusion.5
  163.5 3.8 %bitcast_select_fusion = bf16[1,960,4096]{2,1,0:T(8,128)(2,1)S(1)} fusion(pred[960]{0:T(1024)(128)(4,1)S(1)} %lt.68, bf16[1,960,4096]{2,1,0:T(8,128)(2,1)} %bitcast.96), kind=kLoop, calls=%fused_computation.4 | loop fusion | flops 3932160 | bytes 15729600 | tf_op jit(solution)/shard_map/jit(_where)/select_n | solution.py:80
  167.4 7.6 %fusion.10 = f32[1,960,768]{2,1,0:T(8,128)S(1)} fusion(bf16[768,2048]{1,0:T(8,128)(2,1)} %bitcast.107, bf16[1,960,4096]{2,1,0:T(8,128)(2,1)S(1)} %bitcast_select_fusion), kind=kOutput, calls=%fused_computation.35 | convolution fusion | flops 3019898880 | bytes 10027008 | tf_op jit(solution)/shard_map/erd,egd->erg/dot_general | solution.py:97
  175.1 4.0 %fusion.13 = (bf16[1,960,384]{2,1,0:T(8,128)(2,1)S(1)}, bf16[1,960,384]{2,1,0:T(8,128)(2,1)S(1)}, bf16[960,384]{1,0:T(8,128)(2,1)S(1)}) fusion(f32[1,960,768]{2,1,0:T(8,128)S(1)} %fusion.10, bf16[3,192,2048]{2,1,0:T(8,128)(2,1)} %collective-permute-done.3, bf16[3,192,2048]{2,1,0:T(8,128)(2,1)S(1)} %copy-done.2, bf16[1,960,4096]{2,1,0:T(8,128)(2,1)S(1)} %bitcast_select_fusion), kind=kOutput, calls=%fused_computation.42 | convolution fusion | flops 1518256128 | bytes 13811712 | tf_op jit(solution)/shard_map/erd,efd->erf/dot_general | solution.py:106
  179.1 3.5 %convolution_convert_fusion = bf16[960,2048]{1,0:T(8,128)(2,1)S(1)} fusion(bf16[768,2048]{1,0:T(8,128)(2,1)S(1)} %bitcast.108, bf16[1,960,384]{2,1,0:T(8,128)(2,1)S(1)} %get-tuple-element.39, bf16[1,960,384]{2,1,0:T(8,128)(2,1)S(1)} %get-tuple-element.38), kind=kOutput, calls=%fused_computation.16 | convolution fusion | flops 3024814080 | bytes 8552448 | tf_op jit(solution)/shard_map/erg,egd->erd/dot_general | solution.py:112
  182.6 3.3 convolution_convert_fusion.1
  185.9 3.8 %maximum_bitcast_fusion = bf16[8,2,120,2048]{3,2,1,0:T(8,128)(2,1)} fusion(bf16[1,1,8,120,2048]{4,3,1,2,0:T(8,128)(2,1)S(1)} %bitcast.105, bf16[1,1,8,120,2048]{4,3,1,2,0:T(8,128)(2,1)S(1)} %bitcast.106), kind=kLoop, calls=%fused_computation.3 | loop fusion | flops 3932160 | bytes 15728640 | tf_op jit(solution)/shard_map/reshape | solution.py:122
  189.7 5.3 %all-to-all-start.1 = ((bf16[8,2,120,2048]{3,2,1,0:T(8,128)(2,1)}), bf16[8,2,120,2048]{3,2,1,0:T(8,128)(2,1)}, u32[]{:S(2)}, u32[]{:S(2)}) async-start(bf16[8,2,120,2048]{3,2,1,0:T(8,128)(2,1)} %maximum_bitcast_fusion), calls=%async_computation.1 | async-start | bytes 15728640 | tf_op jit(solution)/shard_map/all_to_all | solution.py:123
  195.1 4.1 %fusion.6 = f32[1,384,2048]{2,1,0:T(8,128)S(1)} fusion(bf16[960,384]{1,0:T(8,128)(2,1)S(1)} %copy-done.12, bf16[1,960,4096]{2,1,0:T(8,128)(2,1)} %copy-done), kind=kOutput, calls=%fused_computation.22 | convolution fusion | flops 1509949440 | bytes 7815168 | tf_op jit(solution)/shard_map/erf,erd->efd/dot_general | solution.py:115
  199.2 5.7 %convolution_bitcast_fusion = f32[1,768,2048]{2,1,0:T(8,128)S(1)} fusion(bf16[1,960,4096]{2,1,0:T(8,128)(2,1)} %copy-done, bf16[1,960,384]{2,1,0:T(8,128)(2,1)S(1)} %copy-done.16, bf16[1,960,384]{2,1,0:T(8,128)(2,1)S(1)} %copy-done.14), kind=kOutput, calls=%fused_computation.15 | convolution fusion | flops 3022848000 | bytes 11698176 | tf_op jit(solution)/shard_map/erg,erd->egd/dot_general | solution.py:116
  205.3 1.2 pad_maximum_fusion
  206.9 1.5 collective-permute-start.6
  208.4 51.8 %collective-permute-done.6 = bf16[3,192,2048]{2,1,0:T(8,128)(2,1)S(1)} collective-permute-done((bf16[3,192,2048]{2,1,0:T(8,128)(2,1)S(1)}, bf16[3,192,2048]{2,1,0:T(8,128)(2,1)S(1)}, u32[]{:S(2)}, u32[]{:S(2)}) %collective-permute-start.6) | collective-permute-done | bytes 2359328 | tf_op jit(solution)/shard_map/ppermute | solution.py:10
  261.1 1.4 fusion.54
  262.6 19.8 %all-to-all-done.1 = bf16[8,2,120,2048]{3,2,1,0:T(8,128)(2,1)} async-done(((bf16[8,2,120,2048]{3,2,1,0:T(8,128)(2,1)}), bf16[8,2,120,2048]{3,2,1,0:T(8,128)(2,1)}, u32[]{:S(2)}, u32[]{:S(2)}) %all-to-all-start.1) | async-done | bytes 7864352 | tf_op jit(solution)/shard_map/all_to_all | solution.py:123
  282.4 3.9 %fusion.52 = (bf16[8,1,120,2048]{3,2,1,0:T(8,128)(2,1)S(1)}, bf16[8,1,120,2048]{3,2,1,0:T(8,128)(2,1)S(1)}) fusion(bf16[8,2,120,2048]{3,2,1,0:T(8,128)(2,1)} %all-to-all-done.1), kind=kLoop, calls=%fused_computation.119 | loop fusion | bytes 15728640 | tf_op jit(solution)/shard_map/slice | solution.py:136
  286.3 1.2 fusion.31
  288.4 1.9 fusion.25
  291.3 3.4 %collective-permute-start.4 = (bf16[128,4096]{1,0:T(8,128)(2,1)S(1)}, bf16[128,4096]{1,0:T(8,128)(2,1)S(1)}, u32[]{:S(2)}, u32[]{:S(2)}) collective-permute-start(bf16[128,4096]{1,0:T(8,128)(2,1)S(1)} %pad_maximum_fusion.2), channel_id=1, source_target_pairs={{0,16},{16,0},{1,17},{17,1},{2,18},{18,2},{3,19},{19,3},{4,20},{20... | collective-permute-start | bytes 3145736 | tf_op jit(solution)/shard_map/ppermute | solution.py:10
  294.8 1.2 convolution_bitcast_fusion.1
  297.1 1.9 fusion.19
  299.0 41.3 %collective-permute-done.5 = f32[128,6]{0,1:T(8,128)S(1)} collective-permute-done((f32[128,6]{0,1:T(8,128)S(1)}, f32[128,6]{0,1:T(8,128)S(1)}, u32[]{:S(2)}, u32[]{:S(2)}) %collective-permute-start.5) | collective-permute-done | bytes 3104 | tf_op jit(solution)/shard_map/ppermute | solution.py:10
  340.9 1.5 add_convert_fusion
  (92 shorter events, 16.4 us)
Async XLA Ops:
  0.6 13.4 %collective-permute-start.2 = (f32[128,6]{0,1:T(8,128)}, f32[128,6]{0,1:T(8,128)S(1)}, u32[]{:S(2)}, u32[]{:S(2)}) collective-permute-start(f32[128,6]{0,1:T(8,128)} %param.11), channel_id=1, source_target_pairs={{0,16},{16,0},{1,17},{17,1},{2,18},{18,2},{3,19},{19,3},{4,20},{20... | collective-permute-start | bytes 9224 | tf_op jit(solution)/shard_map/ppermute | solution.py:10
  6.9 49.9 %collective-permute-start.1 = (bf16[128,4096]{1,0:T(8,128)(2,1)S(1)}, bf16[128,4096]{1,0:T(8,128)(2,1)S(1)}, u32[]{:S(2)}, u32[]{:S(2)}) collective-permute-start(bf16[128,4096]{1,0:T(8,128)(2,1)S(1)} %constant_dynamic-update-slice_fusion), channel_id=1, source_target_pairs={{0,16},{16,0},{1,17},{17,1},{2,18},{18,2},{3,19},{19,3},{4,20},{20... | collective-permute-start | bytes 3145736 | tf_op jit(solution)/shard_map/ppermute | solution.py:10
  11.1 44.0 %collective-permute-start = (s32[128,6]{0,1:T(8,128)S(1)}, s32[128,6]{0,1:T(8,128)S(1)}, u32[]{:S(2)}, u32[]{:S(2)}) collective-permute-start(s32[128,6]{0,1:T(8,128)S(1)} %multiply_add_fusion), channel_id=1, source_target_pairs={{0,16},{16,0},{1,17},{17,1},{2,18},{18,2},{3,19},{19,3},{4,20},{20... | collective-permute-start | bytes 9224 | tf_op jit(solution)/shard_map/ppermute | solution.py:10
  56.8 4.3 %copy-start.7 = (bf16[128,4096]{1,0:T(8,128)(2,1)}, bf16[128,4096]{1,0:T(8,128)(2,1)S(1)}, u32[]{:S(2)}) copy-start(bf16[128,4096]{1,0:T(8,128)(2,1)S(1)} %collective-permute-done.1) | copy-start | bytes 3145732
  61.2 5.0 %copy-start.5 = (bf16[1,192,2048]{2,1,0:T(8,128)(2,1)S(1)}, bf16[1,192,2048]{2,1,0:T(8,128)(2,1)}, u32[]{:S(2)}) copy-start(bf16[1,192,2048]{2,1,0:T(8,128)(2,1)} %param.13) | copy-start | bytes 2359300
  61.2 102.4 %all-to-all-start = ((bf16[8,120,4096]{2,1,0:T(8,128)(2,1)}), bf16[8,120,4096]{2,1,0:T(8,128)(2,1)}, u32[]{:S(2)}, u32[]{:S(2)}) async-start(bf16[8,120,4096]{2,1,0:T(8,128)(2,1)} %bitcast.104), calls=%async_computation | async-start | bytes 15728640 | tf_op jit(solution)/shard_map/all_to_all | solution.py:69
  66.2 1.4 copy-start.6
  66.2 92.1 %copy-start.10 = (s32[16]{0:T(128)S(1)}, s32[16]{0:T(128)}, u32[]{:S(2)}) copy-start(s32[16]{0:T(128)} %param.12) | copy-start | bytes 196
  67.6 95.9 %copy-start.1 = (bf16[3,192,2048]{2,1,0:T(8,128)(2,1)}, bf16[3,192,2048]{2,1,0:T(8,128)(2,1)S(1)}, u32[]{:S(2)}) copy-start(bf16[3,192,2048]{2,1,0:T(8,128)(2,1)S(1)} %constant_dynamic-update-slice_fusion.2) | copy-start | bytes 7077892
  67.6 92.9 %collective-permute-start.3 = (bf16[3,192,2048]{2,1,0:T(8,128)(2,1)S(1)}, bf16[3,192,2048]{2,1,0:T(8,128)(2,1)}, u32[]{:S(2)}, u32[]{:S(2)}) collective-permute-start(bf16[3,192,2048]{2,1,0:T(8,128)(2,1)S(1)} %constant_dynamic-update-slice_fusion.2), channel_id=1, source_target_pairs={{0,1},{1,0},{2,3},{3,2},{4,5},{5,4},{6,7},{7,6},{8,9},{9,8},{10,11... | collective-permute-start | bytes 7077896 | tf_op jit(solution)/shard_map/ppermute | solution.py:10
  167.4 7.7 %copy-start = (bf16[1,960,4096]{2,1,0:T(8,128)(2,1)}, bf16[1,960,4096]{2,1,0:T(8,128)(2,1)S(1)}, u32[]{:S(2)}) copy-start(bf16[1,960,4096]{2,1,0:T(8,128)(2,1)S(1)} %bitcast_select_fusion) | copy-start | bytes 23592964
  167.4 7.7 %copy-start.2 = (bf16[3,192,2048]{2,1,0:T(8,128)(2,1)S(1)}, bf16[3,192,2048]{2,1,0:T(8,128)(2,1)}, u32[]{:S(2)}) copy-start(bf16[3,192,2048]{2,1,0:T(8,128)(2,1)} %copy-done.1) | copy-start | bytes 7077892
  175.0 4.0 %copy-start.3 = (bf16[2,384,2048]{2,1,0:T(8,128)(2,1)S(1)}, bf16[2,384,2048]{2,1,0:T(8,128)(2,1)}, u32[]{:S(2)}) copy-start(bf16[2,384,2048]{2,1,0:T(8,128)(2,1)} %fusion.5) | copy-start | bytes 9437188
  179.0 3.5 %copy-start.13 = (bf16[1,960,384]{2,1,0:T(8,128)(2,1)}, bf16[1,960,384]{2,1,0:T(8,128)(2,1)S(1)}, u32[]{:S(2)}) copy-start(bf16[1,960,384]{2,1,0:T(8,128)(2,1)S(1)} %get-tuple-element.38) | copy-start | bytes 2211844
  179.0 3.5 %copy-start.15 = (bf16[1,960,384]{2,1,0:T(8,128)(2,1)}, bf16[1,960,384]{2,1,0:T(8,128)(2,1)S(1)}, u32[]{:S(2)}) copy-start(bf16[1,960,384]{2,1,0:T(8,128)(2,1)S(1)} %get-tuple-element.39) | copy-start | bytes 2211844
  179.0 3.5 %copy-start.11 = (bf16[960,384]{1,0:T(8,128)(2,1)}, bf16[960,384]{1,0:T(8,128)(2,1)S(1)}, u32[]{:S(2)}) copy-start(bf16[960,384]{1,0:T(8,128)(2,1)S(1)} %get-tuple-element.40) | copy-start | bytes 2211844
  189.7 5.4 %copy-start.12 = (bf16[960,384]{1,0:T(8,128)(2,1)S(1)}, bf16[960,384]{1,0:T(8,128)(2,1)}, u32[]{:S(2)}) copy-start(bf16[960,384]{1,0:T(8,128)(2,1)} %copy-done.11) | copy-start | bytes 2211844
  189.7 92.6 %all-to-all-start.1 = ((bf16[8,2,120,2048]{3,2,1,0:T(8,128)(2,1)}), bf16[8,2,120,2048]{3,2,1,0:T(8,128)(2,1)}, u32[]{:S(2)}, u32[]{:S(2)}) async-start(bf16[8,2,120,2048]{3,2,1,0:T(8,128)(2,1)} %maximum_bitcast_fusion), calls=%async_computation.1 | async-start | bytes 15728640 | tf_op jit(solution)/shard_map/all_to_all | solution.py:123
  195.1 4.1 %copy-start.14 = (bf16[1,960,384]{2,1,0:T(8,128)(2,1)S(1)}, bf16[1,960,384]{2,1,0:T(8,128)(2,1)}, u32[]{:S(2)}) copy-start(bf16[1,960,384]{2,1,0:T(8,128)(2,1)} %copy-done.13) | copy-start | bytes 2211844
  195.1 4.1 %copy-start.16 = (bf16[1,960,384]{2,1,0:T(8,128)(2,1)S(1)}, bf16[1,960,384]{2,1,0:T(8,128)(2,1)}, u32[]{:S(2)}) copy-start(bf16[1,960,384]{2,1,0:T(8,128)(2,1)} %copy-done.15) | copy-start | bytes 2211844
  206.9 53.4 %collective-permute-start.6 = (bf16[3,192,2048]{2,1,0:T(8,128)(2,1)S(1)}, bf16[3,192,2048]{2,1,0:T(8,128)(2,1)S(1)}, u32[]{:S(2)}, u32[]{:S(2)}) collective-permute-start(bf16[3,192,2048]{2,1,0:T(8,128)(2,1)S(1)} %slice.221), channel_id=1, source_target_pairs={{0,1},{1,0},{2,3},{3,2},{4,5},{5,4},{6,7},{7,6},{8,9},{9,8},{10,11... | collective-permute-start | bytes 7077896 | tf_op jit(solution)/shard_map/ppermute | solution.py:10
  262.6 23.7 %copy-start.8 = (bf16[128,4096]{1,0:T(8,128)(2,1)S(1)}, bf16[128,4096]{1,0:T(8,128)(2,1)}, u32[]{:S(2)}) copy-start(bf16[128,4096]{1,0:T(8,128)(2,1)} %copy-done.7) | copy-start | bytes 3145732
  290.5 4.3 %copy-start.4 = (bf16[128,2048]{1,0:T(8,128)(2,1)S(1)}, bf16[128,2048]{1,0:T(8,128)(2,1)}, u32[]{:S(2)}) copy-start(bf16[128,2048]{1,0:T(8,128)(2,1)} %param.9) | copy-start | bytes 1572868
  291.3 4.8 %copy-start.9 = (f32[128,6]{0,1:T(8,128)S(1)}, f32[128,6]{0,1:T(8,128)}, u32[]{:S(2)}) copy-start(f32[128,6]{0,1:T(8,128)} %param.11) | copy-start | bytes 9220
  291.3 49.5 %collective-permute-start.4 = (bf16[128,4096]{1,0:T(8,128)(2,1)S(1)}, bf16[128,4096]{1,0:T(8,128)(2,1)S(1)}, u32[]{:S(2)}, u32[]{:S(2)}) collective-permute-start(bf16[128,4096]{1,0:T(8,128)(2,1)S(1)} %pad_maximum_fusion.2), channel_id=1, source_target_pairs={{0,16},{16,0},{1,17},{17,1},{2,18},{18,2},{3,19},{19,3},{4,20},{20... | collective-permute-start | bytes 3145736 | tf_op jit(solution)/shard_map/ppermute | solution.py:10
  296.0 44.3 %collective-permute-start.5 = (f32[128,6]{0,1:T(8,128)S(1)}, f32[128,6]{0,1:T(8,128)S(1)}, u32[]{:S(2)}, u32[]{:S(2)}) collective-permute-start(f32[128,6]{0,1:T(8,128)S(1)} %get-tuple-element.28), channel_id=1, source_target_pairs={{0,16},{16,0},{1,17},{17,1},{2,18},{18,2},{3,19},{19,3},{4,20},{20... | collective-permute-start | bytes 9224 | tf_op jit(solution)/shard_map/ppermute | solution.py:10

commit v10 on v9

--- a/solution.py
+++ b/solution.py
@@ -50,7 +50,6 @@
     code = (flat_ids * slots + local_rank).reshape(tok_rows, top_count)
     partner_code = shifted(code, "half", 2, 1)
 
-    all_rows = jnp.concatenate([both_rows, partner_rows], axis=0)
     all_gates = jnp.concatenate([gate_vals, partner_gates], axis=0)
     all_code = jnp.concatenate([code, partner_code], axis=0)
     local = all_code // slots - half * half_experts
@@ -60,9 +59,16 @@
 
     slot_ids = jnp.arange(2 * half_rows, dtype=jnp.int32)[:, None, None]
     lands = dest[None, :, :] == slot_ids
-    pick = jnp.any(lands, axis=2).astype(jnp.bfloat16)
     slot_gate = jnp.sum(jnp.where(lands, all_gates[None, :, :], 0.0), axis=(1, 2))
-    picked = jnp.dot(pick, all_rows, preferred_element_type=jnp.float32)
+    picked = jnp.dot(
+        jnp.any(lands[:, :tok_rows], axis=2).astype(jnp.bfloat16),
+        both_rows,
+        preferred_element_type=jnp.float32,
+    ) + jnp.dot(
+        jnp.any(lands[:, tok_rows:], axis=2).astype(jnp.bfloat16),
+        partner_rows,
+        preferred_element_type=jnp.float32,
+    )
     lane = jnp.arange(2 * width, dtype=jnp.int32)[None, :]
     scale = jnp.where(lane < width, 1.0, slot_gate[:, None])
     send = (picked * scale).astype(jnp.bfloat16).reshape(half_experts, 2 * slots, 2 * width)
@@ -144,7 +150,8 @@
         layer = jnp.dot(in_three(weight), out_part, preferred_element_type=jnp.float32)
         layer = layer[:tok_rows] + layer[tok_rows : 2 * tok_rows] + layer[2 * tok_rows :]
         grads = jnp.dot(ones, dx_part, preferred_element_type=jnp.float32)
-        scores = jnp.dot(all_rows[rows, width:], out_part.T, preferred_element_type=jnp.float32)
+        cot_rows = (both_rows if which == 0 else partner_rows)[:, width:]
+        scores = jnp.dot(cot_rows, out_part.T, preferred_element_type=jnp.float32)
         gg = jnp.sum(jnp.where(hit, scores[:, None, :], 0.0), axis=2)
         return layer, grads, gg
 

time: 344 us -> 353 us (1.026)
  matrix products: 40.8 us -> 53.5 us
  waiting for transfers between devices: 153 us -> 148 us
    dot_general x3 -> x4, matrix products: 6.67 us -> 19.1 us  [the longest x1 9.06 us: on_device(): jnp.dot(jnp.any(lands[:, tok_rows:], axis=2).astype(jnp.bfloat16), partne...]
    ppermute x7, waiting for transfers between devices: 134 us -> 128 us  [shifted(): lax.ppermute(value, axis, [(j, (j + shift) % count) for j in range(count)])]
  transfers between devices with their start and end apart: 9 -> 9, of which waited for: 4 -> 4; matrix products, arithmetic and copies ran while one was open for 10% -> 11% of each run, Pallas kernels for 0% -> 0%
where the time goes in v10:
time: 353 us; the launch traced here: 352 us
  waiting for transfers between devices  148 us (42%)
  blocking collectives  90.9 us (26%)
  matrix products  53.5 us (15%)
  starting transfers between devices  23.5 us (7%)
  other arithmetic  22.1 us (6%)
  local copies, waits for them, and re-layouts  13 us (4%)
    ppermute x7, waiting for transfers between devices, shifted(): lax.ppermute(value, axis, [(j, (j + shift) % count) for j in range(count)])  128 us
    psum x1, blocking collectives, on_device(): all_counts = lax.psum(count_rows, ('half', 'inner'))  90.9 us
    all_to_all x1, waiting for transfers between devices, on_device(): lax.all_to_all(back, 'inner', split_axis=0, concat_axis=0, tiled=True)  19.6 us
    ppermute x7, starting transfers between devices, shifted(): lax.ppermute(value, axis, [(j, (j + shift) % count) for j in range(count)])  13.2 us
    dot_general x1, matrix products, on_device(): jnp.dot(jnp.any(lands[:, tok_rows:], axis=2).astype(jnp.bfloat16), partne...  9.06 us
    dot_general x1, matrix products, on_device(): jnp.dot(jnp.any(lands[:, :tok_rows], axis=2).astype(jnp.bfloat16), both_r...  7.69 us
    dot_general x1, matrix products, on_device(): jnp.einsum('erd,egd->erg', rows_in, gate_up, preferred_element_type=jnp.f...  7.64 us
  transfers between devices with their start and end apart: 9, of which 4 were waited for; matrix products, arithmetic and copies ran while one was open for 11% of the time, Pallas kernels for 0%

profile of v10, /device:TPU:0, one launch (start us, length us, event | category | flops | bytes accessed | tf_op | source)
XLA Modules:
  0.0 352.0 jit_solution(3489640751843717668)
XLA Ops:
  1.7 1.7 reduce-window.6
  4.8 4.0 %collective-permute-start = (s32[128,6]{0,1:T(8,128)S(1)}, s32[128,6]{0,1:T(8,128)S(1)}, u32[]{:S(2)}, u32[]{:S(2)}) collective-permute-start(s32[128,6]{0,1:T(8,128)S(1)} %multiply_add_fusion), channel_id=1, source_target_pairs={{0,16},{16,0},{1,17},{17,1},{2,18},{18,2},{3,19},{19,3},{4,20},{20... | collective-permute-start | bytes 9224 | tf_op jit(solution)/shard_map/ppermute | solution.py:10
  11.0 3.0 collective-permute-start.1
  16.0 7.7 %fusion.55 = f32[960,4096]{1,0:T(8,128)} fusion(pred[960,128]{1,0:T(8,128)(4,1)S(1)} %get-tuple-element.29, bf16[128,4096]{1,0:T(8,128)(2,1)S(1)} %constant_dynamic-update-slice_fusion), kind=kOutput, calls=%fused_computation.122 | convolution fusion | flops 1006632960 | bytes 16900096 | tf_op jit(solution)/shard_map/dot_general | solution.py:63
  23.7 35.4 %collective-permute-done.1 = bf16[128,4096]{1,0:T(8,128)(2,1)S(1)} collective-permute-done((bf16[128,4096]{1,0:T(8,128)(2,1)S(1)}, bf16[128,4096]{1,0:T(8,128)(2,1)S(1)}, u32[]{:S(2)}, u32[]{:S(2)}) %collective-permute-start.1) | collective-permute-done | bytes 1048608 | tf_op jit(solution)/shard_map/ppermute | solution.py:10
  59.1 9.1 %multiply_convert_fusion = bf16[960,4096]{1,0:T(8,128)(2,1)} fusion(f32[960,4096]{1,0:T(8,128)} %fusion.55, pred[960,128]{1,0:T(8,128)(4,1)S(1)} %get-tuple-element.28, bf16[128,4096]{1,0:T(8,128)(2,1)S(1)} %collective-permute-done.1, f32[960]{0:T(1024)S(1)} %select_reduce_fusion, pred[4096]{0:T(1024)(128)(4,1)S(1)} %iota_compare_fusion.5), kind=kOutput, calls=%fused_computation.1 | convolution fusion | flops 1022361600 | bytes 24772352 | tf_op jit(solution)/shard_map/dot_general | solution.py:67
  68.1 5.0 %all-to-all-start = ((bf16[8,120,4096]{2,1,0:T(8,128)(2,1)}), bf16[8,120,4096]{2,1,0:T(8,128)(2,1)}, u32[]{:S(2)}, u32[]{:S(2)}) async-start(bf16[8,120,4096]{2,1,0:T(8,128)(2,1)} %bitcast.107), calls=%async_computation | async-start | bytes 15728640 | tf_op jit(solution)/shard_map/all_to_all | solution.py:75
  73.3 1.2 constant_dynamic-update-slice_fusion.3
  74.6 1.6 collective-permute-start.3
  76.6 90.9 %psum.7 = s32[16,16]{1,0:T(8,128)S(1)} all-reduce(s32[16,16]{1,0:T(8,128)S(1)} %broadcast_select_fusion), channel_id=1, replica_groups=mesh['half'=2,'inner'=8,'dp'=2] {'half','inner'}, use_global_device_ids=true, to_apply=%region_4.5 | all-reduce | flops 256 | bytes 2048 | tf_op jit(solution)/shard_map/psum | solution.py:49
  169.9 3.0 fusion.4
  172.9 3.8 %bitcast_select_fusion = bf16[1,960,4096]{2,1,0:T(8,128)(2,1)S(1)} fusion(pred[960]{0:T(1024)(128)(4,1)S(1)} %lt.68, bf16[1,960,4096]{2,1,0:T(8,128)(2,1)} %bitcast.99), kind=kLoop, calls=%fused_computation.4 | loop fusion | flops 3932160 | bytes 15729600 | tf_op jit(solution)/shard_map/jit(_where)/select_n | solution.py:86
  176.8 7.6 %fusion.6 = f32[1,960,768]{2,1,0:T(8,128)S(1)} fusion(bf16[768,2048]{1,0:T(8,128)(2,1)} %bitcast.110, bf16[1,960,4096]{2,1,0:T(8,128)(2,1)S(1)} %bitcast_select_fusion), kind=kOutput, calls=%fused_computation.33 | convolution fusion | flops 3019898880 | bytes 10027008 | tf_op jit(solution)/shard_map/erd,egd->erg/dot_general | solution.py:103
  184.5 4.0 %fusion.9 = (bf16[1,960,384]{2,1,0:T(8,128)(2,1)S(1)}, bf16[1,960,384]{2,1,0:T(8,128)(2,1)S(1)}, bf16[960,384]{1,0:T(8,128)(2,1)S(1)}) fusion(f32[1,960,768]{2,1,0:T(8,128)S(1)} %fusion.6, bf16[3,192,2048]{2,1,0:T(8,128)(2,1)} %collective-permute-done.3, bf16[3,192,2048]{2,1,0:T(8,128)(2,1)S(1)} %copy-done.2, bf16[1,960,4096]{2,1,0:T(8,128)(2,1)S(1)} %bitcast_select_fusion), kind=kOutput, calls=%fused_computation.40 | convolution fusion | flops 1518256128 | bytes 13811712 | tf_op jit(solution)/shard_map/erd,efd->erf/dot_general | solution.py:112
  188.5 3.5 convolution_convert_fusion
  192.0 3.3 convolution_convert_fusion.1
  195.4 3.8 %maximum_bitcast_fusion = bf16[8,2,120,2048]{3,2,1,0:T(8,128)(2,1)} fusion(bf16[1,1,8,120,2048]{4,3,1,2,0:T(8,128)(2,1)S(1)} %bitcast.108, bf16[1,1,8,120,2048]{4,3,1,2,0:T(8,128)(2,1)S(1)} %bitcast.109), kind=kLoop, calls=%fused_computation.3 | loop fusion | flops 3932160 | bytes 15728640 | tf_op jit(solution)/shard_map/reshape | solution.py:128
  199.2 5.2 %all-to-all-start.1 = ((bf16[8,2,120,2048]{3,2,1,0:T(8,128)(2,1)}), bf16[8,2,120,2048]{3,2,1,0:T(8,128)(2,1)}, u32[]{:S(2)}, u32[]{:S(2)}) async-start(bf16[8,2,120,2048]{3,2,1,0:T(8,128)(2,1)} %maximum_bitcast_fusion), calls=%async_computation.1 | async-start | bytes 15728640 | tf_op jit(solution)/shard_map/all_to_all | solution.py:129
  204.4 4.3 %fusion.5 = f32[1,384,2048]{2,1,0:T(8,128)S(1)} fusion(bf16[960,384]{1,0:T(8,128)(2,1)} %copy-done.11, bf16[1,960,4096]{2,1,0:T(8,128)(2,1)} %copy-done), kind=kOutput, calls=%fused_computation.21 | convolution fusion | flops 1509949440 | bytes 7815168 | tf_op jit(solution)/shard_map/erf,erd->efd/dot_general | solution.py:121
  208.7 5.7 %convolution_bitcast_fusion = f32[1,768,2048]{2,1,0:T(8,128)S(1)} fusion(bf16[1,960,4096]{2,1,0:T(8,128)(2,1)} %copy-done, bf16[1,960,384]{2,1,0:T(8,128)(2,1)S(1)} %copy-done.15, bf16[1,960,384]{2,1,0:T(8,128)(2,1)S(1)} %copy-done.13), kind=kOutput, calls=%fused_computation.14 | convolution fusion | flops 3022848000 | bytes 11698176 | tf_op jit(solution)/shard_map/erg,erd->egd/dot_general | solution.py:122
  216.4 1.6 collective-permute-start.6
  217.9 51.8 %collective-permute-done.6 = bf16[3,192,2048]{2,1,0:T(8,128)(2,1)S(1)} collective-permute-done((bf16[3,192,2048]{2,1,0:T(8,128)(2,1)S(1)}, bf16[3,192,2048]{2,1,0:T(8,128)(2,1)S(1)}, u32[]{:S(2)}, u32[]{:S(2)}) %collective-permute-start.6) | collective-permute-done | bytes 2359328 | tf_op jit(solution)/shard_map/ppermute | solution.py:10
  270.6 1.4 fusion.49
  272.1 19.6 %all-to-all-done.1 = bf16[8,2,120,2048]{3,2,1,0:T(8,128)(2,1)} async-done(((bf16[8,2,120,2048]{3,2,1,0:T(8,128)(2,1)}), bf16[8,2,120,2048]{3,2,1,0:T(8,128)(2,1)}, u32[]{:S(2)}, u32[]{:S(2)}) %all-to-all-start.1) | async-done | bytes 7864352 | tf_op jit(solution)/shard_map/all_to_all | solution.py:129
  291.7 3.9 %fusion.47 = (bf16[8,1,120,2048]{3,2,1,0:T(8,128)(2,1)S(1)}, bf16[8,1,120,2048]{3,2,1,0:T(8,128)(2,1)S(1)}) fusion(bf16[8,2,120,2048]{3,2,1,0:T(8,128)(2,1)} %all-to-all-done.1), kind=kLoop, calls=%fused_computation.116 | loop fusion | bytes 15728640 | tf_op jit(solution)/shard_map/slice | solution.py:142
  295.6 1.2 fusion.27
  297.7 1.9 fusion.21
  300.6 1.3 collective-permute-start.4
  303.1 1.8 collective-permute-start.5
  305.8 1.9 fusion.15
  307.7 41.1 %collective-permute-done.5 = f32[128,6]{0,1:T(8,128)S(1)} collective-permute-done((f32[128,6]{0,1:T(8,128)S(1)}, f32[128,6]{0,1:T(8,128)S(1)}, u32[]{:S(2)}, u32[]{:S(2)}) %collective-permute-start.5) | collective-permute-done | bytes 3104 | tf_op jit(solution)/shard_map/ppermute | solution.py:10
  349.4 1.5 add_convert_fusion
  (92 shorter events, 18.1 us)
Async XLA Ops:
  0.6 14.7 %copy-start.9 = (f32[128,6]{0,1:T(8,128)S(1)}, f32[128,6]{0,1:T(8,128)}, u32[]{:S(2)}) copy-start(f32[128,6]{0,1:T(8,128)} %param.11) | copy-start | bytes 9220
  4.8 9.2 %collective-permute-start = (s32[128,6]{0,1:T(8,128)S(1)}, s32[128,6]{0,1:T(8,128)S(1)}, u32[]{:S(2)}, u32[]{:S(2)}) collective-permute-start(s32[128,6]{0,1:T(8,128)S(1)} %multiply_add_fusion), channel_id=1, source_target_pairs={{0,16},{16,0},{1,17},{17,1},{2,18},{18,2},{3,19},{19,3},{4,20},{20... | collective-permute-start | bytes 9224 | tf_op jit(solution)/shard_map/ppermute | solution.py:10
  8.8 6.5 %collective-permute-start.2 = (f32[128,6]{0,1:T(8,128)}, f32[128,6]{0,1:T(8,128)S(1)}, u32[]{:S(2)}, u32[]{:S(2)}) collective-permute-start(f32[128,6]{0,1:T(8,128)} %param.11), channel_id=1, source_target_pairs={{0,16},{16,0},{1,17},{17,1},{2,18},{18,2},{3,19},{19,3},{4,20},{20... | collective-permute-start | bytes 9224 | tf_op jit(solution)/shard_map/ppermute | solution.py:10
  11.0 48.1 %collective-permute-start.1 = (bf16[128,4096]{1,0:T(8,128)(2,1)S(1)}, bf16[128,4096]{1,0:T(8,128)(2,1)S(1)}, u32[]{:S(2)}, u32[]{:S(2)}) collective-permute-start(bf16[128,4096]{1,0:T(8,128)(2,1)S(1)} %constant_dynamic-update-slice_fusion), channel_id=1, source_target_pairs={{0,16},{16,0},{1,17},{17,1},{2,18},{18,2},{3,19},{19,3},{4,20},{20... | collective-permute-start | bytes 3145736 | tf_op jit(solution)/shard_map/ppermute | solution.py:10
  59.1 9.1 %copy-start.4 = (bf16[128,4096]{1,0:T(8,128)(2,1)}, bf16[128,4096]{1,0:T(8,128)(2,1)S(1)}, u32[]{:S(2)}) copy-start(bf16[128,4096]{1,0:T(8,128)(2,1)S(1)} %collective-permute-done.1) | copy-start | bytes 3145732
  68.1 5.0 %copy-start.7 = (bf16[1,192,2048]{2,1,0:T(8,128)(2,1)S(1)}, bf16[1,192,2048]{2,1,0:T(8,128)(2,1)}, u32[]{:S(2)}) copy-start(bf16[1,192,2048]{2,1,0:T(8,128)(2,1)} %param.13) | copy-start | bytes 2359300
  68.1 104.8 %all-to-all-start = ((bf16[8,120,4096]{2,1,0:T(8,128)(2,1)}), bf16[8,120,4096]{2,1,0:T(8,128)(2,1)}, u32[]{:S(2)}, u32[]{:S(2)}) async-start(bf16[8,120,4096]{2,1,0:T(8,128)(2,1)} %bitcast.107), calls=%async_computation | async-start | bytes 15728640 | tf_op jit(solution)/shard_map/all_to_all | solution.py:75
  73.2 1.4 copy-start.8
  73.2 95.3 %copy-start.10 = (s32[16]{0:T(128)S(1)}, s32[16]{0:T(128)}, u32[]{:S(2)}) copy-start(s32[16]{0:T(128)} %param.12) | copy-start | bytes 196
  74.6 98.3 %copy-start.1 = (bf16[3,192,2048]{2,1,0:T(8,128)(2,1)}, bf16[3,192,2048]{2,1,0:T(8,128)(2,1)S(1)}, u32[]{:S(2)}) copy-start(bf16[3,192,2048]{2,1,0:T(8,128)(2,1)S(1)} %constant_dynamic-update-slice_fusion.2) | copy-start | bytes 7077892
  74.6 95.3 %collective-permute-start.3 = (bf16[3,192,2048]{2,1,0:T(8,128)(2,1)S(1)}, bf16[3,192,2048]{2,1,0:T(8,128)(2,1)}, u32[]{:S(2)}, u32[]{:S(2)}) collective-permute-start(bf16[3,192,2048]{2,1,0:T(8,128)(2,1)S(1)} %constant_dynamic-update-slice_fusion.2), channel_id=1, source_target_pairs={{0,1},{1,0},{2,3},{3,2},{4,5},{5,4},{6,7},{7,6},{8,9},{9,8},{10,11... | collective-permute-start | bytes 7077896 | tf_op jit(solution)/shard_map/ppermute | solution.py:10
  176.8 7.7 %copy-start = (bf16[1,960,4096]{2,1,0:T(8,128)(2,1)}, bf16[1,960,4096]{2,1,0:T(8,128)(2,1)S(1)}, u32[]{:S(2)}) copy-start(bf16[1,960,4096]{2,1,0:T(8,128)(2,1)S(1)} %bitcast_select_fusion) | copy-start | bytes 23592964
  176.8 7.7 %copy-start.2 = (bf16[3,192,2048]{2,1,0:T(8,128)(2,1)S(1)}, bf16[3,192,2048]{2,1,0:T(8,128)(2,1)}, u32[]{:S(2)}) copy-start(bf16[3,192,2048]{2,1,0:T(8,128)(2,1)} %copy-done.1) | copy-start | bytes 7077892
  184.5 4.0 %copy-start.3 = (bf16[2,384,2048]{2,1,0:T(8,128)(2,1)S(1)}, bf16[2,384,2048]{2,1,0:T(8,128)(2,1)}, u32[]{:S(2)}) copy-start(bf16[2,384,2048]{2,1,0:T(8,128)(2,1)} %fusion.4) | copy-start | bytes 9437188
  188.4 3.5 %copy-start.12 = (bf16[1,960,384]{2,1,0:T(8,128)(2,1)}, bf16[1,960,384]{2,1,0:T(8,128)(2,1)S(1)}, u32[]{:S(2)}) copy-start(bf16[1,960,384]{2,1,0:T(8,128)(2,1)S(1)} %get-tuple-element.40) | copy-start | bytes 2211844
  188.5 3.5 %copy-start.14 = (bf16[1,960,384]{2,1,0:T(8,128)(2,1)}, bf16[1,960,384]{2,1,0:T(8,128)(2,1)S(1)}, u32[]{:S(2)}) copy-start(bf16[1,960,384]{2,1,0:T(8,128)(2,1)S(1)} %get-tuple-element.41) | copy-start | bytes 2211844
  188.5 3.5 %copy-start.11 = (bf16[960,384]{1,0:T(8,128)(2,1)}, bf16[960,384]{1,0:T(8,128)(2,1)S(1)}, u32[]{:S(2)}) copy-start(bf16[960,384]{1,0:T(8,128)(2,1)S(1)} %get-tuple-element.42) | copy-start | bytes 2211844
  199.2 92.5 %all-to-all-start.1 = ((bf16[8,2,120,2048]{3,2,1,0:T(8,128)(2,1)}), bf16[8,2,120,2048]{3,2,1,0:T(8,128)(2,1)}, u32[]{:S(2)}, u32[]{:S(2)}) async-start(bf16[8,2,120,2048]{3,2,1,0:T(8,128)(2,1)} %maximum_bitcast_fusion), calls=%async_computation.1 | async-start | bytes 15728640 | tf_op jit(solution)/shard_map/all_to_all | solution.py:129
  204.4 4.3 %copy-start.13 = (bf16[1,960,384]{2,1,0:T(8,128)(2,1)S(1)}, bf16[1,960,384]{2,1,0:T(8,128)(2,1)}, u32[]{:S(2)}) copy-start(bf16[1,960,384]{2,1,0:T(8,128)(2,1)} %copy-done.12) | copy-start | bytes 2211844
  204.4 4.3 %copy-start.15 = (bf16[1,960,384]{2,1,0:T(8,128)(2,1)S(1)}, bf16[1,960,384]{2,1,0:T(8,128)(2,1)}, u32[]{:S(2)}) copy-start(bf16[1,960,384]{2,1,0:T(8,128)(2,1)} %copy-done.14) | copy-start | bytes 2211844
  216.4 53.4 %collective-permute-start.6 = (bf16[3,192,2048]{2,1,0:T(8,128)(2,1)S(1)}, bf16[3,192,2048]{2,1,0:T(8,128)(2,1)S(1)}, u32[]{:S(2)}, u32[]{:S(2)}) collective-permute-start(bf16[3,192,2048]{2,1,0:T(8,128)(2,1)S(1)} %slice.233), channel_id=1, source_target_pairs={{0,1},{1,0},{2,3},{3,2},{4,5},{5,4},{6,7},{7,6},{8,9},{9,8},{10,11... | collective-permute-start | bytes 7077896 | tf_op jit(solution)/shard_map/ppermute | solution.py:10
  272.0 23.5 %copy-start.5 = (bf16[128,4096]{1,0:T(8,128)(2,1)S(1)}, bf16[128,4096]{1,0:T(8,128)(2,1)}, u32[]{:S(2)}) copy-start(bf16[128,4096]{1,0:T(8,128)(2,1)} %copy-done.4) | copy-start | bytes 3145732
  299.8 2.1 copy-start.6
  300.6 48.8 %collective-permute-start.4 = (bf16[128,4096]{1,0:T(8,128)(2,1)S(1)}, bf16[128,4096]{1,0:T(8,128)(2,1)S(1)}, u32[]{:S(2)}, u32[]{:S(2)}) collective-permute-start(bf16[128,4096]{1,0:T(8,128)(2,1)S(1)} %pad_maximum_fusion.2), channel_id=1, source_target_pairs={{0,16},{16,0},{1,17},{17,1},{2,18},{18,2},{3,19},{19,3},{4,20},{20... | collective-permute-start | bytes 3145736 | tf_op jit(solution)/shard_map/ppermute | solution.py:10
  303.1 45.7 %collective-permute-start.5 = (f32[128,6]{0,1:T(8,128)S(1)}, f32[128,6]{0,1:T(8,128)S(1)}, u32[]{:S(2)}, u32[]{:S(2)}) collective-permute-start(f32[128,6]{0,1:T(8,128)S(1)} %get-tuple-element.30), channel_id=1, source_target_pairs={{0,16},{16,0},{1,17},{17,1},{2,18},{18,2},{3,19},{19,3},{4,20},{20... | collective-permute-start | bytes 9224 | tf_op jit(solution)/shard_map/ppermute | solution.py:10

commit v11 on v9

--- a/solution.py
+++ b/solution.py
@@ -77,11 +77,12 @@
     before = earlier[sources][:, :, mine].transpose(0, 2, 1)
     ranks = jnp.arange(slots, dtype=jnp.int32)
     keep = before[..., None] + ranks < capacity[mine][None, :, None, None]
-    got = jnp.where(keep[..., None], got, jnp.zeros((), got.dtype))
     if local_experts == 1:
         got = got.reshape(1, n_in * 2 * slots, 2 * width)
+        keep = keep.reshape(1, n_in * 2 * slots, 1)
     else:
         got = got.transpose(1, 0, 2, 3, 4).reshape(local_experts, n_in * 2 * slots, 2 * width)
+        keep = keep.transpose(1, 0, 2, 3).reshape(local_experts, n_in * 2 * slots, 1)
     rows_in = got[:, :, :width]
     rows_cot = got[:, :, width:]
 
@@ -99,7 +100,7 @@
     up_pre = both_pre[..., full_hidden:]
     sigmoid_gate = jax.nn.sigmoid(gate_pre)
     activated = gate_pre * sigmoid_gate
-    hidden = (activated * up_pre).astype(jnp.bfloat16)
+    hidden = jnp.where(keep, activated * up_pre, 0.0).astype(jnp.bfloat16)
     out_rows = jnp.einsum(
         "erf,efd->erd", hidden, full_down, preferred_element_type=jnp.float32
     ).astype(jnp.bfloat16)
@@ -108,7 +109,7 @@
         jnp.bfloat16
     )
     d_up = (d_hidden * activated).astype(jnp.bfloat16)
-    d_both = jnp.concatenate([d_gate, d_up], axis=-1)
+    d_both = jnp.where(keep, jnp.concatenate([d_gate, d_up], axis=-1), jnp.zeros((), jnp.bfloat16))
     dx_rows = jnp.einsum(
         "erg,egd->erd", d_both, gate_up, preferred_element_type=jnp.float32
     ).astype(jnp.bfloat16)

time: 344 us -> 344 us (level)
    select_n x1 -> x0, other arithmetic: 3.82 us -> none  [on_device(): got = jnp.where(keep[..., None], got, jnp.zeros((), got.dtype))]
where the time goes in v11:
time: 344 us
  waiting for transfers between devices  153 us (44%)
  blocking collectives  88.6 us (26%)
  matrix products  43.1 us (13%)
  starting transfers between devices  24 us (7%)
  other arithmetic  20.8 us (6%)
  local copies, waits for them, and re-layouts  13 us (4%)
    ppermute x7, waiting for transfers between devices, shifted(): lax.ppermute(value, axis, [(j, (j + shift) % count) for j in range(count)])  134 us
    psum x1, blocking collectives, on_device(): all_counts = lax.psum(count_rows, ('half', 'inner'))  88.6 us
    all_to_all x1, waiting for transfers between devices, on_device(): lax.all_to_all(back, 'inner', split_axis=0, concat_axis=0, tiled=True)  19.7 us
    ppermute x7, starting transfers between devices, shifted(): lax.ppermute(value, axis, [(j, (j + shift) % count) for j in range(count)])  13.8 us
  transfers between devices with their start and end apart: 9, of which 4 were waited for; matrix products, arithmetic and copies ran while one was open for 10% of the time, Pallas kernels for 0%

profile of v11, /device:TPU:0, one launch (start us, length us, event | category | flops | bytes accessed | tf_op | source)
XLA Modules:
  0.0 343.7 jit_solution(18375190432883290826)
XLA Ops:
  0.6 4.1 %collective-permute-start.2 = (f32[128,6]{0,1:T(8,128)}, f32[128,6]{0,1:T(8,128)S(1)}, u32[]{:S(2)}, u32[]{:S(2)}) collective-permute-start(f32[128,6]{0,1:T(8,128)} %param.11), channel_id=1, source_target_pairs={{0,16},{16,0},{1,17},{17,1},{2,18},{18,2},{3,19},{19,3},{4,20},{20... | collective-permute-start | bytes 9224 | tf_op jit(solution)/shard_map/ppermute | solution.py:10
  8.1 1.7 reduce-window.6
  11.1 2.9 collective-permute-start
  14.7 40.4 %collective-permute-done = s32[128,6]{0,1:T(8,128)S(1)} collective-permute-done((s32[128,6]{0,1:T(8,128)S(1)}, s32[128,6]{0,1:T(8,128)S(1)}, u32[]{:S(2)}, u32[]{:S(2)}) %collective-permute-start) | collective-permute-done | bytes 3104 | tf_op jit(solution)/shard_map/ppermute | solution.py:10
  56.8 4.3 %multiply_convert_fusion = bf16[960,4096]{1,0:T(8,128)(2,1)} fusion(pred[960,256]{1,0:T(8,128)(4,1)S(1)} %fusion, f32[960]{0:T(1024)S(1)} %select_reduce_fusion, pred[4096]{0:T(1024)(128)(4,1)S(1)} %iota_compare_fusion.5, bf16[128,4096]{1,0:T(8,128)(2,1)S(1)} %collective-permute-done.1, bf16[128,4096]{1,0:T(8,128)(2,1)S(1)} %constant_dynamic-update-slice_fusion), kind=kOutput, calls=%fused_computation.1 | convolution fusion | flops 2029256704 | bytes 10215168 | tf_op jit(solution)/shard_map/dot_general | solution.py:65
  61.2 5.0 %all-to-all-start = ((bf16[8,120,4096]{2,1,0:T(8,128)(2,1)}), bf16[8,120,4096]{2,1,0:T(8,128)(2,1)}, u32[]{:S(2)}, u32[]{:S(2)}) async-start(bf16[8,120,4096]{2,1,0:T(8,128)(2,1)} %bitcast.110), calls=%async_computation | async-start | bytes 15728640 | tf_op jit(solution)/shard_map/all_to_all | solution.py:69
  66.3 1.2 constant_dynamic-update-slice_fusion.3
  67.6 1.6 collective-permute-start.3
  69.7 88.6 %psum.7 = s32[16,16]{1,0:T(8,128)S(1)} all-reduce(s32[16,16]{1,0:T(8,128)S(1)} %broadcast_select_fusion), channel_id=1, replica_groups=mesh['half'=2,'inner'=8,'dp'=2] {'half','inner'}, use_global_device_ids=true, to_apply=%region_4.5 | all-reduce | flops 256 | bytes 2048 | tf_op jit(solution)/shard_map/psum | solution.py:49
  160.6 2.9 fusion.5
  163.5 6.3 %fusion.10 = f32[1,960,768]{2,1,0:T(8,128)S(1)} fusion(bf16[768,2048]{1,0:T(8,128)(2,1)} %bitcast.113, bf16[1,960,4096]{2,1,0:T(8,128)(2,1)} %bitcast.9), kind=kOutput, calls=%fused_computation.34 | convolution fusion | flops 3019898880 | bytes 10027008 | tf_op jit(solution)/shard_map/erd,egd->erg/dot_general | solution.py:98
  169.9 5.3 %fusion.21 = (bf16[1,960,1,1,1,1,384]{6,1,5,4,3,2,0:T(8,128)(2,1)S(1)}, bf16[1,960,1,1,1,1,384]{6,1,5,4,3,2,0:T(8,128)(2,1)S(1)}, bf16[960,384]{1,0:T(8,128)(2,1)S(1)}) fusion(f32[1,960,768]{2,1,0:T(8,128)S(1)} %fusion.10, pred[960]{0:T(1024)(128)(4,1)S(1)} %lt.68, bf16[3,192,2048]{2,1,0:T(8,128)(2,1)} %collective-permute-done.3, ...), kind=kOutput, calls=%fused_computation.59 | convolution fusion | flops 1518624768 | bytes 13812672 | tf_op jit(solution)/shard_map/erd,efd->erf/dot_general | solution.py:107
  175.2 3.8 %convolution_convert_fusion = bf16[960,2048]{1,0:T(8,128)(2,1)S(1)} fusion(bf16[768,2048]{1,0:T(8,128)(2,1)S(1)} %bitcast.114, bf16[1,960,1,1,1,1,384]{6,1,5,4,3,2,0:T(8,128)(2,1)S(1)} %get-tuple-element.39, bf16[1,960,1,1,1,1,384]{6,1,5,4,3,2,0:T(8,128)(2,1)S(1)} %get-tuple-element.38, pred[960]{0:T(1024)(128)(4,1)S(1)} %lt.68), kind=kOutput, calls=%fused_computation.15 | convolution fusion | flops 3025551360 | bytes 8553408 | tf_op jit(solution)/shard_map/erg,egd->erd/dot_general | solution.py:113
  179.0 5.2 %convolution_convert_fusion.1 = bf16[960,2048]{1,0:T(8,128)(2,1)} fusion(bf16[960,384]{1,0:T(8,128)(2,1)S(1)} %get-tuple-element.40, bf16[3,192,2048]{2,1,0:T(8,128)(2,1)} %collective-permute-done.3, bf16[3,192,2048]{2,1,0:T(8,128)(2,1)S(1)} %constant_dynamic-update-slice_fusion.2), kind=kOutput, calls=%fused_computation.16 | convolution fusion | flops 1515061248 | bytes 9388032 | tf_op jit(solution)/shard_map/erf,efd->erd/dot_general | solution.py:104
  184.2 6.0 %maximum_bitcast_fusion = bf16[8,2,120,2048]{3,2,1,0:T(8,128)(2,1)} fusion(bf16[1,1,8,120,2048]{4,3,1,2,0:T(8,128)(2,1)S(1)} %bitcast.111, bf16[1,1,8,120,2048]{4,3,1,2,0:T(8,128)(2,1)} %bitcast.112), kind=kLoop, calls=%fused_computation.3 | loop fusion | flops 3932160 | bytes 15728640 | tf_op jit(solution)/shard_map/reshape | solution.py:123
  190.2 5.1 %all-to-all-start.1 = ((bf16[8,2,120,2048]{3,2,1,0:T(8,128)(2,1)}), bf16[8,2,120,2048]{3,2,1,0:T(8,128)(2,1)}, u32[]{:S(2)}, u32[]{:S(2)}) async-start(bf16[8,2,120,2048]{3,2,1,0:T(8,128)(2,1)} %maximum_bitcast_fusion), calls=%async_computation.1 | async-start | bytes 15728640 | tf_op jit(solution)/shard_map/all_to_all | solution.py:124
  195.4 4.1 %fusion.6 = f32[1,384,2048]{2,1,0:T(8,128)S(1)} fusion(bf16[960,384]{1,0:T(8,128)(2,1)S(1)} %get-tuple-element.40, bf16[1,960,4096]{2,1,0:T(8,128)(2,1)} %bitcast.9), kind=kOutput, calls=%fused_computation.21 | convolution fusion | flops 1509949440 | bytes 7815168 | tf_op jit(solution)/shard_map/erf,erd->efd/dot_general | solution.py:116
  199.5 5.8 %convolution_bitcast_fusion = f32[1,768,2048]{2,1,0:T(8,128)S(1)} fusion(bf16[1,960,4096]{2,1,0:T(8,128)(2,1)} %bitcast.9, bf16[1,960,1,1,1,1,384]{6,1,5,4,3,2,0:T(8,128)(2,1)S(1)} %copy-done.11, bf16[1,960,1,1,1,1,384]{6,1,5,4,3,2,0:T(8,128)(2,1)S(1)} %copy-done.9, pred[960]{0:T(1024)(128)(4,1)S(1)} %lt.68), kind=kOutput, calls=%fused_computation.14 | convolution fusion | flops 3023585280 | bytes 11699136 | tf_op jit(solution)/shard_map/erg,erd->egd/dot_general | solution.py:117
  205.7 1.2 pad_maximum_fusion
  207.2 1.5 collective-permute-start.6
  208.8 51.8 %collective-permute-done.6 = bf16[3,192,2048]{2,1,0:T(8,128)(2,1)S(1)} collective-permute-done((bf16[3,192,2048]{2,1,0:T(8,128)(2,1)S(1)}, bf16[3,192,2048]{2,1,0:T(8,128)(2,1)S(1)}, u32[]{:S(2)}, u32[]{:S(2)}) %collective-permute-start.6) | collective-permute-done | bytes 2359328 | tf_op jit(solution)/shard_map/ppermute | solution.py:10
  261.5 1.4 fusion.61
  262.9 19.7 %all-to-all-done.1 = bf16[8,2,120,2048]{3,2,1,0:T(8,128)(2,1)} async-done(((bf16[8,2,120,2048]{3,2,1,0:T(8,128)(2,1)}), bf16[8,2,120,2048]{3,2,1,0:T(8,128)(2,1)}, u32[]{:S(2)}, u32[]{:S(2)}) %all-to-all-start.1) | async-done | bytes 7864352 | tf_op jit(solution)/shard_map/all_to_all | solution.py:124
  282.6 3.9 %fusion.59 = (bf16[8,1,120,2048]{3,2,1,0:T(8,128)(2,1)S(1)}, bf16[8,1,120,2048]{3,2,1,0:T(8,128)(2,1)S(1)}) fusion(bf16[8,2,120,2048]{3,2,1,0:T(8,128)(2,1)} %all-to-all-done.1), kind=kLoop, calls=%fused_computation.123 | loop fusion | bytes 15728640 | tf_op jit(solution)/shard_map/slice | solution.py:137
  286.5 1.2 fusion.34
  288.7 1.9 fusion.28
  291.6 3.4 %collective-permute-start.4 = (bf16[128,4096]{1,0:T(8,128)(2,1)S(1)}, bf16[128,4096]{1,0:T(8,128)(2,1)S(1)}, u32[]{:S(2)}, u32[]{:S(2)}) collective-permute-start(bf16[128,4096]{1,0:T(8,128)(2,1)S(1)} %pad_maximum_fusion.2), channel_id=1, source_target_pairs={{0,16},{16,0},{1,17},{17,1},{2,18},{18,2},{3,19},{19,3},{4,20},{20... | collective-permute-start | bytes 3145736 | tf_op jit(solution)/shard_map/ppermute | solution.py:10
  295.0 1.2 convolution_bitcast_fusion.1
  297.4 1.9 fusion.22
  299.2 41.3 %collective-permute-done.5 = f32[128,6]{0,1:T(8,128)S(1)} collective-permute-done((f32[128,6]{0,1:T(8,128)S(1)}, f32[128,6]{0,1:T(8,128)S(1)}, u32[]{:S(2)}, u32[]{:S(2)}) %collective-permute-start.5) | collective-permute-done | bytes 3104 | tf_op jit(solution)/shard_map/ppermute | solution.py:10
  341.1 1.5 add_convert_fusion
  342.6 1.1 fusion.18
  (81 shorter events, 15.3 us)
Async XLA Ops:
  0.6 13.4 %collective-permute-start.2 = (f32[128,6]{0,1:T(8,128)}, f32[128,6]{0,1:T(8,128)S(1)}, u32[]{:S(2)}, u32[]{:S(2)}) collective-permute-start(f32[128,6]{0,1:T(8,128)} %param.11), channel_id=1, source_target_pairs={{0,16},{16,0},{1,17},{17,1},{2,18},{18,2},{3,19},{19,3},{4,20},{20... | collective-permute-start | bytes 9224 | tf_op jit(solution)/shard_map/ppermute | solution.py:10
  6.9 49.9 %collective-permute-start.1 = (bf16[128,4096]{1,0:T(8,128)(2,1)S(1)}, bf16[128,4096]{1,0:T(8,128)(2,1)S(1)}, u32[]{:S(2)}, u32[]{:S(2)}) collective-permute-start(bf16[128,4096]{1,0:T(8,128)(2,1)S(1)} %constant_dynamic-update-slice_fusion), channel_id=1, source_target_pairs={{0,16},{16,0},{1,17},{17,1},{2,18},{18,2},{3,19},{19,3},{4,20},{20... | collective-permute-start | bytes 3145736 | tf_op jit(solution)/shard_map/ppermute | solution.py:10
  11.1 44.0 %collective-permute-start = (s32[128,6]{0,1:T(8,128)S(1)}, s32[128,6]{0,1:T(8,128)S(1)}, u32[]{:S(2)}, u32[]{:S(2)}) collective-permute-start(s32[128,6]{0,1:T(8,128)S(1)} %multiply_add_fusion), channel_id=1, source_target_pairs={{0,16},{16,0},{1,17},{17,1},{2,18},{18,2},{3,19},{19,3},{4,20},{20... | collective-permute-start | bytes 9224 | tf_op jit(solution)/shard_map/ppermute | solution.py:10
  56.8 4.3 %copy-start.4 = (bf16[128,4096]{1,0:T(8,128)(2,1)}, bf16[128,4096]{1,0:T(8,128)(2,1)S(1)}, u32[]{:S(2)}) copy-start(bf16[128,4096]{1,0:T(8,128)(2,1)S(1)} %collective-permute-done.1) | copy-start | bytes 3145732
  61.2 5.0 %copy-start.2 = (bf16[1,192,2048]{2,1,0:T(8,128)(2,1)S(1)}, bf16[1,192,2048]{2,1,0:T(8,128)(2,1)}, u32[]{:S(2)}) copy-start(bf16[1,192,2048]{2,1,0:T(8,128)(2,1)} %param.13) | copy-start | bytes 2359300
  61.2 102.4 %all-to-all-start = ((bf16[8,120,4096]{2,1,0:T(8,128)(2,1)}), bf16[8,120,4096]{2,1,0:T(8,128)(2,1)}, u32[]{:S(2)}, u32[]{:S(2)}) async-start(bf16[8,120,4096]{2,1,0:T(8,128)(2,1)} %bitcast.110), calls=%async_computation | async-start | bytes 15728640 | tf_op jit(solution)/shard_map/all_to_all | solution.py:69
  66.2 1.4 copy-start.3
  66.2 92.1 %copy-start.7 = (s32[16]{0:T(128)S(1)}, s32[16]{0:T(128)}, u32[]{:S(2)}) copy-start(s32[16]{0:T(128)} %param.12) | copy-start | bytes 196
  67.6 92.9 %collective-permute-start.3 = (bf16[3,192,2048]{2,1,0:T(8,128)(2,1)S(1)}, bf16[3,192,2048]{2,1,0:T(8,128)(2,1)}, u32[]{:S(2)}, u32[]{:S(2)}) collective-permute-start(bf16[3,192,2048]{2,1,0:T(8,128)(2,1)S(1)} %constant_dynamic-update-slice_fusion.2), channel_id=1, source_target_pairs={{0,1},{1,0},{2,3},{3,2},{4,5},{5,4},{6,7},{7,6},{8,9},{9,8},{10,11... | collective-permute-start | bytes 7077896 | tf_op jit(solution)/shard_map/ppermute | solution.py:10
  169.9 5.3 %copy-start = (bf16[2,384,2048]{2,1,0:T(8,128)(2,1)S(1)}, bf16[2,384,2048]{2,1,0:T(8,128)(2,1)}, u32[]{:S(2)}) copy-start(bf16[2,384,2048]{2,1,0:T(8,128)(2,1)} %fusion.5) | copy-start | bytes 9437188
  175.1 3.8 %copy-start.8 = (bf16[1,960,1,1,1,1,384]{6,1,5,4,3,2,0:T(8,128)(2,1)}, bf16[1,960,1,1,1,1,384]{6,1,5,4,3,2,0:T(8,128)(2,1)S(1)}, u32[]{:S(2)}) copy-start(bf16[1,960,1,1,1,1,384]{6,1,5,4,3,2,0:T(8,128)(2,1)S(1)} %get-tuple-element.38) | copy-start | bytes 2211844
  175.1 3.8 %copy-start.10 = (bf16[1,960,1,1,1,1,384]{6,1,5,4,3,2,0:T(8,128)(2,1)}, bf16[1,960,1,1,1,1,384]{6,1,5,4,3,2,0:T(8,128)(2,1)S(1)}, u32[]{:S(2)}) copy-start(bf16[1,960,1,1,1,1,384]{6,1,5,4,3,2,0:T(8,128)(2,1)S(1)} %get-tuple-element.39) | copy-start | bytes 2211844
  190.2 92.4 %all-to-all-start.1 = ((bf16[8,2,120,2048]{3,2,1,0:T(8,128)(2,1)}), bf16[8,2,120,2048]{3,2,1,0:T(8,128)(2,1)}, u32[]{:S(2)}, u32[]{:S(2)}) async-start(bf16[8,2,120,2048]{3,2,1,0:T(8,128)(2,1)} %maximum_bitcast_fusion), calls=%async_computation.1 | async-start | bytes 15728640 | tf_op jit(solution)/shard_map/all_to_all | solution.py:124
  195.3 4.1 %copy-start.9 = (bf16[1,960,1,1,1,1,384]{6,1,5,4,3,2,0:T(8,128)(2,1)S(1)}, bf16[1,960,1,1,1,1,384]{6,1,5,4,3,2,0:T(8,128)(2,1)}, u32[]{:S(2)}) copy-start(bf16[1,960,1,1,1,1,384]{6,1,5,4,3,2,0:T(8,128)(2,1)} %copy-done.8) | copy-start | bytes 2211844
  195.4 4.1 %copy-start.11 = (bf16[1,960,1,1,1,1,384]{6,1,5,4,3,2,0:T(8,128)(2,1)S(1)}, bf16[1,960,1,1,1,1,384]{6,1,5,4,3,2,0:T(8,128)(2,1)}, u32[]{:S(2)}) copy-start(bf16[1,960,1,1,1,1,384]{6,1,5,4,3,2,0:T(8,128)(2,1)} %copy-done.10) | copy-start | bytes 2211844
  207.2 53.4 %collective-permute-start.6 = (bf16[3,192,2048]{2,1,0:T(8,128)(2,1)S(1)}, bf16[3,192,2048]{2,1,0:T(8,128)(2,1)S(1)}, u32[]{:S(2)}, u32[]{:S(2)}) collective-permute-start(bf16[3,192,2048]{2,1,0:T(8,128)(2,1)S(1)} %slice.223), channel_id=1, source_target_pairs={{0,1},{1,0},{2,3},{3,2},{4,5},{5,4},{6,7},{7,6},{8,9},{9,8},{10,11... | collective-permute-start | bytes 7077896 | tf_op jit(solution)/shard_map/ppermute | solution.py:10
  262.9 23.6 %copy-start.5 = (bf16[128,4096]{1,0:T(8,128)(2,1)S(1)}, bf16[128,4096]{1,0:T(8,128)(2,1)}, u32[]{:S(2)}) copy-start(bf16[128,4096]{1,0:T(8,128)(2,1)} %copy-done.4) | copy-start | bytes 3145732
  290.7 4.3 %copy-start.1 = (bf16[128,2048]{1,0:T(8,128)(2,1)S(1)}, bf16[128,2048]{1,0:T(8,128)(2,1)}, u32[]{:S(2)}) copy-start(bf16[128,2048]{1,0:T(8,128)(2,1)} %param.9) | copy-start | bytes 1572868
  291.6 4.8 %copy-start.6 = (f32[128,6]{0,1:T(8,128)S(1)}, f32[128,6]{0,1:T(8,128)}, u32[]{:S(2)}) copy-start(f32[128,6]{0,1:T(8,128)} %param.11) | copy-start | bytes 9220
  291.6 49.5 %collective-permute-start.4 = (bf16[128,4096]{1,0:T(8,128)(2,1)S(1)}, bf16[128,4096]{1,0:T(8,128)(2,1)S(1)}, u32[]{:S(2)}, u32[]{:S(2)}) collective-permute-start(bf16[128,4096]{1,0:T(8,128)(2,1)S(1)} %pad_maximum_fusion.2), channel_id=1, source_target_pairs={{0,16},{16,0},{1,17},{17,1},{2,18},{18,2},{3,19},{19,3},{4,20},{20... | collective-permute-start | bytes 3145736 | tf_op jit(solution)/shard_map/ppermute | solution.py:10
  296.2 44.3 %collective-permute-start.5 = (f32[128,6]{0,1:T(8,128)S(1)}, f32[128,6]{0,1:T(8,128)S(1)}, u32[]{:S(2)}, u32[]{:S(2)}) collective-permute-start(f32[128,6]{0,1:T(8,128)S(1)} %get-tuple-element.28), channel_id=1, source_target_pairs={{0,16},{16,0},{1,17},{17,1},{2,18},{18,2},{3,19},{19,3},{4,20},{20... | collective-permute-start | bytes 9224 | tf_op jit(solution)/shard_map/ppermute | solution.py:10
